TPU v7x, 256 devices: a whole 4x4x8 slice. The times are simulated.
256 devices in a mesh: ctx: 64 (over z, x, core), head: 4 (over y).
Axes of the slice: x: 4, y: 4, z: 8, core: 2. Of those that a mesh axis runs over, the one named last changes fastest.
Arguments:
- queries: bfloat16 [8192, 32, 128], P('ctx', 'head'), may hold values from -14 to 14
- keys: bfloat16 [8192, 32, 128], P('ctx', 'head'), may hold values from -14 to 14
- values: bfloat16 [8192, 32, 128], P('ctx', 'head'), may hold values from -6 to 6
- gain: float32 [32, 128], P('head'), may hold values from 0.1 to 1.9
- doc_lengths: int32 [64], replicated, may hold values from 1 to 2048, 8192 in all
- cotangent: bfloat16 [8192, 32, 128], P('ctx', 'head'), may hold values from -6 to 6
Outputs:
- mixed: bfloat16 [8192, 32, 128], P('ctx', 'head')
- query_grad: bfloat16 [8192, 32, 128], P('ctx', 'head')
- key_grad: bfloat16 [8192, 32, 128], P('ctx', 'head')
- value_grad: bfloat16 [8192, 32, 128], P('ctx', 'head')
All inputs are finite; a program needn't handle non-finite values.
Results may differ from a plain program's by a relative error of at most 0.0054.
Values may be sent and summed in bfloat16 or wider, within the bound.
No kernel may reach another device: no remote copies, remote signals or barrier semaphores. Data moves between devices by JAX's collectives and lax.ppermute only.
A program may use at most 128 MiB of HBM per device.

v0:
```python
import jax
import jax.numpy as jnp
from jax import lax
from jax.sharding import PartitionSpec as P

SPAN = 2


neg_large = -1e30
norm_eps = 1e-06


def from_behind(x, axis, by):
    devices = lax.axis_size(axis)
    pairs = [(i, i + by) for i in range(devices) if 0 <= i + by < devices]
    return lax.ppermute(x, axis, pairs)


def carried_in(part, axis, combine, identity, reverse):
    count = lax.axis_size(axis)
    place = lax.axis_index(axis)
    ahead = count - 1 - place if reverse else place
    gathered = jax.tree.map(lambda a: lax.all_gather(a, axis), part)
    state = jax.tree.map(lambda a, e: jnp.zeros_like(a) + jnp.asarray(e, a.dtype), part, identity)

    def one(hop, state):
        source = count - 1 - hop if reverse else hop
        return combine(
            state, jax.tree.map(lambda a: lax.dynamic_index_in_dim(a, source, 0, False), gathered)
        )

    return lax.fori_loop(0, ahead, one, state)


def wide(form, left, right):
    return jnp.einsum(form, left, right, precision=lax.Precision.HIGHEST)


def narrow(form, left, right):
    return jnp.einsum(form, left, right, preferred_element_type=jnp.float32)


def doc_index(doc_lengths, positions):
    starts = jnp.cumsum(doc_lengths) - doc_lengths
    return jnp.sum((starts[None, :] <= positions[:, None]).astype(jnp.int32), axis=1) - 1


def one_doc(doc_lengths, position):
    return doc_index(doc_lengths, jnp.reshape(position, (1,)))[0]


def join_states(earlier, later):
    return (later[0] + (1.0 - later[1]) * earlier[0], jnp.maximum(earlier[1], later[1]))


def masked_scores(query_block, key_block, mask, scale):
    raw = narrow("thd,uhd->htu", query_block, key_block) * scale
    return jnp.where(mask[None], raw, neg_large)


def key_terms(dscores, weights, query_block, grad_block, scale):
    key_part = narrow("htu,thd->uhd", dscores, query_block) * scale
    value_part = narrow("htu,thd->uhd", weights, grad_block)
    return (key_part, value_part)


def per_device(queries, keys, values, gain, doc_lengths, cotangent):
    tile, heads, width = queries.shape
    features = heads * lax.axis_size("head") * width
    scale = width ** (-0.5)
    base = lax.axis_index("ctx") * tile
    offsets = jnp.arange(tile, dtype=jnp.int32)
    own_pos = base + offsets
    own_doc = doc_index(doc_lengths, own_pos)
    prev_doc = one_doc(doc_lengths, base - 1)
    next_doc = one_doc(doc_lengths, base + tile)
    pair = jnp.stack([keys, values])
    arrived = [from_behind(pair, "ctx", shift) for shift in range(SPAN, 0, -1)]
    key_tiles = [piece[0] for piece in arrived] + [keys]
    value_tiles = [piece[1] for piece in arrived] + [values]
    masks = []
    for position in range(SPAN + 1):
        key_pos = base - (SPAN - position) * tile + offsets
        key_doc = doc_index(doc_lengths, key_pos)
        masks.append(
            (own_doc[:, None] == key_doc[None, :]) & (key_pos[None, :] <= own_pos[:, None])
        )
    score_list = [
        masked_scores(queries, key_tiles[position], masks[position], scale)
        for position in range(SPAN + 1)
    ]
    top = score_list[0].max(axis=-1)
    for position in range(1, SPAN + 1):
        top = jnp.maximum(top, score_list[position].max(axis=-1))
    total = jnp.zeros((heads, tile), jnp.float32)
    for position in range(SPAN + 1):
        total = total + jnp.sum(jnp.exp(score_list[position] - top[..., None]), axis=-1)
    log_total = top + jnp.log(total)
    prob_list = []
    weight_list = []
    soft_out = jnp.zeros((tile, heads, width), jnp.float32)
    for position in range(SPAN + 1):
        probs = jnp.exp(score_list[position] - log_total[..., None])
        weights = probs.astype(jnp.bfloat16)
        prob_list.append(probs)
        weight_list.append(weights)
        soft_out = soft_out + narrow("htu,uhd->thd", weights, value_tiles[position])
    same_tile = masks[SPAN].astype(jnp.float32)
    carried_prev = (own_doc == prev_doc).astype(jnp.float32)
    carried_next = (own_doc == next_doc).astype(jnp.float32)
    keep_last = (own_doc == own_doc[tile - 1])[:, None, None]
    keep_first = (own_doc == own_doc[0])[:, None, None]
    reset_front = (prev_doc != own_doc[tile - 1]).astype(jnp.float32)
    reset_back = (next_doc != own_doc[0]).astype(jnp.float32)
    query_wide = queries.astype(jnp.float32)
    attend = (narrow("thd,uhd->htu", queries, keys) * same_tile).astype(jnp.bfloat16)
    local_state = narrow("uhd,uhe->hde", jnp.where(keep_last, keys, jnp.zeros_like(keys)), values)
    zero_state = jnp.zeros_like(local_state)
    incoming, front_flag = carried_in(
        (local_state, reset_front), "ctx", join_states, (zero_state, jnp.float32(0.0)), False
    )
    linear_out = (
        narrow("htu,uhd->thd", attend, values)
        + wide("thd,hde->the", query_wide, incoming) * carried_prev[:, None, None]
    )
    squares = lax.psum(jnp.sum(linear_out * linear_out, axis=(1, 2)), "head")
    inverse = lax.rsqrt(squares / features + norm_eps)
    mixed = (linear_out * inverse[:, None, None] * gain[None] + soft_out).astype(jnp.bfloat16)
    grad_wide = cotangent.astype(jnp.float32)
    weighted = grad_wide * gain[None]
    projection = lax.psum(jnp.sum(weighted * linear_out, axis=(1, 2)), "head")
    inner = (
        inverse[:, None, None] * weighted
        - linear_out * (inverse**3 * projection / features)[:, None, None]
    ).astype(jnp.bfloat16)
    row_dot = jnp.sum(grad_wide * soft_out, axis=-1).T
    query_soft = jnp.zeros((tile, heads, width), jnp.float32)
    dscore_list = []
    for position in range(SPAN + 1):
        dprobs = narrow("thd,uhd->htu", cotangent, value_tiles[position])
        dscores = (prob_list[position] * (dprobs - row_dot[..., None])).astype(jnp.bfloat16)
        query_soft = query_soft + narrow("htu,uhd->thd", dscores, key_tiles[position]) * scale
        dscore_list.append(dscores)
    inner_wide = inner.astype(jnp.float32)
    back = (narrow("thd,uhd->htu", inner, values) * same_tile).astype(jnp.bfloat16)
    query_linear = (
        narrow("htu,uhd->thd", back, keys)
        + wide("the,hde->thd", inner_wide, incoming) * carried_prev[:, None, None]
    )
    tile_sum = narrow(
        "thd,the->hde", jnp.where(keep_first, queries, jnp.zeros_like(queries)), inner
    )
    later, back_flag = carried_in(
        (tile_sum, reset_back), "ctx", join_states, (zero_state, jnp.float32(0.0)), True
    )
    key_linear = (
        narrow("htu,thd->uhd", back, queries)
        + wide("uhe,hde->uhd", values.astype(jnp.float32), later) * carried_next[:, None, None]
    )
    value_linear = (
        narrow("htu,the->uhe", attend, inner)
        + wide("uhd,hde->uhe", keys.astype(jnp.float32), later) * carried_next[:, None, None]
    )
    parts = [
        key_terms(dscore_list[position], weight_list[position], queries, cotangent, scale)
        for position in range(SPAN + 1)
    ]
    key_soft, value_soft = parts[SPAN]
    for shift in range(1, SPAN + 1):
        sent = jnp.stack([parts[SPAN - shift][0], parts[SPAN - shift][1]])
        returned = from_behind(sent.astype(jnp.bfloat16), "ctx", -shift).astype(sent.dtype)
        key_soft = key_soft + returned[0]
        value_soft = value_soft + returned[1]
    query_grad = (query_linear + query_soft).astype(jnp.bfloat16)
    key_grad = (key_linear + key_soft).astype(jnp.bfloat16)
    value_grad = (value_linear + value_soft).astype(jnp.bfloat16)
    return (mixed, query_grad, key_grad, value_grad)


def solution(mesh):
    placed = (
        P("ctx", "head", None),
        P("ctx", "head", None),
        P("ctx", "head", None),
        P("head", None),
        P(),
        P("ctx", "head", None),
    )
    return jax.shard_map(
        per_device,
        mesh=mesh,
        in_specs=placed,
        out_specs=(
            P("ctx", "head", None),
            P("ctx", "head", None),
            P("ctx", "head", None),
            P("ctx", "head", None),
        ),
        check_vma=False,
    )
```

profile of v0, /device:TPU:8, one launch (start us, length us, event | category | flops | bytes accessed | tf_op | source)
XLA Modules:
  0.0 664.7 jit_solution(4182333826920939034)
XLA Ops:
  8.3 1.3 fusion.88
  11.7 1.3 compare_convert_fusion
  14.2 2.0 fusion.55
  18.3 1.8 collective-permute-start.1
  20.0 3.6 collective-permute-start
  23.6 1.9 broadcast_select_fusion
  28.2 1.3 dynamic-slice
  31.1 139.8 %all-reduce.2 = (f32[64]{0:T(128)S(1)}, f32[64]{0:T(128)S(1)}) all-reduce(f32[64]{0:T(128)S(1)} %dynamic-update-slice, f32[64]{0:T(128)S(1)} %dynamic-update-slice.1), channel_id=1, replica_groups=mesh['ctx'=64,'head'=4] {'ctx'}, use_global_device_ids=true, to_apply=%add | all-reduce | flops 128 | bytes 1024
  170.9 1.3 fusion.52
  172.2 1.5 fusion.95
  173.7 1.5 fusion.94
  178.2 1.4 fusion.23
  179.6 2.3 fusion.39
  181.9 8.6 %all-reduce.3 = (f32[128]{0:T(128)S(1)}, f32[128]{0:T(128)S(1)}) all-reduce(f32[128]{0:T(128)S(1)} %get-tuple-element.151, f32[128]{0:T(128)S(1)} %get-tuple-element.150), channel_id=1, replica_groups=mesh['ctx'=64,'head'=4] {'head'}, use_global_device_ids=true, to_apply=%region_6.7 | all-reduce | flops 256 | bytes 2048 | tf_op jit(solution)/shard_map/psum | solution.py:126
  190.5 2.2 fusion.38
  192.7 2.0 fusion.53
  198.2 1.8 copy.266
  200.1 1.3 fusion.25
  201.6 1.3 collective-permute-start.2
  202.9 1.3 fusion.24
  204.5 1.3 collective-permute-start.3
  207.7 1.3 fusion.12
  212.2 12.1 %collective-permute-done.3 = bf16[2,128,8,128]{3,1,2,0:T(8,128)(2,1)S(1)} collective-permute-done((bf16[2,128,8,128]{3,1,2,0:T(8,128)(2,1)S(1)}, bf16[2,128,8,128]{3,1,2,0:T(8,128)(2,1)S(1)}, u32[]{:S(2)}, u32[]{:S(2)}) %collective-permute-start.3) | collective-permute-done | bytes 524320 | tf_op jit(solution)/shard_map/ppermute | solution.py:16
  225.5 260.4 %all-gather.7.cloned.1.call-done = f32[512,128,128]{2,1,0:T(8,128)} async-done(((f32[8,128,128]{2,1,0:T(8,128)}), f32[512,128,128]{2,1,0:T(8,128)}) %all-gather.7.cloned.1.call-update) | async-done | bytes 33554448 | tf_op jit(solution)/shard_map/all_gather | solution.py:23
  485.9 165.8 %while.27 = (s32[]{:T(128)}, f32[8,128,128]{2,1,0:T(8,128)S(1)}, s32[]{:T(128)}, f32[64,8,128,128]{3,2,1,0:T(8,128)}, f32[64]{0:T(128)S(1)}, /*index=5*/s32[]{:T(128)}, s32[]{:T(128)}, s32[]{:T(128)}, s32[]{:T(128)}, f32[1]{0:T(128)}) while((s32[]{:T(128)}, f32[8,128,128]{2,1,0:T(8,128)S(1)}, s32[]{:T(128)}, ...), condition=%wide.region_20.21_spmd, body=%wide.region_19.20_spmd.sunk | while | flops 262151 | bytes 1573051 | solution.py:32
  487.3 1.2 bitcast_add_fusion.5
  489.9 1.2 bitcast_add_fusion.5
  492.5 1.2 bitcast_add_fusion.5
  497.8 1.2 bitcast_add_fusion.5
  500.4 1.2 bitcast_add_fusion.5
  505.7 1.2 bitcast_add_fusion.5
  508.3 1.2 bitcast_add_fusion.5
  511.0 1.2 bitcast_add_fusion.5
  513.6 1.2 bitcast_add_fusion.5
  516.2 1.2 bitcast_add_fusion.5
  518.9 1.2 bitcast_add_fusion.5
  521.5 1.2 bitcast_add_fusion.5
  526.7 1.2 bitcast_add_fusion.5
  529.4 1.2 bitcast_add_fusion.5
  534.6 1.2 bitcast_add_fusion.5
  537.3 1.2 bitcast_add_fusion.5
  539.9 1.2 bitcast_add_fusion.5
  542.5 1.2 bitcast_add_fusion.5
  547.8 1.2 bitcast_add_fusion.5
  550.4 1.2 bitcast_add_fusion.5
  555.7 1.2 bitcast_add_fusion.5
  558.3 1.2 bitcast_add_fusion.5
  560.9 1.2 bitcast_add_fusion.5
  563.6 1.2 bitcast_add_fusion.5
  566.2 1.2 bitcast_add_fusion.5
  568.8 1.2 bitcast_add_fusion.5
  571.5 1.2 bitcast_add_fusion.5
  576.7 1.2 bitcast_add_fusion.5
  579.4 1.2 bitcast_add_fusion.5
  584.6 1.2 bitcast_add_fusion.5
  587.3 1.2 bitcast_add_fusion.5
  589.9 1.2 bitcast_add_fusion.5
  592.5 1.2 bitcast_add_fusion.5
  597.8 1.2 bitcast_add_fusion.5
  600.4 1.2 bitcast_add_fusion.5
  605.7 1.2 bitcast_add_fusion.5
  608.3 1.2 bitcast_add_fusion.5
  653.0 1.5 fusion.47
  655.4 1.6 fusion.43
  (161 shorter events, 98.5 us)
Async XLA Ops:
  7.2 201.8 %copy-start.2 = (bf16[128,8,128]{2,1,0:T(8,128)(2,1)S(1)}, bf16[128,8,128]{2,1,0:T(8,128)(2,1)}, u32[]{:S(2)}) copy-start(bf16[128,8,128]{2,1,0:T(8,128)(2,1)} %param.11) | copy-start | bytes 786436
  7.2 198.6 %copy-start.3 = (bf16[128,8,128]{2,1,0:T(8,128)(2,1)S(1)}, bf16[128,8,128]{2,1,0:T(8,128)(2,1)}, u32[]{:S(2)}) copy-start(bf16[128,8,128]{2,1,0:T(8,128)(2,1)} %param.12) | copy-start | bytes 786436
  7.2 194.1 %copy-start.1 = (bf16[128,8,128]{2,1,0:T(8,128)(2,1)S(1)}, bf16[128,8,128]{2,1,0:T(8,128)(2,1)}, u32[]{:S(2)}) copy-start(bf16[128,8,128]{2,1,0:T(8,128)(2,1)} %param.10) | copy-start | bytes 786436
  7.2 189.9 %copy-start = (bf16[128,8,128]{2,1,0:T(8,128)(2,1)S(1)}, bf16[128,8,128]{2,1,0:T(8,128)(2,1)}, u32[]{:S(2)}) copy-start(bf16[128,8,128]{2,1,0:T(8,128)(2,1)} %param.15) | copy-start | bytes 786436
  7.2 170.9 %all-gather.5.cloned.1.call-start = ((), (), s32[]{:S(2)}) async-start(), calls=%async_computation | async-start | bytes 34078720 | tf_op jit(solution)/shard_map/all_gather | solution.py:23
  16.2 469.6 %all-gather.7.cloned.1.call-start = ((), (), s32[]{:S(2)}) async-start(), calls=%async_computation.1 | async-start | bytes 34078720 | tf_op jit(solution)/shard_map/all_gather | solution.py:23
  18.3 153.9 %collective-permute-start.1 = (bf16[2,128,8,128]{3,1,2,0:T(8,128)(2,1)}, bf16[2,128,8,128]{3,1,2,0:T(8,128)(2,1)S(1)}, u32[]{:S(2)}, u32[]{:S(2)}) collective-permute-start(bf16[2,128,8,128]{3,1,2,0:T(8,128)(2,1)} %pad_maximum_fusion), channel_id=1, source_target_pairs={{0,4},{4,8},{8,12},{12,16},{16,20},{20,24},{24,28},{28,32},{32,36}... | collective-permute-start | bytes 1572872 | tf_op jit(solution)/shard_map/ppermute | solution.py:16
  20.0 153.7 %collective-permute-start = (bf16[2,128,8,128]{3,1,2,0:T(8,128)(2,1)}, bf16[2,128,8,128]{3,1,2,0:T(8,128)(2,1)S(1)}, u32[]{:S(2)}, u32[]{:S(2)}) collective-permute-start(bf16[2,128,8,128]{3,1,2,0:T(8,128)(2,1)} %pad_maximum_fusion), channel_id=1, source_target_pairs={{0,8},{4,12},{8,16},{12,20},{16,24},{20,28},{24,32},{28,36},{32,40... | collective-permute-start | bytes 1572872 | tf_op jit(solution)/shard_map/ppermute | solution.py:16
  172.2 1.5 copy-start.5
  173.7 4.4 copy-start.4
  201.6 9.5 %collective-permute-start.2 = (bf16[2,128,8,128]{3,1,2,0:T(8,128)(2,1)S(1)}, bf16[2,128,8,128]{3,1,2,0:T(8,128)(2,1)S(1)}, u32[]{:S(2)}, u32[]{:S(2)}) collective-permute-start(bf16[2,128,8,128]{3,1,2,0:T(8,128)(2,1)S(1)} %pad_maximum_fusion.1), channel_id=1, source_target_pairs={{4,0},{8,4},{12,8},{16,12},{20,16},{24,20},{28,24},{32,28},{36,32}... | collective-permute-start | bytes 1572872 | tf_op jit(solution)/shard_map/ppermute | solution.py:16
  204.5 19.9 %collective-permute-start.3 = (bf16[2,128,8,128]{3,1,2,0:T(8,128)(2,1)S(1)}, bf16[2,128,8,128]{3,1,2,0:T(8,128)(2,1)S(1)}, u32[]{:S(2)}, u32[]{:S(2)}) collective-permute-start(bf16[2,128,8,128]{3,1,2,0:T(8,128)(2,1)S(1)} %pad_maximum_fusion.2), channel_id=1, source_target_pairs={{8,0},{12,4},{16,8},{20,12},{24,16},{28,20},{32,24},{36,28},{40,32... | collective-permute-start | bytes 1572872 | tf_op jit(solution)/shard_map/ppermute | solution.py:16
  207.6 1.6 copy-start.6
Sparse Core Ops, SparseCore 0:
  16.4 149.9 all-gather.4
  194.9 290.9 all-gather.6
where the time goes:
time: 669 us; the launch traced here: 665 us
  waiting for transfers between devices  273 us (41%)
  blocking collectives  148 us (22%)
  other arithmetic  90.3 us (13%)
  local copies, waits for them, and re-layouts  53.1 us (8%)
  loops' own time  45.3 us (7%)
  matrix products  29.8 us (4%)
  between operations  17.1 us (3%)
  starting transfers between devices  8 us (1%)
    all_gather x2, waiting for transfers between devices, carried_in(): gathered = jax.tree.map(lambda a: lax.all_gather(a, axis), part)  260 us
    unnamed x1, blocking collectives  140 us
    add x63, other arithmetic, join_states(): later[0] + (1.0 - later[1]) * earlier[0]  78.5 us
    another operation x2, loops' own time, carried_in(): return lax.fori_loop(0, ahead, one, state)  45.3 us
    dynamic_slice x63, local copies, waits for them, and re-layouts, one(): lax.dynamic_index_in_dim(a, source, 0, False)  41.9 us
    dot_general x25, matrix products, narrow(): return jnp.einsum(form, left, right, preferred_element_type=jnp.float32)  26.7 us
  transfers between devices with their start and end apart: 6, of which 2 were waited for; matrix products, arithmetic and copies ran while one was open for 5% of the time, Pallas kernels for 0%

commit v1 on v0

--- a/solution.py
+++ b/solution.py
@@ -4,6 +4,7 @@
 from jax.sharding import PartitionSpec as P
 
 SPAN = 2
+MAXDOC = 2048
 
 
 neg_large = -1e30
@@ -16,20 +17,31 @@
     return lax.ppermute(x, axis, pairs)
 
 
-def carried_in(part, axis, combine, identity, reverse):
-    count = lax.axis_size(axis)
-    place = lax.axis_index(axis)
-    ahead = count - 1 - place if reverse else place
-    gathered = jax.tree.map(lambda a: lax.all_gather(a, axis), part)
-    state = jax.tree.map(lambda a, e: jnp.zeros_like(a) + jnp.asarray(e, a.dtype), part, identity)
-
-    def one(hop, state):
-        source = count - 1 - hop if reverse else hop
-        return combine(
-            state, jax.tree.map(lambda a: lax.dynamic_index_in_dim(a, source, 0, False), gathered)
-        )
-
-    return lax.fori_loop(0, ahead, one, state)
+def tile_state(keys_t, values_t, doc_lengths, start):
+    tile = keys_t.shape[0]
+    docs = doc_index(doc_lengths, start + jnp.arange(tile, dtype=jnp.int32))
+    keep = (docs == docs[tile - 1])[:, None, None]
+    state = narrow("uhd,uhe->hde", jnp.where(keep, keys_t, jnp.zeros_like(keys_t)), values_t)
+    flag = (one_doc(doc_lengths, start - 1) != docs[tile - 1]).astype(jnp.float32)
+    return (state, flag)
+
+
+def scan_from_window(window, covered, need, axis):
+    while covered < need:
+        window = join_states(from_behind(window, axis, covered), window)
+        covered *= 2
+    return window
+
+
+def suffix_scan(part, need, axis):
+    covered = 1
+    while 2 * covered < need:
+        part = join_states(from_behind(part, axis, -covered), part)
+        covered *= 2
+    near = from_behind(part, axis, -1)
+    if covered >= need:
+        return near
+    return join_states(from_behind(part, axis, -1 - covered), near)
 
 
 def wide(form, left, right):
@@ -108,17 +120,21 @@
     same_tile = masks[SPAN].astype(jnp.float32)
     carried_prev = (own_doc == prev_doc).astype(jnp.float32)
     carried_next = (own_doc == next_doc).astype(jnp.float32)
-    keep_last = (own_doc == own_doc[tile - 1])[:, None, None]
     keep_first = (own_doc == own_doc[0])[:, None, None]
-    reset_front = (prev_doc != own_doc[tile - 1]).astype(jnp.float32)
     reset_back = (next_doc != own_doc[0]).astype(jnp.float32)
     query_wide = queries.astype(jnp.float32)
     attend = (narrow("thd,uhd->htu", queries, keys) * same_tile).astype(jnp.bfloat16)
-    local_state = narrow("uhd,uhe->hde", jnp.where(keep_last, keys, jnp.zeros_like(keys)), values)
-    zero_state = jnp.zeros_like(local_state)
-    incoming, front_flag = carried_in(
-        (local_state, reset_front), "ctx", join_states, (zero_state, jnp.float32(0.0)), False
-    )
+    need = min(-(-MAXDOC // tile), lax.axis_size("ctx"))
+    window = tile_state(key_tiles[0], value_tiles[0], doc_lengths, base - SPAN * tile)
+    for position in range(1, SPAN):
+        window = join_states(
+            window,
+            tile_state(
+                key_tiles[position], value_tiles[position], doc_lengths,
+                base - (SPAN - position) * tile,
+            ),
+        )
+    incoming, front_flag = scan_from_window(window, SPAN, need, "ctx")
     linear_out = (
         narrow("htu,uhd->thd", attend, values)
         + wide("thd,hde->the", query_wide, incoming) * carried_prev[:, None, None]
@@ -150,9 +166,7 @@
     tile_sum = narrow(
         "thd,the->hde", jnp.where(keep_first, queries, jnp.zeros_like(queries)), inner
     )
-    later, back_flag = carried_in(
-        (tile_sum, reset_back), "ctx", join_states, (zero_state, jnp.float32(0.0)), True
-    )
+    later, back_flag = suffix_scan((tile_sum, reset_back), need, "ctx")
     key_linear = (
         narrow("htu,thd->uhd", back, queries)
         + wide("uhe,hde->uhd", values.astype(jnp.float32), later) * carried_next[:, None, None]

time: 669 us -> 220 us (0.33)
  the two profiles are of different devices: /device:TPU:8 before, /device:TPU:103 now
where the time goes in v1:
time: 220 us; the launch traced here: 216 us
  waiting for transfers between devices  110 us (50%)
  starting transfers between devices  61.2 us (28%)
  matrix products  13.6 us (6%)
  between operations  9.13 us (4%)
  blocking collectives  8.71 us (4%)
  local copies, waits for them, and re-layouts  8.3 us (4%)
  other arithmetic  4.79 us (2%)
    ppermute x18, waiting for transfers between devices, from_behind(): return lax.ppermute(x, axis, pairs)  110 us
    ppermute x18, starting transfers between devices, from_behind(): return lax.ppermute(x, axis, pairs)  61.2 us
    dot_general x26, matrix products, narrow(): return jnp.einsum(form, left, right, preferred_element_type=jnp.float32)  10.3 us
    psum x1, blocking collectives, per_device(): squares = lax.psum(jnp.sum(linear_out * linear_out, axis=(1, 2)), 'head')  8.71 us
    unnamed x40, local copies, waits for them, and re-layouts  5.83 us
  transfers between devices with their start and end apart: 18, of which 11 were waited for; matrix products, arithmetic and copies ran while one was open for 7% of the time, Pallas kernels for 0%

profile of v1, /device:TPU:103, one launch (start us, length us, event | category | flops | bytes accessed | tf_op | source)
XLA Modules:
  0.0 216.2 jit_solution(5376948834445775825)
XLA Ops:
  0.6 1.1 copy_bitcast_fusion
  1.9 4.8 %collective-permute-start.1 = (bf16[2,128,8,128]{3,1,2,0:T(8,128)(2,1)S(1)}, bf16[2,128,8,128]{3,1,2,0:T(8,128)(2,1)S(1)}, u32[]{:S(2)}, u32[]{:S(2)}) collective-permute-start(bf16[2,128,8,128]{3,1,2,0:T(8,128)(2,1)S(1)} %pad_maximum_fusion), channel_id=1, source_target_pairs={{0,8},{4,12},{8,16},{12,20},{16,24},{20,28},{24,32},{28,36},{32,40... | collective-permute-start | bytes 1572872 | tf_op jit(solution)/shard_map/ppermute | solution.py:17
  6.7 4.0 %collective-permute-start = (bf16[2,128,8,128]{3,1,2,0:T(8,128)(2,1)S(1)}, bf16[2,128,8,128]{3,1,2,0:T(8,128)(2,1)S(1)}, u32[]{:S(2)}, u32[]{:S(2)}) collective-permute-start(bf16[2,128,8,128]{3,1,2,0:T(8,128)(2,1)S(1)} %pad_maximum_fusion), channel_id=1, source_target_pairs={{0,4},{4,8},{8,12},{12,16},{16,20},{20,24},{24,28},{28,32},{32,36}... | collective-permute-start | bytes 1572872 | tf_op jit(solution)/shard_map/ppermute | solution.py:17
  11.0 0.7 fusion.100
  12.4 0.6 slice.36
  13.7 0.7 slice.39
  15.7 8.4 %collective-permute-start.3 = (f32[]{:T(128)}, f32[]{:T(128)}, u32[]{:S(2)}, u32[]{:S(2)}) collective-permute-start(f32[]{:T(128)} %max.38), channel_id=1, source_target_pairs={{0,8},{4,12},{8,16},{12,20},{16,24},{20,28},{24,32},{28,36},{32,40... | collective-permute-start | bytes 20 | tf_op jit(solution)/shard_map/ppermute | solution.py:17
  24.7 2.9 %collective-permute-start.8 = (f32[]{:T(128)}, f32[]{:T(128)}, u32[]{:S(2)}, u32[]{:S(2)}) collective-permute-start(f32[]{:T(128)} %convert_element_type.135), channel_id=1, source_target_pairs={{4,0},{8,4},{12,8},{16,12},{20,16},{24,20},{28,24},{32,28},{36,32}... | collective-permute-start | bytes 20 | tf_op jit(solution)/shard_map/ppermute | solution.py:17
  27.8 0.3 fusion.53
  28.1 1.3 broadcast_compare_fusion.1
  30.2 1.1 convolution_bitcast_fusion.4
  32.0 4.8 %collective-permute-start.5 = (f32[]{:T(128)}, f32[]{:T(128)}, u32[]{:S(2)}, u32[]{:S(2)}) collective-permute-start(f32[]{:T(128)} %max.39), channel_id=1, source_target_pairs={{0,16},{4,20},{8,24},{12,28},{16,32},{20,36},{24,40},{28,44},{32,4... | collective-permute-start | bytes 20 | tf_op jit(solution)/shard_map/ppermute | solution.py:17
  37.3 2.6 %collective-permute-start.10 = (f32[]{:T(128)}, f32[]{:T(128)}, u32[]{:S(2)}, u32[]{:S(2)}) collective-permute-start(f32[]{:T(128)} %max.43), channel_id=1, source_target_pairs={{8,0},{12,4},{16,8},{20,12},{24,16},{28,20},{32,24},{36,28},{40,32... | collective-permute-start | bytes 20 | tf_op jit(solution)/shard_map/ppermute | solution.py:17
  39.9 5.0 %collective-permute-done.10 = f32[]{:T(128)} collective-permute-done((f32[]{:T(128)}, f32[]{:T(128)}, u32[]{:S(2)}, u32[]{:S(2)}) %collective-permute-start.10) | collective-permute-done | bytes 36 | tf_op jit(solution)/shard_map/ppermute | solution.py:17
  45.5 2.6 %collective-permute-start.13 = (f32[]{:T(128)}, f32[]{:T(128)}, u32[]{:S(2)}, u32[]{:S(2)}) collective-permute-start(f32[]{:T(128)} %max.44), channel_id=1, source_target_pairs={{16,0},{20,4},{24,8},{28,12},{32,16},{36,20},{40,24},{44,28},{48,3... | collective-permute-start | bytes 20 | tf_op jit(solution)/shard_map/ppermute | solution.py:17
  48.8 4.5 %collective-permute-done.13 = f32[]{:T(128)} collective-permute-done((f32[]{:T(128)}, f32[]{:T(128)}, u32[]{:S(2)}, u32[]{:S(2)}) %collective-permute-start.13) | collective-permute-done | bytes 36 | tf_op jit(solution)/shard_map/ppermute | solution.py:17
  53.9 7.1 %collective-permute-start.14 = (f32[]{:T(128)}, f32[]{:T(128)}, u32[]{:S(2)}, u32[]{:S(2)}) collective-permute-start(f32[]{:T(128)} %max.45), channel_id=1, source_target_pairs={{4,0},{8,4},{12,8},{16,12},{20,16},{24,20},{28,24},{32,28},{36,32}... | collective-permute-start | bytes 20 | tf_op jit(solution)/shard_map/ppermute | solution.py:17
  61.1 1.2 collective-permute-done.14
  62.9 0.4 convolution_multiply_fusion.7
  63.3 0.4 convolution_add_fusion.2
  63.7 1.9 collective-permute-start.2
  65.6 0.3 fusion.108
  65.9 0.3 fusion.109
  66.6 0.6 copy-done
  67.2 0.9 fusion.39
  68.1 10.9 %collective-permute-done.2 = f32[8,128,128]{2,1,0:T(8,128)S(1)} collective-permute-done((f32[8,128,128]{2,1,0:T(8,128)S(1)}, f32[8,128,128]{2,1,0:T(8,128)S(1)}, u32[]{:S(2)}, u32[]{:S(2)}) %collective-permute-start.2) | collective-permute-done | bytes 524320 | tf_op jit(solution)/shard_map/ppermute | solution.py:17
  79.1 1.9 collective-permute-start.4
  81.1 0.9 fusion.38
  82.0 0.3 convolution_bitcast_fusion.3
  82.3 1.1 convolution_bitcast_fusion
  83.4 12.2 %collective-permute-done.4 = f32[8,128,128]{2,1,0:T(8,128)S(1)} collective-permute-done((f32[8,128,128]{2,1,0:T(8,128)S(1)}, f32[8,128,128]{2,1,0:T(8,128)S(1)}, u32[]{:S(2)}, u32[]{:S(2)}) %collective-permute-start.4) | collective-permute-done | bytes 524320 | tf_op jit(solution)/shard_map/ppermute | solution.py:17
  95.7 2.1 collective-permute-start.6
  98.1 0.3 fusion.12
  98.4 11.6 %collective-permute-done.6 = f32[8,128,128]{2,1,0:T(8,128)S(1)} collective-permute-done((f32[8,128,128]{2,1,0:T(8,128)S(1)}, f32[8,128,128]{2,1,0:T(8,128)S(1)}, u32[]{:S(2)}, u32[]{:S(2)}) %collective-permute-start.6) | collective-permute-done | bytes 524320 | tf_op jit(solution)/shard_map/ppermute | solution.py:17
  110.0 1.4 fusion.44
  111.3 8.7 %all-reduce = (f32[128]{0:T(128)S(1)}, f32[128]{0:T(128)S(1)}) all-reduce(f32[128]{0:T(128)S(1)} %get-tuple-element.17, f32[128]{0:T(128)S(1)} %get-tuple-element.16), channel_id=1, replica_groups=mesh['ctx'=64,'head'=4] {'head'}, use_global_device_ids=true, to_apply=%region_8.9 | all-reduce | flops 256 | bytes 2048 | tf_op jit(solution)/shard_map/psum | solution.py:142
  120.1 1.3 fusion.43
  121.4 0.3 fusion.33
  121.7 0.7 copy-done.7
  122.4 0.3 fusion.30
  123.0 0.7 copy-done.15
  123.7 2.1 collective-permute-start.17
  125.8 0.3 fusion.31
  126.4 0.3 fusion.54
  126.7 6.2 %collective-permute-start.7 = (f32[8,128,128]{2,1,0:T(8,128)S(1)}, f32[8,128,128]{2,1,0:T(8,128)S(1)}, u32[]{:S(2)}, u32[]{:S(2)}) collective-permute-start(f32[8,128,128]{2,1,0:T(8,128)S(1)} %fusion.54), channel_id=1, source_target_pairs={{4,0},{8,4},{12,8},{16,12},{20,16},{24,20},{28,24},{32,28},{36,32}... | collective-permute-start | bytes 1572872 | tf_op jit(solution)/shard_map/ppermute | solution.py:17
  133.0 1.9 collective-permute-start.16
  135.5 13.8 %collective-permute-done.7 = f32[8,128,128]{2,1,0:T(8,128)S(1)} collective-permute-done((f32[8,128,128]{2,1,0:T(8,128)S(1)}, f32[8,128,128]{2,1,0:T(8,128)S(1)}, u32[]{:S(2)}, u32[]{:S(2)}) %collective-permute-start.7) | collective-permute-done | bytes 524320 | tf_op jit(solution)/shard_map/ppermute | solution.py:17
  149.4 2.1 collective-permute-start.9
  151.7 0.7 fusion.24
  152.4 13.7 %collective-permute-done.9 = f32[8,128,128]{2,1,0:T(8,128)S(1)} collective-permute-done((f32[8,128,128]{2,1,0:T(8,128)S(1)}, f32[8,128,128]{2,1,0:T(8,128)S(1)}, u32[]{:S(2)}, u32[]{:S(2)}) %collective-permute-start.9) | collective-permute-done | bytes 524320 | tf_op jit(solution)/shard_map/ppermute | solution.py:17
  166.2 1.9 collective-permute-start.11
  168.1 0.3 fusion.32
  168.4 0.3 fusion.27
  168.7 15.5 %collective-permute-done.11 = f32[8,128,128]{2,1,0:T(8,128)S(1)} collective-permute-done((f32[8,128,128]{2,1,0:T(8,128)S(1)}, f32[8,128,128]{2,1,0:T(8,128)S(1)}, u32[]{:S(2)}, u32[]{:S(2)}) %collective-permute-start.11) | collective-permute-done | bytes 524320 | tf_op jit(solution)/shard_map/ppermute | solution.py:17
  184.3 1.9 collective-permute-start.12
  186.3 2.1 collective-permute-start.15
  188.6 0.9 copy.204
  189.5 0.9 copy.205
  191.0 15.0 %collective-permute-done.12 = f32[8,128,128]{2,1,0:T(8,128)S(1)} collective-permute-done((f32[8,128,128]{2,1,0:T(8,128)S(1)}, f32[8,128,128]{2,1,0:T(8,128)S(1)}, u32[]{:S(2)}, u32[]{:S(2)}) %collective-permute-start.12) | collective-permute-done | bytes 524320 | tf_op jit(solution)/shard_map/ppermute | solution.py:17
  206.1 6.9 %collective-permute-done.15 = f32[8,128,128]{2,1,0:T(8,128)S(1)} collective-permute-done((f32[8,128,128]{2,1,0:T(8,128)S(1)}, f32[8,128,128]{2,1,0:T(8,128)S(1)}, u32[]{:S(2)}, u32[]{:S(2)}) %collective-permute-start.15) | collective-permute-done | bytes 524320 | tf_op jit(solution)/shard_map/ppermute | solution.py:17
  213.0 0.7 fusion.28
  213.8 0.9 copy.206
  214.8 0.5 fusion.29
  215.3 0.9 copy.207
  (75 shorter events, 4.0 us)
Async XLA Ops:
  1.8 8.9 %copy-start.17 = (s32[64]{0:T(128)S(1)}, s32[64]{0:T(128)}, u32[]{:S(2)}) copy-start(s32[64]{0:T(128)} %param.10) | copy-start | bytes 772
  1.8 26.0 %copy-start.3 = (bf16[128,8,128]{2,1,0:T(8,128)(2,1)S(1)}, bf16[128,8,128]{2,1,0:T(8,128)(2,1)}, u32[]{:S(2)}) copy-start(bf16[128,8,128]{2,1,0:T(8,128)(2,1)} %param.7) | copy-start | bytes 786436
  1.8 25.9 %copy-start.1 = (bf16[128,8,128]{2,1,0:T(8,128)(2,1)S(1)}, bf16[128,8,128]{2,1,0:T(8,128)(2,1)}, u32[]{:S(2)}) copy-start(bf16[128,8,128]{2,1,0:T(8,128)(2,1)} %param.6) | copy-start | bytes 786436
  1.9 61.1 %collective-permute-start.1 = (bf16[2,128,8,128]{3,1,2,0:T(8,128)(2,1)S(1)}, bf16[2,128,8,128]{3,1,2,0:T(8,128)(2,1)S(1)}, u32[]{:S(2)}, u32[]{:S(2)}) collective-permute-start(bf16[2,128,8,128]{3,1,2,0:T(8,128)(2,1)S(1)} %pad_maximum_fusion), channel_id=1, source_target_pairs={{0,8},{4,12},{8,16},{12,20},{16,24},{20,28},{24,32},{28,36},{32,40... | collective-permute-start | bytes 1572872 | tf_op jit(solution)/shard_map/ppermute | solution.py:17
  6.7 56.6 %collective-permute-start = (bf16[2,128,8,128]{3,1,2,0:T(8,128)(2,1)S(1)}, bf16[2,128,8,128]{3,1,2,0:T(8,128)(2,1)S(1)}, u32[]{:S(2)}, u32[]{:S(2)}) collective-permute-start(bf16[2,128,8,128]{3,1,2,0:T(8,128)(2,1)S(1)} %pad_maximum_fusion), channel_id=1, source_target_pairs={{0,4},{4,8},{8,12},{12,16},{16,20},{20,24},{24,28},{28,32},{32,36}... | collective-permute-start | bytes 1572872 | tf_op jit(solution)/shard_map/ppermute | solution.py:17
  15.7 15.6 %collective-permute-start.3 = (f32[]{:T(128)}, f32[]{:T(128)}, u32[]{:S(2)}, u32[]{:S(2)}) collective-permute-start(f32[]{:T(128)} %max.38), channel_id=1, source_target_pairs={{0,8},{4,12},{8,16},{12,20},{16,24},{20,28},{24,32},{28,36},{32,40... | collective-permute-start | bytes 20 | tf_op jit(solution)/shard_map/ppermute | solution.py:17
  24.7 12.0 %collective-permute-start.8 = (f32[]{:T(128)}, f32[]{:T(128)}, u32[]{:S(2)}, u32[]{:S(2)}) collective-permute-start(f32[]{:T(128)} %convert_element_type.135), channel_id=1, source_target_pairs={{4,0},{8,4},{12,8},{16,12},{20,16},{24,20},{28,24},{32,28},{36,32}... | collective-permute-start | bytes 20 | tf_op jit(solution)/shard_map/ppermute | solution.py:17
  27.8 2.4 %copy-start.2 = (bf16[128,8,128]{2,1,0:T(8,128)(2,1)S(1)}, bf16[128,8,128]{2,1,0:T(8,128)(2,1)}, u32[]{:S(2)}) copy-start(bf16[128,8,128]{2,1,0:T(8,128)(2,1)} %param.8) | copy-start | bytes 786436
  32.0 16.1 %collective-permute-start.5 = (f32[]{:T(128)}, f32[]{:T(128)}, u32[]{:S(2)}, u32[]{:S(2)}) collective-permute-start(f32[]{:T(128)} %max.39), channel_id=1, source_target_pairs={{0,16},{4,20},{8,24},{12,28},{16,32},{20,36},{24,40},{28,44},{32,4... | collective-permute-start | bytes 20 | tf_op jit(solution)/shard_map/ppermute | solution.py:17
  37.3 7.6 %collective-permute-start.10 = (f32[]{:T(128)}, f32[]{:T(128)}, u32[]{:S(2)}, u32[]{:S(2)}) collective-permute-start(f32[]{:T(128)} %max.43), channel_id=1, source_target_pairs={{8,0},{12,4},{16,8},{20,12},{24,16},{28,20},{32,24},{36,28},{40,32... | collective-permute-start | bytes 20 | tf_op jit(solution)/shard_map/ppermute | solution.py:17
  45.5 7.9 %collective-permute-start.13 = (f32[]{:T(128)}, f32[]{:T(128)}, u32[]{:S(2)}, u32[]{:S(2)}) collective-permute-start(f32[]{:T(128)} %max.44), channel_id=1, source_target_pairs={{16,0},{20,4},{24,8},{28,12},{32,16},{36,20},{40,24},{44,28},{48,3... | collective-permute-start | bytes 20 | tf_op jit(solution)/shard_map/ppermute | solution.py:17
  53.9 8.3 %collective-permute-start.14 = (f32[]{:T(128)}, f32[]{:T(128)}, u32[]{:S(2)}, u32[]{:S(2)}) collective-permute-start(f32[]{:T(128)} %max.45), channel_id=1, source_target_pairs={{4,0},{8,4},{12,8},{16,12},{20,16},{24,20},{28,24},{32,28},{36,32}... | collective-permute-start | bytes 20 | tf_op jit(solution)/shard_map/ppermute | solution.py:17
  62.9 2.7 %copy-start.5 = (bf16[2,128,8,128]{3,1,2,0:T(8,128)(2,1)}, bf16[2,128,8,128]{3,1,2,0:T(8,128)(2,1)S(1)}, u32[]{:S(2)}) copy-start(bf16[2,128,8,128]{3,1,2,0:T(8,128)(2,1)S(1)} %collective-permute-done.1) | copy-start | bytes 1572868
  63.3 34.5 %copy-start.8 = (bf16[2,128,8,128]{3,1,2,0:T(8,128)(2,1)}, bf16[2,128,8,128]{3,1,2,0:T(8,128)(2,1)S(1)}, u32[]{:S(2)}) copy-start(bf16[2,128,8,128]{3,1,2,0:T(8,128)(2,1)S(1)} %collective-permute-done) | copy-start | bytes 1572868
  63.7 15.4 %collective-permute-start.2 = (f32[8,128,128]{2,1,0:T(8,128)S(1)}, f32[8,128,128]{2,1,0:T(8,128)S(1)}, u32[]{:S(2)}, u32[]{:S(2)}) collective-permute-start(f32[8,128,128]{2,1,0:T(8,128)S(1)} %convolution_add_fusion.2), channel_id=1, source_target_pairs={{0,8},{4,12},{8,16},{12,20},{16,24},{20,28},{24,32},{28,36},{32,40... | collective-permute-start | bytes 1572872 | tf_op jit(solution)/shard_map/ppermute | solution.py:17
  66.3 1.0 copy-start
  79.1 16.5 %collective-permute-start.4 = (f32[8,128,128]{2,1,0:T(8,128)S(1)}, f32[8,128,128]{2,1,0:T(8,128)S(1)}, u32[]{:S(2)}, u32[]{:S(2)}) collective-permute-start(f32[8,128,128]{2,1,0:T(8,128)S(1)} %multiply_add_fusion.6), channel_id=1, source_target_pairs={{0,16},{4,20},{8,24},{12,28},{16,32},{20,36},{24,40},{28,44},{32,4... | collective-permute-start | bytes 1572872 | tf_op jit(solution)/shard_map/ppermute | solution.py:17
  95.7 2.4 %copy-start.6 = (bf16[2,128,8,128]{3,1,2,0:T(8,128)(2,1)S(1)}, bf16[2,128,8,128]{3,1,2,0:T(8,128)(2,1)}, u32[]{:S(2)}) copy-start(bf16[2,128,8,128]{3,1,2,0:T(8,128)(2,1)} %copy-done.5) | copy-start | bytes 1572868
  95.7 14.3 %collective-permute-start.6 = (f32[8,128,128]{2,1,0:T(8,128)S(1)}, f32[8,128,128]{2,1,0:T(8,128)S(1)}, u32[]{:S(2)}, u32[]{:S(2)}) collective-permute-start(f32[8,128,128]{2,1,0:T(8,128)S(1)} %multiply_add_fusion.5), channel_id=1, source_target_pairs={{0,32},{4,36},{8,40},{12,44},{16,48},{20,52},{24,56},{28,60},{32,6... | collective-permute-start | bytes 1572872 | tf_op jit(solution)/shard_map/ppermute | solution.py:17
  98.1 11.9 %copy-start.10 = (f32[128,8,128]{2,0,1:T(8,128)S(1)}, f32[128,8,128]{2,0,1:T(8,128)}, u32[]{:S(2)}) copy-start(f32[128,8,128]{2,0,1:T(8,128)} %convolution_bitcast_fusion.4) | copy-start | bytes 1572868
  98.1 11.9 %copy-start.16 = (f32[8,128]{1,0:T(8,128)S(1)}, f32[8,128]{1,0:T(8,128)}, u32[]{:S(2)}) copy-start(f32[8,128]{1,0:T(8,128)} %param.9) | copy-start | bytes 12292
  110.0 1.4 copy-start.12
  121.4 1.0 copy-start.7
  122.7 1.0 copy-start.15
  123.7 2.1 copy-start.9
  123.7 67.1 %collective-permute-start.17 = (bf16[2,128,8,128]{3,1,2,0:T(8,128)(2,1)S(1)}, bf16[2,128,8,128]{3,1,2,0:T(8,128)(2,1)S(1)}, u32[]{:S(2)}, u32[]{:S(2)}) collective-permute-start(bf16[2,128,8,128]{3,1,2,0:T(8,128)(2,1)S(1)} %pad_maximum_fusion.2), channel_id=1, source_target_pairs={{8,0},{12,4},{16,8},{20,12},{24,16},{28,20},{32,24},{36,28},{40,32... | collective-permute-start | bytes 1572872 | tf_op jit(solution)/shard_map/ppermute | solution.py:17
  126.4 6.5 %copy-start.14 = (bf16[1,128,8,128]{3,1,2,0:T(8,128)(2,1)S(1)}, bf16[1,128,8,128]{3,1,2,0:T(8,128)(2,1)}, u32[]{:S(2)}) copy-start(bf16[1,128,8,128]{3,1,2,0:T(8,128)(2,1)} %fusion.38) | copy-start | bytes 786436
  126.7 22.6 %collective-permute-start.7 = (f32[8,128,128]{2,1,0:T(8,128)S(1)}, f32[8,128,128]{2,1,0:T(8,128)S(1)}, u32[]{:S(2)}, u32[]{:S(2)}) collective-permute-start(f32[8,128,128]{2,1,0:T(8,128)S(1)} %fusion.54), channel_id=1, source_target_pairs={{4,0},{8,4},{12,8},{16,12},{20,16},{24,20},{28,24},{32,28},{36,32}... | collective-permute-start | bytes 1572872 | tf_op jit(solution)/shard_map/ppermute | solution.py:17
  133.0 57.9 %collective-permute-start.16 = (bf16[2,128,8,128]{3,1,2,0:T(8,128)(2,1)S(1)}, bf16[2,128,8,128]{3,1,2,0:T(8,128)(2,1)S(1)}, u32[]{:S(2)}, u32[]{:S(2)}) collective-permute-start(bf16[2,128,8,128]{3,1,2,0:T(8,128)(2,1)S(1)} %pad_maximum_fusion.1), channel_id=1, source_target_pairs={{4,0},{8,4},{12,8},{16,12},{20,16},{24,20},{28,24},{32,28},{36,32}... | collective-permute-start | bytes 1572872 | tf_op jit(solution)/shard_map/ppermute | solution.py:17
  135.5 16.0 %copy-start.4 = (bf16[128,8,128]{2,1,0:T(8,128)(2,1)S(1)}, bf16[128,8,128]{2,1,0:T(8,128)(2,1)}, u32[]{:S(2)}) copy-start(bf16[128,8,128]{2,1,0:T(8,128)(2,1)} %param.7) | copy-start | bytes 786436
  149.4 2.4 %copy-start.13 = (f32[8,128,128]{2,1,0:T(8,128)S(1)}, f32[8,128,128]{2,1,0:T(8,128)}, u32[]{:S(2)}) copy-start(f32[8,128,128]{2,1,0:T(8,128)} %copy-done.12) | copy-start | bytes 1572868
  149.4 16.8 %collective-permute-start.9 = (f32[8,128,128]{2,1,0:T(8,128)S(1)}, f32[8,128,128]{2,1,0:T(8,128)S(1)}, u32[]{:S(2)}, u32[]{:S(2)}) collective-permute-start(f32[8,128,128]{2,1,0:T(8,128)S(1)} %multiply_add_fusion.3), channel_id=1, source_target_pairs={{8,0},{12,4},{16,8},{20,12},{24,16},{28,20},{32,24},{36,28},{40,32... | collective-permute-start | bytes 1572872 | tf_op jit(solution)/shard_map/ppermute | solution.py:17
  166.2 18.1 %collective-permute-start.11 = (f32[8,128,128]{2,1,0:T(8,128)S(1)}, f32[8,128,128]{2,1,0:T(8,128)S(1)}, u32[]{:S(2)}, u32[]{:S(2)}) collective-permute-start(f32[8,128,128]{2,1,0:T(8,128)S(1)} %multiply_add_fusion.2), channel_id=1, source_target_pairs={{16,0},{20,4},{24,8},{28,12},{32,16},{36,20},{40,24},{44,28},{48,3... | collective-permute-start | bytes 1572872 | tf_op jit(solution)/shard_map/ppermute | solution.py:17
  184.3 21.7 %collective-permute-start.12 = (f32[8,128,128]{2,1,0:T(8,128)S(1)}, f32[8,128,128]{2,1,0:T(8,128)S(1)}, u32[]{:S(2)}, u32[]{:S(2)}) collective-permute-start(f32[8,128,128]{2,1,0:T(8,128)S(1)} %multiply_add_fusion.1), channel_id=1, source_target_pairs={{4,0},{8,4},{12,8},{16,12},{20,16},{24,20},{28,24},{32,28},{36,32}... | collective-permute-start | bytes 1572872 | tf_op jit(solution)/shard_map/ppermute | solution.py:17
  186.3 26.7 %collective-permute-start.15 = (f32[8,128,128]{2,1,0:T(8,128)S(1)}, f32[8,128,128]{2,1,0:T(8,128)S(1)}, u32[]{:S(2)}, u32[]{:S(2)}) collective-permute-start(f32[8,128,128]{2,1,0:T(8,128)S(1)} %multiply_add_fusion.1), channel_id=1, source_target_pairs={{36,0},{40,4},{44,8},{48,12},{52,16},{56,20},{60,24},{64,28},{68,3... | collective-permute-start | bytes 1572872 | tf_op jit(solution)/shard_map/ppermute | solution.py:17
  213.7 1.0 copy-start.11

commit v2 on v0

--- a/solution.py
+++ b/solution.py
@@ -4,6 +4,7 @@
 from jax.sharding import PartitionSpec as P
 
 SPAN = 2
+MAXDOC = 2048
 
 
 neg_large = -1e30
@@ -16,20 +17,34 @@
     return lax.ppermute(x, axis, pairs)
 
 
-def carried_in(part, axis, combine, identity, reverse):
-    count = lax.axis_size(axis)
-    place = lax.axis_index(axis)
-    ahead = count - 1 - place if reverse else place
-    gathered = jax.tree.map(lambda a: lax.all_gather(a, axis), part)
-    state = jax.tree.map(lambda a, e: jnp.zeros_like(a) + jnp.asarray(e, a.dtype), part, identity)
-
-    def one(hop, state):
-        source = count - 1 - hop if reverse else hop
-        return combine(
-            state, jax.tree.map(lambda a: lax.dynamic_index_in_dim(a, source, 0, False), gathered)
-        )
-
-    return lax.fori_loop(0, ahead, one, state)
+def tile_state(keys_t, values_t, doc_lengths, start):
+    tile = keys_t.shape[0]
+    docs = doc_index(doc_lengths, start + jnp.arange(tile, dtype=jnp.int32))
+    keep = (docs == docs[tile - 1])[:, None, None]
+    return narrow("uhd,uhe->hde", jnp.where(keep, keys_t, jnp.zeros_like(keys_t)), values_t)
+
+
+def fold_states(pieces, flags):
+    total = pieces[0]
+    for piece, flag in zip(pieces[1:], flags[1:]):
+        total = piece + (1.0 - flag) * total
+    return total
+
+
+def front_flags(doc_lengths, spans, tile):
+    low = jnp.stack([lo * tile - 1 for lo, hi in spans])
+    high = jnp.stack([hi * tile + tile - 1 for lo, hi in spans])
+    docs = doc_index(doc_lengths, jnp.concatenate([low, high]).astype(jnp.int32))
+    count = len(spans)
+    return (docs[:count] != docs[count:]).astype(jnp.float32)
+
+
+def back_flags(doc_lengths, spans, tile):
+    low = jnp.stack([lo * tile for lo, hi in spans])
+    high = jnp.stack([hi * tile + tile for lo, hi in spans])
+    docs = doc_index(doc_lengths, jnp.concatenate([low, high]).astype(jnp.int32))
+    count = len(spans)
+    return (docs[:count] != docs[count:]).astype(jnp.float32)
 
 
 def wide(form, left, right):
@@ -47,10 +62,6 @@
 
 def one_doc(doc_lengths, position):
     return doc_index(doc_lengths, jnp.reshape(position, (1,)))[0]
-
-
-def join_states(earlier, later):
-    return (later[0] + (1.0 - later[1]) * earlier[0], jnp.maximum(earlier[1], later[1]))
 
 
 def masked_scores(query_block, key_block, mask, scale):
@@ -108,16 +119,31 @@
     same_tile = masks[SPAN].astype(jnp.float32)
     carried_prev = (own_doc == prev_doc).astype(jnp.float32)
     carried_next = (own_doc == next_doc).astype(jnp.float32)
-    keep_last = (own_doc == own_doc[tile - 1])[:, None, None]
     keep_first = (own_doc == own_doc[0])[:, None, None]
-    reset_front = (prev_doc != own_doc[tile - 1]).astype(jnp.float32)
-    reset_back = (next_doc != own_doc[0]).astype(jnp.float32)
     query_wide = queries.astype(jnp.float32)
     attend = (narrow("thd,uhd->htu", queries, keys) * same_tile).astype(jnp.bfloat16)
-    local_state = narrow("uhd,uhe->hde", jnp.where(keep_last, keys, jnp.zeros_like(keys)), values)
-    zero_state = jnp.zeros_like(local_state)
-    incoming, front_flag = carried_in(
-        (local_state, reset_front), "ctx", join_states, (zero_state, jnp.float32(0.0)), False
+    place = lax.axis_index("ctx")
+    need = min(-(-MAXDOC // tile), lax.axis_size("ctx"))
+    group = SPAN + 2
+    rounds = -(-need // group)
+    own_state = tile_state(keys, values, doc_lengths, base)
+    far_states = [
+        from_behind(own_state, "ctx", shift) for shift in range(group - 1, SPAN, -1)
+    ]
+    near_states = [
+        tile_state(key_tiles[position], value_tiles[position], doc_lengths,
+                   base - (SPAN - position) * tile)
+        for position in range(SPAN)
+    ]
+    group_spans = [(place - shift, place - shift) for shift in range(group - 1, -1, -1)]
+    group_state = fold_states(
+        far_states + near_states + [own_state], front_flags(doc_lengths, group_spans, tile)
+    )
+    shifts = [1 + group * k for k in range(rounds - 1, -1, -1)]
+    window_spans = [(place - shift - group + 1, place - shift) for shift in shifts]
+    incoming = fold_states(
+        [from_behind(group_state, "ctx", shift) for shift in shifts],
+        front_flags(doc_lengths, window_spans, tile),
     )
     linear_out = (
         narrow("htu,uhd->thd", attend, values)
@@ -150,8 +176,15 @@
     tile_sum = narrow(
         "thd,the->hde", jnp.where(keep_first, queries, jnp.zeros_like(queries)), inner
     )
-    later, back_flag = carried_in(
-        (tile_sum, reset_back), "ctx", join_states, (zero_state, jnp.float32(0.0)), True
+    back_states = [
+        from_behind(tile_sum, "ctx", -shift) for shift in range(group - 1, 0, -1)
+    ] + [tile_sum]
+    back_spans = [(place + shift, place + shift) for shift in range(group - 1, -1, -1)]
+    back_group = fold_states(back_states, back_flags(doc_lengths, back_spans, tile))
+    back_window = [(place + shift, place + shift + group - 1) for shift in shifts]
+    later = fold_states(
+        [from_behind(back_group, "ctx", -shift) for shift in shifts],
+        back_flags(doc_lengths, back_window, tile),
     )
     key_linear = (
         narrow("htu,thd->uhd", back, queries)

time: 669 us -> 235 us (0.35)
  the two profiles are of different devices: /device:TPU:8 before, /device:TPU:67 now
where the time goes in v2:
time: 235 us; the launch traced here: 234 us
  starting transfers between devices  95.2 us (41%)
  waiting for transfers between devices  83.6 us (36%)
  local copies, waits for them, and re-layouts  14.9 us (6%)
  matrix products  14.3 us (6%)
  between operations  10.3 us (4%)
  blocking collectives  8.7 us (4%)
  other arithmetic  7.28 us (3%)
    ppermute x16, starting transfers between devices, from_behind(): return lax.ppermute(x, axis, pairs)  95.2 us
    ppermute x16, waiting for transfers between devices, from_behind(): return lax.ppermute(x, axis, pairs)  83.6 us
    dot_general x27, matrix products, narrow(): return jnp.einsum(form, left, right, preferred_element_type=jnp.float32)  11.1 us
    unnamed x37, local copies, waits for them, and re-layouts  9 us
    psum x1, blocking collectives, per_device(): squares = lax.psum(jnp.sum(linear_out * linear_out, axis=(1, 2)), 'head')  8.7 us
  transfers between devices with their start and end apart: 16, of which 6 were waited for; matrix products, arithmetic and copies ran while one was open for 10% of the time, Pallas kernels for 0%

profile of v2, /device:TPU:67, one launch (start us, length us, event | category | flops | bytes accessed | tf_op | source)
XLA Modules:
  0.0 234.4 jit_solution(17210112491992321629)
XLA Ops:
  0.6 1.1 copy_bitcast_fusion
  1.8 0.8 pad_maximum_fusion
  2.6 3.1 %collective-permute-start.1 = (bf16[2,128,8,128]{3,1,2,0:T(8,128)(2,1)}, bf16[2,128,8,128]{3,1,2,0:T(8,128)(2,1)S(1)}, u32[]{:S(2)}, u32[]{:S(2)}) collective-permute-start(bf16[2,128,8,128]{3,1,2,0:T(8,128)(2,1)} %pad_maximum_fusion), channel_id=1, source_target_pairs={{0,8},{4,12},{8,16},{12,20},{16,24},{20,28},{24,32},{28,36},{32,40... | collective-permute-start | bytes 1572872 | tf_op jit(solution)/shard_map/ppermute | solution.py:17
  5.7 3.7 %collective-permute-start = (bf16[2,128,8,128]{3,1,2,0:T(8,128)(2,1)}, bf16[2,128,8,128]{3,1,2,0:T(8,128)(2,1)S(1)}, u32[]{:S(2)}, u32[]{:S(2)}) collective-permute-start(bf16[2,128,8,128]{3,1,2,0:T(8,128)(2,1)} %pad_maximum_fusion), channel_id=1, source_target_pairs={{0,4},{4,8},{8,12},{12,16},{16,20},{20,24},{24,28},{28,32},{32,36}... | collective-permute-start | bytes 1572872 | tf_op jit(solution)/shard_map/ppermute | solution.py:17
  9.5 0.6 copy-done.15
  10.4 0.7 fusion.105
  11.9 0.6 fusion.116
  13.2 1.2 compare_convert_fusion
  14.4 0.3 fusion.61
  14.8 3.2 %collective-permute-start.2 = (f32[8,128,128]{2,1,0:T(8,128)S(1)}, f32[8,128,128]{2,1,0:T(8,128)}, u32[]{:S(2)}, u32[]{:S(2)}) collective-permute-start(f32[8,128,128]{2,1,0:T(8,128)S(1)} %fusion.61), channel_id=1, source_target_pairs={{0,12},{4,16},{8,20},{12,24},{16,28},{20,32},{24,36},{28,40},{32,4... | collective-permute-start | bytes 1572872 | tf_op jit(solution)/shard_map/ppermute | solution.py:17
  18.0 0.7 slice.82
  18.8 0.6 slice.79
  20.1 0.6 fusion.118
  20.7 0.7 fusion.117
  21.5 0.7 fusion.115
  22.2 1.3 broadcast_compare_fusion.1
  23.5 0.7 fusion.114
  24.4 0.7 copy-done.1
  25.1 0.3 fusion.56
  33.0 0.3 convolution_bitcast_fusion.4
  33.3 1.6 fusion.17
  35.0 0.4 fusion.19
  35.3 5.5 %collective-permute-start.3 = (f32[8,128,128]{2,1,0:T(8,128)S(1)}, f32[8,128,128]{2,1,0:T(8,128)S(1)}, u32[]{:S(2)}, u32[]{:S(2)}) collective-permute-start(f32[8,128,128]{2,1,0:T(8,128)S(1)} %fusion.19), channel_id=1, source_target_pairs={{0,4},{4,8},{8,12},{12,16},{16,20},{20,24},{24,28},{28,32},{32,36}... | collective-permute-start | bytes 1572872 | tf_op jit(solution)/shard_map/ppermute | solution.py:17
  40.8 5.5 %collective-permute-start.4 = (f32[8,128,128]{2,1,0:T(8,128)S(1)}, f32[8,128,128]{2,1,0:T(8,128)S(1)}, u32[]{:S(2)}, u32[]{:S(2)}) collective-permute-start(f32[8,128,128]{2,1,0:T(8,128)S(1)} %fusion.19), channel_id=1, source_target_pairs={{0,20},{4,24},{8,28},{12,32},{16,36},{20,40},{24,44},{28,48},{32,5... | collective-permute-start | bytes 1572872 | tf_op jit(solution)/shard_map/ppermute | solution.py:17
  46.4 12.2 %collective-permute-start.5 = (f32[8,128,128]{2,1,0:T(8,128)S(1)}, f32[8,128,128]{2,1,0:T(8,128)S(1)}, u32[]{:S(2)}, u32[]{:S(2)}) collective-permute-start(f32[8,128,128]{2,1,0:T(8,128)S(1)} %fusion.19), channel_id=1, source_target_pairs={{0,36},{4,40},{8,44},{12,48},{16,52},{20,56},{24,60},{28,64},{32,6... | collective-permute-start | bytes 1572872 | tf_op jit(solution)/shard_map/ppermute | solution.py:17
  58.5 1.9 collective-permute-start.6
  61.4 0.3 convolution_bitcast_fusion.3
  61.7 0.6 copy-done
  62.3 0.9 fusion.42
  63.3 0.9 fusion.41
  64.2 1.0 convolution_bitcast_fusion
  65.6 0.8 copy-done.7
  66.6 4.2 %collective-permute-done.5 = f32[8,128,128]{2,1,0:T(8,128)S(1)} collective-permute-done((f32[8,128,128]{2,1,0:T(8,128)S(1)}, f32[8,128,128]{2,1,0:T(8,128)S(1)}, u32[]{:S(2)}, u32[]{:S(2)}) %collective-permute-start.5) | collective-permute-done | bytes 524320 | tf_op jit(solution)/shard_map/ppermute | solution.py:17
  70.8 11.6 %collective-permute-done.6 = f32[8,128,128]{2,1,0:T(8,128)S(1)} collective-permute-done((f32[8,128,128]{2,1,0:T(8,128)S(1)}, f32[8,128,128]{2,1,0:T(8,128)S(1)}, u32[]{:S(2)}, u32[]{:S(2)}) %collective-permute-start.6) | collective-permute-done | bytes 524320 | tf_op jit(solution)/shard_map/ppermute | solution.py:17
  82.5 0.6 copy-done.14
  83.1 1.4 fusion.47
  84.5 8.7 %all-reduce = (f32[128]{0:T(128)S(1)}, f32[128]{0:T(128)S(1)}) all-reduce(f32[128]{0:T(128)S(1)} %get-tuple-element.17, f32[128]{0:T(128)S(1)} %get-tuple-element.16), channel_id=1, replica_groups=mesh['ctx'=64,'head'=4] {'head'}, use_global_device_ids=true, to_apply=%region_8.9 | all-reduce | flops 256 | bytes 2048 | tf_op jit(solution)/shard_map/psum | solution.py:152
  93.2 1.3 fusion.46
  94.8 0.4 fusion.57
  95.1 6.3 %collective-permute-start.7 = (f32[8,128,128]{2,1,0:T(8,128)S(1)}, f32[8,128,128]{2,1,0:T(8,128)S(1)}, u32[]{:S(2)}, u32[]{:S(2)}) collective-permute-start(f32[8,128,128]{2,1,0:T(8,128)S(1)} %fusion.57), channel_id=1, source_target_pairs={{4,0},{8,4},{12,8},{16,12},{20,16},{24,20},{28,24},{32,28},{36,32}... | collective-permute-start | bytes 1572872 | tf_op jit(solution)/shard_map/ppermute | solution.py:17
  101.4 2.5 %collective-permute-start.8 = (f32[8,128,128]{2,1,0:T(8,128)S(1)}, f32[8,128,128]{2,1,0:T(8,128)S(1)}, u32[]{:S(2)}, u32[]{:S(2)}) collective-permute-start(f32[8,128,128]{2,1,0:T(8,128)S(1)} %fusion.57), channel_id=1, source_target_pairs={{8,0},{12,4},{16,8},{20,12},{24,16},{28,20},{32,24},{36,28},{40,32... | collective-permute-start | bytes 1572872 | tf_op jit(solution)/shard_map/ppermute | solution.py:17
  103.9 18.1 %collective-permute-start.9 = (f32[8,128,128]{2,1,0:T(8,128)S(1)}, f32[8,128,128]{2,1,0:T(8,128)S(1)}, u32[]{:S(2)}, u32[]{:S(2)}) collective-permute-start(f32[8,128,128]{2,1,0:T(8,128)S(1)} %fusion.57), channel_id=1, source_target_pairs={{12,0},{16,4},{20,8},{24,12},{28,16},{32,20},{36,24},{40,28},{44,3... | collective-permute-start | bytes 1572872 | tf_op jit(solution)/shard_map/ppermute | solution.py:17
  122.3 0.7 fusion.27
  123.0 0.4 copy-done.8
  123.9 0.7 copy-done.13
  124.7 2.1 collective-permute-start.15
  126.8 0.3 fusion.34
  127.3 0.7 copy-done.12
  128.1 2.3 collective-permute-start.14
  131.0 0.3 fusion.35
  131.6 8.1 %collective-permute-done.9 = f32[8,128,128]{2,1,0:T(8,128)S(1)} collective-permute-done((f32[8,128,128]{2,1,0:T(8,128)S(1)}, f32[8,128,128]{2,1,0:T(8,128)S(1)}, u32[]{:S(2)}, u32[]{:S(2)}) %collective-permute-start.9) | collective-permute-done | bytes 524320 | tf_op jit(solution)/shard_map/ppermute | solution.py:17
  139.9 8.1 %collective-permute-start.10 = (f32[8,128,128]{2,1,0:T(8,128)S(1)}, f32[8,128,128]{2,1,0:T(8,128)S(1)}, u32[]{:S(2)}, u32[]{:S(2)}) collective-permute-start(f32[8,128,128]{2,1,0:T(8,128)S(1)} %multiply_add_fusion.1), channel_id=1, source_target_pairs={{4,0},{8,4},{12,8},{16,12},{20,16},{24,20},{28,24},{32,28},{36,32}... | collective-permute-start | bytes 1572872 | tf_op jit(solution)/shard_map/ppermute | solution.py:17
  148.0 16.8 %collective-permute-start.11 = (f32[8,128,128]{2,1,0:T(8,128)S(1)}, f32[8,128,128]{2,1,0:T(8,128)S(1)}, u32[]{:S(2)}, u32[]{:S(2)}) collective-permute-start(f32[8,128,128]{2,1,0:T(8,128)S(1)} %multiply_add_fusion.1), channel_id=1, source_target_pairs={{20,0},{24,4},{28,8},{32,12},{36,16},{40,20},{44,24},{48,28},{52,3... | collective-permute-start | bytes 1572872 | tf_op jit(solution)/shard_map/ppermute | solution.py:17
  164.8 1.9 collective-permute-start.12
  166.7 2.1 collective-permute-start.13
  169.1 0.9 copy.213
  170.0 0.9 copy.214
  171.5 1.1 collective-permute-done.10
  172.6 28.9 %collective-permute-done.11 = f32[8,128,128]{2,1,0:T(8,128)S(1)} collective-permute-done((f32[8,128,128]{2,1,0:T(8,128)S(1)}, f32[8,128,128]{2,1,0:T(8,128)S(1)}, u32[]{:S(2)}, u32[]{:S(2)}) %collective-permute-start.11) | collective-permute-done | bytes 524320 | tf_op jit(solution)/shard_map/ppermute | solution.py:17
  201.5 29.7 %collective-permute-done.13 = f32[8,128,128]{2,1,0:T(8,128)S(1)} collective-permute-done((f32[8,128,128]{2,1,0:T(8,128)S(1)}, f32[8,128,128]{2,1,0:T(8,128)S(1)}, u32[]{:S(2)}, u32[]{:S(2)}) %collective-permute-start.13) | collective-permute-done | bytes 524320 | tf_op jit(solution)/shard_map/ppermute | solution.py:17
  231.3 0.7 fusion.31
  232.0 0.9 copy.215
  233.0 0.4 fusion.32
  233.5 0.9 copy.216
  (83 shorter events, 6.9 us)
Async XLA Ops:
  1.8 12.6 %copy-start.2 = (bf16[128,8,128]{2,1,0:T(8,128)(2,1)S(1)}, bf16[128,8,128]{2,1,0:T(8,128)(2,1)}, u32[]{:S(2)}) copy-start(bf16[128,8,128]{2,1,0:T(8,128)(2,1)} %param.8) | copy-start | bytes 786436
  1.8 12.6 %copy-start.3 = (bf16[128,8,128]{2,1,0:T(8,128)(2,1)S(1)}, bf16[128,8,128]{2,1,0:T(8,128)(2,1)}, u32[]{:S(2)}) copy-start(bf16[128,8,128]{2,1,0:T(8,128)(2,1)} %param.7) | copy-start | bytes 786436
  2.6 30.7 %collective-permute-start.1 = (bf16[2,128,8,128]{3,1,2,0:T(8,128)(2,1)}, bf16[2,128,8,128]{3,1,2,0:T(8,128)(2,1)S(1)}, u32[]{:S(2)}, u32[]{:S(2)}) collective-permute-start(bf16[2,128,8,128]{3,1,2,0:T(8,128)(2,1)} %pad_maximum_fusion), channel_id=1, source_target_pairs={{0,8},{4,12},{8,16},{12,20},{16,24},{20,28},{24,32},{28,36},{32,40... | collective-permute-start | bytes 1572872 | tf_op jit(solution)/shard_map/ppermute | solution.py:17
  5.7 29.2 %collective-permute-start = (bf16[2,128,8,128]{3,1,2,0:T(8,128)(2,1)}, bf16[2,128,8,128]{3,1,2,0:T(8,128)(2,1)S(1)}, u32[]{:S(2)}, u32[]{:S(2)}) collective-permute-start(bf16[2,128,8,128]{3,1,2,0:T(8,128)(2,1)} %pad_maximum_fusion), channel_id=1, source_target_pairs={{0,4},{4,8},{8,12},{12,16},{16,20},{20,24},{24,28},{28,32},{32,36}... | collective-permute-start | bytes 1572872 | tf_op jit(solution)/shard_map/ppermute | solution.py:17
  9.4 0.7 copy-start.15
  14.8 18.6 %collective-permute-start.2 = (f32[8,128,128]{2,1,0:T(8,128)S(1)}, f32[8,128,128]{2,1,0:T(8,128)}, u32[]{:S(2)}, u32[]{:S(2)}) collective-permute-start(f32[8,128,128]{2,1,0:T(8,128)S(1)} %fusion.61), channel_id=1, source_target_pairs={{0,12},{4,16},{8,20},{12,24},{16,28},{20,32},{24,36},{28,40},{32,4... | collective-permute-start | bytes 1572872 | tf_op jit(solution)/shard_map/ppermute | solution.py:17
  24.1 1.0 copy-start.1
  33.3 27.1 %copy-start.6 = (bf16[2,128,8,128]{3,1,2,0:T(8,128)(2,1)}, bf16[2,128,8,128]{3,1,2,0:T(8,128)(2,1)S(1)}, u32[]{:S(2)}) copy-start(bf16[2,128,8,128]{3,1,2,0:T(8,128)(2,1)S(1)} %collective-permute-done.1) | copy-start | bytes 1572868
  34.9 30.3 %copy-start.9 = (bf16[2,128,8,128]{3,1,2,0:T(8,128)(2,1)}, bf16[2,128,8,128]{3,1,2,0:T(8,128)(2,1)S(1)}, u32[]{:S(2)}) copy-start(bf16[2,128,8,128]{3,1,2,0:T(8,128)(2,1)S(1)} %collective-permute-done) | copy-start | bytes 1572868
  35.3 31.3 %collective-permute-start.3 = (f32[8,128,128]{2,1,0:T(8,128)S(1)}, f32[8,128,128]{2,1,0:T(8,128)S(1)}, u32[]{:S(2)}, u32[]{:S(2)}) collective-permute-start(f32[8,128,128]{2,1,0:T(8,128)S(1)} %fusion.19), channel_id=1, source_target_pairs={{0,4},{4,8},{8,12},{12,16},{16,20},{20,24},{24,28},{28,32},{32,36}... | collective-permute-start | bytes 1572872 | tf_op jit(solution)/shard_map/ppermute | solution.py:17
  40.8 25.8 %collective-permute-start.4 = (f32[8,128,128]{2,1,0:T(8,128)S(1)}, f32[8,128,128]{2,1,0:T(8,128)S(1)}, u32[]{:S(2)}, u32[]{:S(2)}) collective-permute-start(f32[8,128,128]{2,1,0:T(8,128)S(1)} %fusion.19), channel_id=1, source_target_pairs={{0,20},{4,24},{8,28},{12,32},{16,36},{20,40},{24,44},{28,48},{32,5... | collective-permute-start | bytes 1572872 | tf_op jit(solution)/shard_map/ppermute | solution.py:17
  46.4 24.5 %collective-permute-start.5 = (f32[8,128,128]{2,1,0:T(8,128)S(1)}, f32[8,128,128]{2,1,0:T(8,128)S(1)}, u32[]{:S(2)}, u32[]{:S(2)}) collective-permute-start(f32[8,128,128]{2,1,0:T(8,128)S(1)} %fusion.19), channel_id=1, source_target_pairs={{0,36},{4,40},{8,44},{12,48},{16,52},{20,56},{24,60},{28,64},{32,6... | collective-permute-start | bytes 1572872 | tf_op jit(solution)/shard_map/ppermute | solution.py:17
  58.5 23.9 %collective-permute-start.6 = (f32[8,128,128]{2,1,0:T(8,128)S(1)}, f32[8,128,128]{2,1,0:T(8,128)S(1)}, u32[]{:S(2)}, u32[]{:S(2)}) collective-permute-start(f32[8,128,128]{2,1,0:T(8,128)S(1)} %fusion.19), channel_id=1, source_target_pairs={{0,52},{4,56},{8,60},{12,64},{16,68},{20,72},{24,76},{28,80},{32,8... | collective-permute-start | bytes 1572872 | tf_op jit(solution)/shard_map/ppermute | solution.py:17
  61.4 1.0 copy-start
  65.3 1.0 copy-start.7
  82.4 0.7 copy-start.14
  82.5 1.9 copy-start.4
  95.1 27.2 %copy-start.5 = (f32[8,128,128]{2,1,0:T(8,128)S(1)}, f32[8,128,128]{2,1,0:T(8,128)}, u32[]{:S(2)}) copy-start(f32[8,128,128]{2,1,0:T(8,128)} %copy-done.4) | copy-start | bytes 1572868
  95.1 36.4 %collective-permute-start.7 = (f32[8,128,128]{2,1,0:T(8,128)S(1)}, f32[8,128,128]{2,1,0:T(8,128)S(1)}, u32[]{:S(2)}, u32[]{:S(2)}) collective-permute-start(f32[8,128,128]{2,1,0:T(8,128)S(1)} %fusion.57), channel_id=1, source_target_pairs={{4,0},{8,4},{12,8},{16,12},{20,16},{24,20},{28,24},{32,28},{36,32}... | collective-permute-start | bytes 1572872 | tf_op jit(solution)/shard_map/ppermute | solution.py:17
  101.4 30.2 %collective-permute-start.8 = (f32[8,128,128]{2,1,0:T(8,128)S(1)}, f32[8,128,128]{2,1,0:T(8,128)S(1)}, u32[]{:S(2)}, u32[]{:S(2)}) collective-permute-start(f32[8,128,128]{2,1,0:T(8,128)S(1)} %fusion.57), channel_id=1, source_target_pairs={{8,0},{12,4},{16,8},{20,12},{24,16},{28,20},{32,24},{36,28},{40,32... | collective-permute-start | bytes 1572872 | tf_op jit(solution)/shard_map/ppermute | solution.py:17
  103.9 35.8 %collective-permute-start.9 = (f32[8,128,128]{2,1,0:T(8,128)S(1)}, f32[8,128,128]{2,1,0:T(8,128)S(1)}, u32[]{:S(2)}, u32[]{:S(2)}) collective-permute-start(f32[8,128,128]{2,1,0:T(8,128)S(1)} %fusion.57), channel_id=1, source_target_pairs={{12,0},{16,4},{20,8},{24,12},{28,16},{32,20},{36,24},{40,28},{44,3... | collective-permute-start | bytes 1572872 | tf_op jit(solution)/shard_map/ppermute | solution.py:17
  122.3 1.0 copy-start.8
  123.7 1.0 copy-start.13
  124.6 2.1 copy-start.10
  124.7 42.1 %collective-permute-start.15 = (bf16[2,128,8,128]{3,1,2,0:T(8,128)(2,1)S(1)}, bf16[2,128,8,128]{3,1,2,0:T(8,128)(2,1)S(1)}, u32[]{:S(2)}, u32[]{:S(2)}) collective-permute-start(bf16[2,128,8,128]{3,1,2,0:T(8,128)(2,1)S(1)} %pad_maximum_fusion.2), channel_id=1, source_target_pairs={{8,0},{12,4},{16,8},{20,12},{24,16},{28,20},{32,24},{36,28},{40,32... | collective-permute-start | bytes 1572872 | tf_op jit(solution)/shard_map/ppermute | solution.py:17
  127.1 1.0 copy-start.12
  128.1 43.3 %collective-permute-start.14 = (bf16[2,128,8,128]{3,1,2,0:T(8,128)(2,1)S(1)}, bf16[2,128,8,128]{3,1,2,0:T(8,128)(2,1)S(1)}, u32[]{:S(2)}, u32[]{:S(2)}) collective-permute-start(bf16[2,128,8,128]{3,1,2,0:T(8,128)(2,1)S(1)} %pad_maximum_fusion.1), channel_id=1, source_target_pairs={{4,0},{8,4},{12,8},{16,12},{20,16},{24,20},{28,24},{32,28},{36,32}... | collective-permute-start | bytes 1572872 | tf_op jit(solution)/shard_map/ppermute | solution.py:17
  139.9 32.7 %collective-permute-start.10 = (f32[8,128,128]{2,1,0:T(8,128)S(1)}, f32[8,128,128]{2,1,0:T(8,128)S(1)}, u32[]{:S(2)}, u32[]{:S(2)}) collective-permute-start(f32[8,128,128]{2,1,0:T(8,128)S(1)} %multiply_add_fusion.1), channel_id=1, source_target_pairs={{4,0},{8,4},{12,8},{16,12},{20,16},{24,20},{28,24},{32,28},{36,32}... | collective-permute-start | bytes 1572872 | tf_op jit(solution)/shard_map/ppermute | solution.py:17
  148.0 53.5 %collective-permute-start.11 = (f32[8,128,128]{2,1,0:T(8,128)S(1)}, f32[8,128,128]{2,1,0:T(8,128)S(1)}, u32[]{:S(2)}, u32[]{:S(2)}) collective-permute-start(f32[8,128,128]{2,1,0:T(8,128)S(1)} %multiply_add_fusion.1), channel_id=1, source_target_pairs={{20,0},{24,4},{28,8},{32,12},{36,16},{40,20},{44,24},{48,28},{52,3... | collective-permute-start | bytes 1572872 | tf_op jit(solution)/shard_map/ppermute | solution.py:17
  164.8 36.7 %collective-permute-start.12 = (f32[8,128,128]{2,1,0:T(8,128)S(1)}, f32[8,128,128]{2,1,0:T(8,128)S(1)}, u32[]{:S(2)}, u32[]{:S(2)}) collective-permute-start(f32[8,128,128]{2,1,0:T(8,128)S(1)} %multiply_add_fusion.1), channel_id=1, source_target_pairs={{36,0},{40,4},{44,8},{48,12},{52,16},{56,20},{60,24},{64,28},{68,3... | collective-permute-start | bytes 1572872 | tf_op jit(solution)/shard_map/ppermute | solution.py:17
  166.7 64.4 %collective-permute-start.13 = (f32[8,128,128]{2,1,0:T(8,128)S(1)}, f32[8,128,128]{2,1,0:T(8,128)S(1)}, u32[]{:S(2)}, u32[]{:S(2)}) collective-permute-start(f32[8,128,128]{2,1,0:T(8,128)S(1)} %multiply_add_fusion.1), channel_id=1, source_target_pairs={{52,0},{56,4},{60,8},{64,12},{68,16},{72,20},{76,24},{80,28},{84,3... | collective-permute-start | bytes 1572872 | tf_op jit(solution)/shard_map/ppermute | solution.py:17
  232.0 1.0 copy-start.11

commit v3 on v2

--- a/solution.py
+++ b/solution.py
@@ -124,27 +124,18 @@
     attend = (narrow("thd,uhd->htu", queries, keys) * same_tile).astype(jnp.bfloat16)
     place = lax.axis_index("ctx")
     need = min(-(-MAXDOC // tile), lax.axis_size("ctx"))
-    group = SPAN + 2
-    rounds = -(-need // group)
-    own_state = tile_state(keys, values, doc_lengths, base)
-    far_states = [
-        from_behind(own_state, "ctx", shift) for shift in range(group - 1, SPAN, -1)
-    ]
     near_states = [
         tile_state(key_tiles[position], value_tiles[position], doc_lengths,
                    base - (SPAN - position) * tile)
         for position in range(SPAN)
     ]
-    group_spans = [(place - shift, place - shift) for shift in range(group - 1, -1, -1)]
-    group_state = fold_states(
-        far_states + near_states + [own_state], front_flags(doc_lengths, group_spans, tile)
-    )
-    shifts = [1 + group * k for k in range(rounds - 1, -1, -1)]
-    window_spans = [(place - shift - group + 1, place - shift) for shift in shifts]
-    incoming = fold_states(
-        [from_behind(group_state, "ctx", shift) for shift in shifts],
-        front_flags(doc_lengths, window_spans, tile),
-    )
+    near_spans = [(place - SPAN + position, place - SPAN + position) for position in range(SPAN)]
+    incoming = fold_states(near_states, front_flags(doc_lengths, near_spans, tile))
+    covered = SPAN
+    while covered < need:
+        (flag,) = front_flags(doc_lengths, [(place - covered, place - 1)], tile)
+        incoming = incoming + (1.0 - flag) * from_behind(incoming, "ctx", covered)
+        covered *= 2
     linear_out = (
         narrow("htu,uhd->thd", attend, values)
         + wide("thd,hde->the", query_wide, incoming) * carried_prev[:, None, None]
@@ -176,16 +167,16 @@
     tile_sum = narrow(
         "thd,the->hde", jnp.where(keep_first, queries, jnp.zeros_like(queries)), inner
     )
-    back_states = [
-        from_behind(tile_sum, "ctx", -shift) for shift in range(group - 1, 0, -1)
-    ] + [tile_sum]
-    back_spans = [(place + shift, place + shift) for shift in range(group - 1, -1, -1)]
-    back_group = fold_states(back_states, back_flags(doc_lengths, back_spans, tile))
-    back_window = [(place + shift, place + shift + group - 1) for shift in shifts]
-    later = fold_states(
-        [from_behind(back_group, "ctx", -shift) for shift in shifts],
-        back_flags(doc_lengths, back_window, tile),
-    )
+    part = tile_sum
+    covered = 1
+    while 2 * covered < need:
+        (flag,) = back_flags(doc_lengths, [(place, place + covered - 1)], tile)
+        part = part + (1.0 - flag) * from_behind(part, "ctx", -covered)
+        covered *= 2
+    later = from_behind(part, "ctx", -1)
+    if covered < need:
+        (flag,) = back_flags(doc_lengths, [(place + 1, place + covered)], tile)
+        later = later + (1.0 - flag) * from_behind(part, "ctx", -1 - covered)
     key_linear = (
         narrow("htu,thd->uhd", back, queries)
         + wide("uhe,hde->uhd", values.astype(jnp.float32), later) * carried_next[:, None, None]

time: 235 us -> 191 us (0.81)
  the two profiles are of different devices: /device:TPU:67 before, /device:TPU:71 now
where the time goes in v3:
time: 191 us
  waiting for transfers between devices  98.5 us (52%)
  starting transfers between devices  39.5 us (21%)
  local copies, waits for them, and re-layouts  13.3 us (7%)
  matrix products  12.8 us (7%)
  between operations  12.1 us (6%)
  blocking collectives  8.7 us (5%)
  other arithmetic  5.63 us (3%)
    ppermute x12, waiting for transfers between devices, from_behind(): return lax.ppermute(x, axis, pairs)  98.5 us
    ppermute x12, starting transfers between devices, from_behind(): return lax.ppermute(x, axis, pairs)  39.5 us
    dot_general x26, matrix products, narrow(): return jnp.einsum(form, left, right, preferred_element_type=jnp.float32)  9.52 us
    psum x1, blocking collectives, per_device(): squares = lax.psum(jnp.sum(linear_out * linear_out, axis=(1, 2)), 'head')  8.7 us
    unnamed x38, local copies, waits for them, and re-layouts  5.83 us
  transfers between devices with their start and end apart: 12, of which 8 were waited for; matrix products, arithmetic and copies ran while one was open for 11% of the time, Pallas kernels for 0%

profile of v3, /device:TPU:71, one launch (start us, length us, event | category | flops | bytes accessed | tf_op | source)
XLA Modules:
  0.0 190.5 jit_solution(2380406194241300697)
XLA Ops:
  0.6 1.1 copy_bitcast_fusion
  1.9 3.6 %collective-permute-start.1 = (bf16[2,128,8,128]{3,1,2,0:T(8,128)(2,1)S(1)}, bf16[2,128,8,128]{3,1,2,0:T(8,128)(2,1)S(1)}, u32[]{:S(2)}, u32[]{:S(2)}) collective-permute-start(bf16[2,128,8,128]{3,1,2,0:T(8,128)(2,1)S(1)} %pad_maximum_fusion), channel_id=1, source_target_pairs={{0,8},{4,12},{8,16},{12,20},{16,24},{20,28},{24,32},{28,36},{32,40... | collective-permute-start | bytes 1572872 | tf_op jit(solution)/shard_map/ppermute | solution.py:17
  5.5 4.0 %collective-permute-start = (bf16[2,128,8,128]{3,1,2,0:T(8,128)(2,1)S(1)}, bf16[2,128,8,128]{3,1,2,0:T(8,128)(2,1)S(1)}, u32[]{:S(2)}, u32[]{:S(2)}) collective-permute-start(bf16[2,128,8,128]{3,1,2,0:T(8,128)(2,1)S(1)} %pad_maximum_fusion), channel_id=1, source_target_pairs={{0,4},{4,8},{8,12},{12,16},{16,20},{20,24},{24,28},{28,32},{32,36}... | collective-permute-start | bytes 1572872 | tf_op jit(solution)/shard_map/ppermute | solution.py:17
  9.8 0.6 fusion.105
  10.6 0.7 slice.94
  11.2 0.6 slice.87
  13.9 0.3 fusion.102
  14.2 0.6 fusion.119
  14.8 0.6 fusion.118
  15.4 0.6 fusion.117
  16.1 0.6 fusion.116
  16.7 0.3 fusion.53
  17.0 1.3 broadcast_compare_fusion.1
  18.3 0.7 fusion.115
  19.0 0.7 fusion.114
  19.6 0.7 fusion.113
  20.3 0.6 slice.92
  30.7 0.4 convolution_multiply_fusion.7
  31.1 0.4 convolution_add_fusion.2
  31.4 3.1 %collective-permute-start.2 = (f32[8,128,128]{2,1,0:T(8,128)S(1)}, f32[8,128,128]{2,1,0:T(8,128)S(1)}, u32[]{:S(2)}, u32[]{:S(2)}) collective-permute-start(f32[8,128,128]{2,1,0:T(8,128)S(1)} %convolution_add_fusion.2), channel_id=1, source_target_pairs={{0,8},{4,12},{8,16},{12,20},{16,24},{20,28},{24,32},{28,36},{32,40... | collective-permute-start | bytes 1572872 | tf_op jit(solution)/shard_map/ppermute | solution.py:17
  34.5 0.3 fusion.120
  34.9 0.3 fusion.121
  35.5 0.6 copy-done
  36.1 0.9 fusion.39
  37.1 9.3 %collective-permute-done.2 = f32[8,128,128]{2,1,0:T(8,128)S(1)} collective-permute-done((f32[8,128,128]{2,1,0:T(8,128)S(1)}, f32[8,128,128]{2,1,0:T(8,128)S(1)}, u32[]{:S(2)}, u32[]{:S(2)}) %collective-permute-start.2) | collective-permute-done | bytes 524320 | tf_op jit(solution)/shard_map/ppermute | solution.py:17
  46.4 4.0 %collective-permute-start.3 = (f32[8,128,128]{2,1,0:T(8,128)S(1)}, f32[8,128,128]{2,1,0:T(8,128)S(1)}, u32[]{:S(2)}, u32[]{:S(2)}) collective-permute-start(f32[8,128,128]{2,1,0:T(8,128)S(1)} %multiply_add_fusion.6), channel_id=1, source_target_pairs={{0,16},{4,20},{8,24},{12,28},{16,32},{20,36},{24,40},{28,44},{32,4... | collective-permute-start | bytes 1572872 | tf_op jit(solution)/shard_map/ppermute | solution.py:17
  50.4 0.9 fusion.38
  51.4 0.3 convolution_bitcast_fusion.3
  51.7 1.0 convolution_bitcast_fusion
  52.7 10.5 %collective-permute-done.3 = f32[8,128,128]{2,1,0:T(8,128)S(1)} collective-permute-done((f32[8,128,128]{2,1,0:T(8,128)S(1)}, f32[8,128,128]{2,1,0:T(8,128)S(1)}, u32[]{:S(2)}, u32[]{:S(2)}) %collective-permute-start.3) | collective-permute-done | bytes 524320 | tf_op jit(solution)/shard_map/ppermute | solution.py:17
  63.3 4.9 %collective-permute-start.4 = (f32[8,128,128]{2,1,0:T(8,128)S(1)}, f32[8,128,128]{2,1,0:T(8,128)S(1)}, u32[]{:S(2)}, u32[]{:S(2)}) collective-permute-start(f32[8,128,128]{2,1,0:T(8,128)S(1)} %multiply_add_fusion.5), channel_id=1, source_target_pairs={{0,32},{4,36},{8,40},{12,44},{16,48},{20,52},{24,56},{28,60},{32,6... | collective-permute-start | bytes 1572872 | tf_op jit(solution)/shard_map/ppermute | solution.py:17
  68.5 0.3 fusion.12
  68.8 9.7 %collective-permute-done.4 = f32[8,128,128]{2,1,0:T(8,128)S(1)} collective-permute-done((f32[8,128,128]{2,1,0:T(8,128)S(1)}, f32[8,128,128]{2,1,0:T(8,128)S(1)}, u32[]{:S(2)}, u32[]{:S(2)}) %collective-permute-start.4) | collective-permute-done | bytes 524320 | tf_op jit(solution)/shard_map/ppermute | solution.py:17
  78.5 1.4 fusion.44
  79.9 8.7 %all-reduce = (f32[128]{0:T(128)S(1)}, f32[128]{0:T(128)S(1)}) all-reduce(f32[128]{0:T(128)S(1)} %get-tuple-element.17, f32[128]{0:T(128)S(1)} %get-tuple-element.16), channel_id=1, replica_groups=mesh['ctx'=64,'head'=4] {'head'}, use_global_device_ids=true, to_apply=%region_10.11 | all-reduce | flops 256 | bytes 2048 | tf_op jit(solution)/shard_map/psum | solution.py:143
  88.6 1.3 fusion.43
  89.9 0.3 fusion.33
  90.2 0.7 copy-done.7
  91.0 0.3 fusion.30
  91.5 0.7 copy-done.14
  92.3 3.4 %collective-permute-start.11 = (bf16[2,128,8,128]{3,1,2,0:T(8,128)(2,1)S(1)}, bf16[2,128,8,128]{3,1,2,0:T(8,128)(2,1)S(1)}, u32[]{:S(2)}, u32[]{:S(2)}) collective-permute-start(bf16[2,128,8,128]{3,1,2,0:T(8,128)(2,1)S(1)} %pad_maximum_fusion.2), channel_id=1, source_target_pairs={{8,0},{12,4},{16,8},{20,12},{24,16},{28,20},{32,24},{36,28},{40,32... | collective-permute-start | bytes 1572872 | tf_op jit(solution)/shard_map/ppermute | solution.py:17
  95.7 0.3 fusion.31
  96.3 0.3 fusion.54
  96.7 6.0 %collective-permute-start.5 = (f32[8,128,128]{2,1,0:T(8,128)S(1)}, f32[8,128,128]{2,1,0:T(8,128)S(1)}, u32[]{:S(2)}, u32[]{:S(2)}) collective-permute-start(f32[8,128,128]{2,1,0:T(8,128)S(1)} %fusion.54), channel_id=1, source_target_pairs={{4,0},{8,4},{12,8},{16,12},{20,16},{24,20},{28,24},{32,28},{36,32}... | collective-permute-start | bytes 1572872 | tf_op jit(solution)/shard_map/ppermute | solution.py:17
  102.7 1.9 %collective-permute-start.10 = (bf16[2,128,8,128]{3,1,2,0:T(8,128)(2,1)S(1)}, bf16[2,128,8,128]{3,1,2,0:T(8,128)(2,1)S(1)}, u32[]{:S(2)}, u32[]{:S(2)}) collective-permute-start(bf16[2,128,8,128]{3,1,2,0:T(8,128)(2,1)S(1)} %pad_maximum_fusion.1), channel_id=1, source_target_pairs={{4,0},{8,4},{12,8},{16,12},{20,16},{24,20},{28,24},{32,28},{36,32}... | collective-permute-start | bytes 1572872 | tf_op jit(solution)/shard_map/ppermute | solution.py:17
  104.9 0.3 fusion.8
  105.2 13.5 %collective-permute-done.5 = f32[8,128,128]{2,1,0:T(8,128)S(1)} collective-permute-done((f32[8,128,128]{2,1,0:T(8,128)S(1)}, f32[8,128,128]{2,1,0:T(8,128)S(1)}, u32[]{:S(2)}, u32[]{:S(2)}) %collective-permute-start.5) | collective-permute-done | bytes 524320 | tf_op jit(solution)/shard_map/ppermute | solution.py:17
  118.9 2.1 %collective-permute-start.6 = (f32[8,128,128]{2,1,0:T(8,128)S(1)}, f32[8,128,128]{2,1,0:T(8,128)S(1)}, u32[]{:S(2)}, u32[]{:S(2)}) collective-permute-start(f32[8,128,128]{2,1,0:T(8,128)S(1)} %multiply_add_fusion.3), channel_id=1, source_target_pairs={{8,0},{12,4},{16,8},{20,12},{24,16},{28,20},{32,24},{36,28},{40,32... | collective-permute-start | bytes 1572872 | tf_op jit(solution)/shard_map/ppermute | solution.py:17
  121.2 0.7 fusion.24
  121.9 13.7 %collective-permute-done.6 = f32[8,128,128]{2,1,0:T(8,128)S(1)} collective-permute-done((f32[8,128,128]{2,1,0:T(8,128)S(1)}, f32[8,128,128]{2,1,0:T(8,128)S(1)}, u32[]{:S(2)}, u32[]{:S(2)}) %collective-permute-start.6) | collective-permute-done | bytes 524320 | tf_op jit(solution)/shard_map/ppermute | solution.py:17
  135.7 1.9 %collective-permute-start.7 = (f32[8,128,128]{2,1,0:T(8,128)S(1)}, f32[8,128,128]{2,1,0:T(8,128)S(1)}, u32[]{:S(2)}, u32[]{:S(2)}) collective-permute-start(f32[8,128,128]{2,1,0:T(8,128)S(1)} %multiply_add_fusion.2), channel_id=1, source_target_pairs={{16,0},{20,4},{24,8},{28,12},{32,16},{36,20},{40,24},{44,28},{48,3... | collective-permute-start | bytes 1572872 | tf_op jit(solution)/shard_map/ppermute | solution.py:17
  137.6 0.3 fusion.32
  137.9 0.3 fusion.27
  138.2 15.6 %collective-permute-done.7 = f32[8,128,128]{2,1,0:T(8,128)S(1)} collective-permute-done((f32[8,128,128]{2,1,0:T(8,128)S(1)}, f32[8,128,128]{2,1,0:T(8,128)S(1)}, u32[]{:S(2)}, u32[]{:S(2)}) %collective-permute-start.7) | collective-permute-done | bytes 524320 | tf_op jit(solution)/shard_map/ppermute | solution.py:17
  153.9 2.4 %collective-permute-start.8 = (f32[8,128,128]{2,1,0:T(8,128)S(1)}, f32[8,128,128]{2,1,0:T(8,128)S(1)}, u32[]{:S(2)}, u32[]{:S(2)}) collective-permute-start(f32[8,128,128]{2,1,0:T(8,128)S(1)} %multiply_add_fusion.1), channel_id=1, source_target_pairs={{4,0},{8,4},{12,8},{16,12},{20,16},{24,20},{28,24},{32,28},{36,32}... | collective-permute-start | bytes 1572872 | tf_op jit(solution)/shard_map/ppermute | solution.py:17
  156.3 2.1 %collective-permute-start.9 = (f32[8,128,128]{2,1,0:T(8,128)S(1)}, f32[8,128,128]{2,1,0:T(8,128)S(1)}, u32[]{:S(2)}, u32[]{:S(2)}) collective-permute-start(f32[8,128,128]{2,1,0:T(8,128)S(1)} %multiply_add_fusion.1), channel_id=1, source_target_pairs={{36,0},{40,4},{44,8},{48,12},{52,16},{56,20},{60,24},{64,28},{68,3... | collective-permute-start | bytes 1572872 | tf_op jit(solution)/shard_map/ppermute | solution.py:17
  158.6 0.9 copy.204
  159.5 0.9 copy.205
  161.1 9.4 %collective-permute-done.8 = f32[8,128,128]{2,1,0:T(8,128)S(1)} collective-permute-done((f32[8,128,128]{2,1,0:T(8,128)S(1)}, f32[8,128,128]{2,1,0:T(8,128)S(1)}, u32[]{:S(2)}, u32[]{:S(2)}) %collective-permute-start.8) | collective-permute-done | bytes 524320 | tf_op jit(solution)/shard_map/ppermute | solution.py:17
  170.5 16.9 %collective-permute-done.9 = f32[8,128,128]{2,1,0:T(8,128)S(1)} collective-permute-done((f32[8,128,128]{2,1,0:T(8,128)S(1)}, f32[8,128,128]{2,1,0:T(8,128)S(1)}, u32[]{:S(2)}, u32[]{:S(2)}) %collective-permute-start.9) | collective-permute-done | bytes 524320 | tf_op jit(solution)/shard_map/ppermute | solution.py:17
  187.3 0.7 fusion.28
  188.1 0.9 copy.206
  189.1 0.5 fusion.29
  189.6 0.9 copy.207
  (85 shorter events, 4.7 us)
Async XLA Ops:
  1.8 7.7 %copy-start.16 = (s32[64]{0:T(128)S(1)}, s32[64]{0:T(128)}, u32[]{:S(2)}) copy-start(s32[64]{0:T(128)} %param.10) | copy-start | bytes 772
  1.8 14.9 %copy-start.3 = (bf16[128,8,128]{2,1,0:T(8,128)(2,1)S(1)}, bf16[128,8,128]{2,1,0:T(8,128)(2,1)}, u32[]{:S(2)}) copy-start(bf16[128,8,128]{2,1,0:T(8,128)(2,1)} %param.7) | copy-start | bytes 786436
  1.8 14.8 %copy-start.1 = (bf16[128,8,128]{2,1,0:T(8,128)(2,1)S(1)}, bf16[128,8,128]{2,1,0:T(8,128)(2,1)}, u32[]{:S(2)}) copy-start(bf16[128,8,128]{2,1,0:T(8,128)(2,1)} %param.6) | copy-start | bytes 786436
  1.9 28.8 %collective-permute-start.1 = (bf16[2,128,8,128]{3,1,2,0:T(8,128)(2,1)S(1)}, bf16[2,128,8,128]{3,1,2,0:T(8,128)(2,1)S(1)}, u32[]{:S(2)}, u32[]{:S(2)}) collective-permute-start(bf16[2,128,8,128]{3,1,2,0:T(8,128)(2,1)S(1)} %pad_maximum_fusion), channel_id=1, source_target_pairs={{0,8},{4,12},{8,16},{12,20},{16,24},{20,28},{24,32},{28,36},{32,40... | collective-permute-start | bytes 1572872 | tf_op jit(solution)/shard_map/ppermute | solution.py:17
  5.5 25.6 %collective-permute-start = (bf16[2,128,8,128]{3,1,2,0:T(8,128)(2,1)S(1)}, bf16[2,128,8,128]{3,1,2,0:T(8,128)(2,1)S(1)}, u32[]{:S(2)}, u32[]{:S(2)}) collective-permute-start(bf16[2,128,8,128]{3,1,2,0:T(8,128)(2,1)S(1)} %pad_maximum_fusion), channel_id=1, source_target_pairs={{0,4},{4,8},{8,12},{12,16},{16,20},{20,24},{24,28},{28,32},{32,36}... | collective-permute-start | bytes 1572872 | tf_op jit(solution)/shard_map/ppermute | solution.py:17
  16.7 13.7 %copy-start.2 = (bf16[128,8,128]{2,1,0:T(8,128)(2,1)S(1)}, bf16[128,8,128]{2,1,0:T(8,128)(2,1)}, u32[]{:S(2)}) copy-start(bf16[128,8,128]{2,1,0:T(8,128)(2,1)} %param.8) | copy-start | bytes 786436
  30.7 3.9 %copy-start.5 = (bf16[2,128,8,128]{3,1,2,0:T(8,128)(2,1)}, bf16[2,128,8,128]{3,1,2,0:T(8,128)(2,1)S(1)}, u32[]{:S(2)}) copy-start(bf16[2,128,8,128]{3,1,2,0:T(8,128)(2,1)S(1)} %collective-permute-done.1) | copy-start | bytes 1572868
  31.0 37.1 %copy-start.8 = (bf16[2,128,8,128]{3,1,2,0:T(8,128)(2,1)}, bf16[2,128,8,128]{3,1,2,0:T(8,128)(2,1)S(1)}, u32[]{:S(2)}) copy-start(bf16[2,128,8,128]{3,1,2,0:T(8,128)(2,1)S(1)} %collective-permute-done) | copy-start | bytes 1572868
  31.4 14.9 %collective-permute-start.2 = (f32[8,128,128]{2,1,0:T(8,128)S(1)}, f32[8,128,128]{2,1,0:T(8,128)S(1)}, u32[]{:S(2)}, u32[]{:S(2)}) collective-permute-start(f32[8,128,128]{2,1,0:T(8,128)S(1)} %convolution_add_fusion.2), channel_id=1, source_target_pairs={{0,8},{4,12},{8,16},{12,20},{16,24},{20,28},{24,32},{28,36},{32,40... | collective-permute-start | bytes 1572872 | tf_op jit(solution)/shard_map/ppermute | solution.py:17
  35.2 1.0 copy-start
  46.4 16.8 %collective-permute-start.3 = (f32[8,128,128]{2,1,0:T(8,128)S(1)}, f32[8,128,128]{2,1,0:T(8,128)S(1)}, u32[]{:S(2)}, u32[]{:S(2)}) collective-permute-start(f32[8,128,128]{2,1,0:T(8,128)S(1)} %multiply_add_fusion.6), channel_id=1, source_target_pairs={{0,16},{4,20},{8,24},{12,28},{16,32},{20,36},{24,40},{28,44},{32,4... | collective-permute-start | bytes 1572872 | tf_op jit(solution)/shard_map/ppermute | solution.py:17
  63.3 5.2 %copy-start.6 = (bf16[2,128,8,128]{3,1,2,0:T(8,128)(2,1)S(1)}, bf16[2,128,8,128]{3,1,2,0:T(8,128)(2,1)}, u32[]{:S(2)}) copy-start(bf16[2,128,8,128]{3,1,2,0:T(8,128)(2,1)} %copy-done.5) | copy-start | bytes 1572868
  63.3 15.2 %collective-permute-start.4 = (f32[8,128,128]{2,1,0:T(8,128)S(1)}, f32[8,128,128]{2,1,0:T(8,128)S(1)}, u32[]{:S(2)}, u32[]{:S(2)}) collective-permute-start(f32[8,128,128]{2,1,0:T(8,128)S(1)} %multiply_add_fusion.5), channel_id=1, source_target_pairs={{0,32},{4,36},{8,40},{12,44},{16,48},{20,52},{24,56},{28,60},{32,6... | collective-permute-start | bytes 1572872 | tf_op jit(solution)/shard_map/ppermute | solution.py:17
  68.5 10.0 %copy-start.15 = (f32[8,128]{1,0:T(8,128)S(1)}, f32[8,128]{1,0:T(8,128)}, u32[]{:S(2)}) copy-start(f32[8,128]{1,0:T(8,128)} %param.9) | copy-start | bytes 12292
  78.5 1.4 copy-start.11
  89.9 1.0 copy-start.7
  91.3 1.0 copy-start.14
  92.2 3.5 %copy-start.9 = (bf16[2,128,8,128]{3,1,2,0:T(8,128)(2,1)S(1)}, bf16[2,128,8,128]{3,1,2,0:T(8,128)(2,1)}, u32[]{:S(2)}) copy-start(bf16[2,128,8,128]{3,1,2,0:T(8,128)(2,1)} %copy-done.8) | copy-start | bytes 1572868
  92.3 68.5 %collective-permute-start.11 = (bf16[2,128,8,128]{3,1,2,0:T(8,128)(2,1)S(1)}, bf16[2,128,8,128]{3,1,2,0:T(8,128)(2,1)S(1)}, u32[]{:S(2)}, u32[]{:S(2)}) collective-permute-start(bf16[2,128,8,128]{3,1,2,0:T(8,128)(2,1)S(1)} %pad_maximum_fusion.2), channel_id=1, source_target_pairs={{8,0},{12,4},{16,8},{20,12},{24,16},{28,20},{32,24},{36,28},{40,32... | collective-permute-start | bytes 1572872 | tf_op jit(solution)/shard_map/ppermute | solution.py:17
  96.3 6.4 %copy-start.13 = (bf16[1,128,8,128]{3,1,2,0:T(8,128)(2,1)S(1)}, bf16[1,128,8,128]{3,1,2,0:T(8,128)(2,1)}, u32[]{:S(2)}) copy-start(bf16[1,128,8,128]{3,1,2,0:T(8,128)(2,1)} %fusion.38) | copy-start | bytes 786436
  96.7 22.1 %collective-permute-start.5 = (f32[8,128,128]{2,1,0:T(8,128)S(1)}, f32[8,128,128]{2,1,0:T(8,128)S(1)}, u32[]{:S(2)}, u32[]{:S(2)}) collective-permute-start(f32[8,128,128]{2,1,0:T(8,128)S(1)} %fusion.54), channel_id=1, source_target_pairs={{4,0},{8,4},{12,8},{16,12},{20,16},{24,20},{28,24},{32,28},{36,32}... | collective-permute-start | bytes 1572872 | tf_op jit(solution)/shard_map/ppermute | solution.py:17
  102.7 58.2 %collective-permute-start.10 = (bf16[2,128,8,128]{3,1,2,0:T(8,128)(2,1)S(1)}, bf16[2,128,8,128]{3,1,2,0:T(8,128)(2,1)S(1)}, u32[]{:S(2)}, u32[]{:S(2)}) collective-permute-start(bf16[2,128,8,128]{3,1,2,0:T(8,128)(2,1)S(1)} %pad_maximum_fusion.1), channel_id=1, source_target_pairs={{4,0},{8,4},{12,8},{16,12},{20,16},{24,20},{28,24},{32,28},{36,32}... | collective-permute-start | bytes 1572872 | tf_op jit(solution)/shard_map/ppermute | solution.py:17
  118.8 2.2 %copy-start.4 = (bf16[128,8,128]{2,1,0:T(8,128)(2,1)S(1)}, bf16[128,8,128]{2,1,0:T(8,128)(2,1)}, u32[]{:S(2)}) copy-start(bf16[128,8,128]{2,1,0:T(8,128)(2,1)} %param.7) | copy-start | bytes 786436
  118.8 2.4 %copy-start.12 = (f32[8,128,128]{2,1,0:T(8,128)S(1)}, f32[8,128,128]{2,1,0:T(8,128)}, u32[]{:S(2)}) copy-start(f32[8,128,128]{2,1,0:T(8,128)} %copy-done.11) | copy-start | bytes 1572868
  118.9 16.8 %collective-permute-start.6 = (f32[8,128,128]{2,1,0:T(8,128)S(1)}, f32[8,128,128]{2,1,0:T(8,128)S(1)}, u32[]{:S(2)}, u32[]{:S(2)}) collective-permute-start(f32[8,128,128]{2,1,0:T(8,128)S(1)} %multiply_add_fusion.3), channel_id=1, source_target_pairs={{8,0},{12,4},{16,8},{20,12},{24,16},{28,20},{32,24},{36,28},{40,32... | collective-permute-start | bytes 1572872 | tf_op jit(solution)/shard_map/ppermute | solution.py:17
  135.7 18.1 %collective-permute-start.7 = (f32[8,128,128]{2,1,0:T(8,128)S(1)}, f32[8,128,128]{2,1,0:T(8,128)S(1)}, u32[]{:S(2)}, u32[]{:S(2)}) collective-permute-start(f32[8,128,128]{2,1,0:T(8,128)S(1)} %multiply_add_fusion.2), channel_id=1, source_target_pairs={{16,0},{20,4},{24,8},{28,12},{32,16},{36,20},{40,24},{44,28},{48,3... | collective-permute-start | bytes 1572872 | tf_op jit(solution)/shard_map/ppermute | solution.py:17
  153.9 16.6 %collective-permute-start.8 = (f32[8,128,128]{2,1,0:T(8,128)S(1)}, f32[8,128,128]{2,1,0:T(8,128)S(1)}, u32[]{:S(2)}, u32[]{:S(2)}) collective-permute-start(f32[8,128,128]{2,1,0:T(8,128)S(1)} %multiply_add_fusion.1), channel_id=1, source_target_pairs={{4,0},{8,4},{12,8},{16,12},{20,16},{24,20},{28,24},{32,28},{36,32}... | collective-permute-start | bytes 1572872 | tf_op jit(solution)/shard_map/ppermute | solution.py:17
  156.3 31.0 %collective-permute-start.9 = (f32[8,128,128]{2,1,0:T(8,128)S(1)}, f32[8,128,128]{2,1,0:T(8,128)S(1)}, u32[]{:S(2)}, u32[]{:S(2)}) collective-permute-start(f32[8,128,128]{2,1,0:T(8,128)S(1)} %multiply_add_fusion.1), channel_id=1, source_target_pairs={{36,0},{40,4},{44,8},{48,12},{52,16},{56,20},{60,24},{64,28},{68,3... | collective-permute-start | bytes 1572872 | tf_op jit(solution)/shard_map/ppermute | solution.py:17
  188.1 1.0 copy-start.10

commit v4 on v3

--- a/solution.py
+++ b/solution.py
@@ -15,6 +15,23 @@
     devices = lax.axis_size(axis)
     pairs = [(i, i + by) for i in range(devices) if 0 <= i + by < devices]
     return lax.ppermute(x, axis, pairs)
+
+
+def send_state(x, axis, by):
+    return from_behind(x.astype(jnp.bfloat16), axis, by).astype(jnp.float32)
+
+
+def send_with(state, extra, axis, by):
+    width = state.shape[-1]
+    flat = jnp.concatenate(
+        [state.astype(jnp.bfloat16).reshape(-1, width), extra.astype(jnp.bfloat16).reshape(-1, width)]
+    )
+    moved = from_behind(flat, axis, by)
+    cut = state.size // width
+    return (
+        moved[:cut].reshape(state.shape).astype(jnp.float32),
+        moved[cut:].reshape(extra.shape).astype(jnp.float32),
+    )
 
 
 def tile_state(keys_t, values_t, doc_lengths, start):
@@ -134,7 +151,7 @@
     covered = SPAN
     while covered < need:
         (flag,) = front_flags(doc_lengths, [(place - covered, place - 1)], tile)
-        incoming = incoming + (1.0 - flag) * from_behind(incoming, "ctx", covered)
+        incoming = incoming + (1.0 - flag) * send_state(incoming, "ctx", covered)
         covered *= 2
     linear_out = (
         narrow("htu,uhd->thd", attend, values)
@@ -167,34 +184,45 @@
     tile_sum = narrow(
         "thd,the->hde", jnp.where(keep_first, queries, jnp.zeros_like(queries)), inner
     )
-    part = tile_sum
-    covered = 1
-    while 2 * covered < need:
-        (flag,) = back_flags(doc_lengths, [(place, place + covered - 1)], tile)
-        part = part + (1.0 - flag) * from_behind(part, "ctx", -covered)
-        covered *= 2
-    later = from_behind(part, "ctx", -1)
-    if covered < need:
-        (flag,) = back_flags(doc_lengths, [(place + 1, place + covered)], tile)
-        later = later + (1.0 - flag) * from_behind(part, "ctx", -1 - covered)
-    key_linear = (
-        narrow("htu,thd->uhd", back, queries)
-        + wide("uhe,hde->uhd", values.astype(jnp.float32), later) * carried_next[:, None, None]
-    )
-    value_linear = (
-        narrow("htu,the->uhe", attend, inner)
-        + wide("uhd,hde->uhe", keys.astype(jnp.float32), later) * carried_next[:, None, None]
-    )
     parts = [
         key_terms(dscore_list[position], weight_list[position], queries, cotangent, scale)
         for position in range(SPAN + 1)
     ]
     key_soft, value_soft = parts[SPAN]
-    for shift in range(1, SPAN + 1):
+    pending = list(range(1, SPAN + 1))
+
+    def returned_soft(key_soft, value_soft, moved):
+        return (key_soft + moved[0], value_soft + moved[1])
+
+    part = tile_sum
+    covered = 1
+    while 2 * covered < need:
+        (flag,) = back_flags(doc_lengths, [(place, place + covered - 1)], tile)
+        if covered in pending:
+            pending.remove(covered)
+            sent = jnp.stack(list(parts[SPAN - covered]))
+            received, moved = send_with(part, sent, "ctx", -covered)
+            key_soft, value_soft = returned_soft(key_soft, value_soft, moved)
+        else:
+            received = send_state(part, "ctx", -covered)
+        part = part + (1.0 - flag) * received
+        covered *= 2
+    later = send_state(part, "ctx", -1)
+    if covered < need:
+        (flag,) = back_flags(doc_lengths, [(place + 1, place + covered)], tile)
+        later = later + (1.0 - flag) * send_state(part, "ctx", -1 - covered)
+    for shift in pending:
         sent = jnp.stack([parts[SPAN - shift][0], parts[SPAN - shift][1]])
-        returned = from_behind(sent.astype(jnp.bfloat16), "ctx", -shift).astype(sent.dtype)
-        key_soft = key_soft + returned[0]
-        value_soft = value_soft + returned[1]
+        moved = from_behind(sent.astype(jnp.bfloat16), "ctx", -shift).astype(sent.dtype)
+        key_soft, value_soft = returned_soft(key_soft, value_soft, moved)
+    key_linear = (
+        narrow("htu,thd->uhd", back, queries)
+        + wide("uhe,hde->uhd", values.astype(jnp.float32), later) * carried_next[:, None, None]
+    )
+    value_linear = (
+        narrow("htu,the->uhe", attend, inner)
+        + wide("uhd,hde->uhe", keys.astype(jnp.float32), later) * carried_next[:, None, None]
+    )
     query_grad = (query_linear + query_soft).astype(jnp.bfloat16)
     key_grad = (key_linear + key_soft).astype(jnp.bfloat16)
     value_grad = (value_linear + value_soft).astype(jnp.bfloat16)

time: 191 us -> 152 us (0.80)
  the two profiles are of different devices: /device:TPU:71 before, /device:TPU:103 now
where the time goes in v4:
time: 152 us; the launch traced here: 151 us
  waiting for transfers between devices  63.1 us (42%)
  starting transfers between devices  32 us (21%)
  local copies, waits for them, and re-layouts  16 us (11%)
  matrix products  12.9 us (8%)
  between operations  12.1 us (8%)
  blocking collectives  8.71 us (6%)
  other arithmetic  5.93 us (4%)
    ppermute x10, waiting for transfers between devices, from_behind(): return lax.ppermute(x, axis, pairs)  63.1 us
    ppermute x10, starting transfers between devices, from_behind(): return lax.ppermute(x, axis, pairs)  32 us
    dot_general x26, matrix products, narrow(): return jnp.einsum(form, left, right, preferred_element_type=jnp.float32)  10.4 us
    psum x1, blocking collectives, per_device(): squares = lax.psum(jnp.sum(linear_out * linear_out, axis=(1, 2)), 'head')  8.71 us
    unnamed x36, local copies, waits for them, and re-layouts  7.87 us
  transfers between devices with their start and end apart: 10, of which 8 were waited for; matrix products, arithmetic and copies ran while one was open for 13% of the time, Pallas kernels for 0%

profile of v4, /device:TPU:103, one launch (start us, length us, event | category | flops | bytes accessed | tf_op | source)
XLA Modules:
  0.0 150.7 jit_solution(18302369360210774210)
XLA Ops:
  0.6 1.1 copy_bitcast_fusion
  1.9 4.8 %collective-permute-start.1 = (bf16[2,128,8,128]{3,1,2,0:T(8,128)(2,1)S(1)}, bf16[2,128,8,128]{3,1,2,0:T(8,128)(2,1)S(1)}, u32[]{:S(2)}, u32[]{:S(2)}) collective-permute-start(bf16[2,128,8,128]{3,1,2,0:T(8,128)(2,1)S(1)} %pad_maximum_fusion.2), channel_id=1, source_target_pairs={{0,8},{4,12},{8,16},{12,20},{16,24},{20,28},{24,32},{28,36},{32,40... | collective-permute-start | bytes 1572872 | tf_op jit(solution)/shard_map/ppermute | solution.py:17
  6.7 4.0 %collective-permute-start = (bf16[2,128,8,128]{3,1,2,0:T(8,128)(2,1)S(1)}, bf16[2,128,8,128]{3,1,2,0:T(8,128)(2,1)S(1)}, u32[]{:S(2)}, u32[]{:S(2)}) collective-permute-start(bf16[2,128,8,128]{3,1,2,0:T(8,128)(2,1)S(1)} %pad_maximum_fusion.2), channel_id=1, source_target_pairs={{0,4},{4,8},{8,12},{12,16},{16,20},{20,24},{24,28},{28,32},{32,36}... | collective-permute-start | bytes 1572872 | tf_op jit(solution)/shard_map/ppermute | solution.py:17
  11.0 0.6 fusion.106
  14.0 0.6 fusion.123
  14.6 0.7 fusion.118
  15.2 0.7 fusion.119
  15.9 0.6 fusion.120
  16.6 0.6 slice.103
  17.2 0.6 slice.110
  17.9 1.3 broadcast_compare_fusion.1
  19.3 0.6 fusion.121
  19.9 0.6 fusion.122
  20.5 0.6 fusion.117
  21.1 0.6 slice.108
  31.2 0.3 fusion.49
  31.5 0.4 convolution_multiply_fusion.7
  31.9 0.4 fusion.124
  32.3 3.1 %collective-permute-start.2 = (bf16[8,128,128]{2,1,0:T(8,128)(2,1)S(1)}, bf16[8,128,128]{2,1,0:T(8,128)(2,1)S(1)}, u32[]{:S(2)}, u32[]{:S(2)}) collective-permute-start(bf16[8,128,128]{2,1,0:T(8,128)(2,1)S(1)} %get-tuple-element.72), channel_id=1, source_target_pairs={{0,8},{4,12},{8,16},{12,20},{16,24},{20,28},{24,32},{28,36},{32,40... | collective-permute-start | bytes 786440 | tf_op jit(solution)/shard_map/ppermute | solution.py:17
  35.4 0.3 fusion.125
  35.7 0.3 fusion.126
  36.6 0.6 copy-done
  37.2 0.9 fusion.39
  38.2 0.3 convolution_bitcast_fusion.3
  38.5 3.1 %collective-permute-done.2 = bf16[8,128,128]{2,1,0:T(8,128)(2,1)S(1)} collective-permute-done((bf16[8,128,128]{2,1,0:T(8,128)(2,1)S(1)}, bf16[8,128,128]{2,1,0:T(8,128)(2,1)S(1)}, u32[]{:S(2)}, u32[]{:S(2)}) %collective-permute-start.2) | collective-permute-done | bytes 262176 | tf_op jit(solution)/shard_map/ppermute | solution.py:17
  41.6 4.0 %collective-permute-start.3 = (bf16[8,128,128]{2,1,0:T(8,128)(2,1)S(1)}, bf16[8,128,128]{2,1,0:T(8,128)(2,1)S(1)}, u32[]{:S(2)}, u32[]{:S(2)}) collective-permute-start(bf16[8,128,128]{2,1,0:T(8,128)(2,1)S(1)} %fusion.50), channel_id=1, source_target_pairs={{0,16},{4,20},{8,24},{12,28},{16,32},{20,36},{24,40},{28,44},{32,4... | collective-permute-start | bytes 786440 | tf_op jit(solution)/shard_map/ppermute | solution.py:17
  46.0 6.8 %collective-permute-done.3 = bf16[8,128,128]{2,1,0:T(8,128)(2,1)S(1)} collective-permute-done((bf16[8,128,128]{2,1,0:T(8,128)(2,1)S(1)}, bf16[8,128,128]{2,1,0:T(8,128)(2,1)S(1)}, u32[]{:S(2)}, u32[]{:S(2)}) %collective-permute-start.3) | collective-permute-done | bytes 262176 | tf_op jit(solution)/shard_map/ppermute | solution.py:17
  53.0 2.7 %collective-permute-start.4 = (bf16[8,128,128]{2,1,0:T(8,128)(2,1)S(1)}, bf16[8,128,128]{2,1,0:T(8,128)(2,1)S(1)}, u32[]{:S(2)}, u32[]{:S(2)}) collective-permute-start(bf16[8,128,128]{2,1,0:T(8,128)(2,1)S(1)} %get-tuple-element.41), channel_id=1, source_target_pairs={{0,32},{4,36},{8,40},{12,44},{16,48},{20,52},{24,56},{28,60},{32,6... | collective-permute-start | bytes 786440 | tf_op jit(solution)/shard_map/ppermute | solution.py:17
  55.6 0.9 fusion.38
  56.6 1.0 convolution_bitcast_fusion
  57.6 4.2 %collective-permute-done.4 = bf16[8,128,128]{2,1,0:T(8,128)(2,1)S(1)} collective-permute-done((bf16[8,128,128]{2,1,0:T(8,128)(2,1)S(1)}, bf16[8,128,128]{2,1,0:T(8,128)(2,1)S(1)}, u32[]{:S(2)}, u32[]{:S(2)}) %collective-permute-start.4) | collective-permute-done | bytes 262176 | tf_op jit(solution)/shard_map/ppermute | solution.py:17
  61.8 0.7 copy-done.11
  62.5 0.4 fusion.26
  63.0 1.2 fusion.44
  64.1 8.7 %all-reduce = (f32[128]{0:T(128)S(1)}, f32[128]{0:T(128)S(1)}) all-reduce(f32[128]{0:T(128)S(1)} %get-tuple-element.17, f32[128]{0:T(128)S(1)} %get-tuple-element.16), channel_id=1, replica_groups=mesh['ctx'=64,'head'=4] {'head'}, use_global_device_ids=true, to_apply=%region_10.11 | all-reduce | flops 256 | bytes 2048 | tf_op jit(solution)/shard_map/psum | solution.py:160
  72.9 1.3 fusion.43
  74.7 0.3 fusion.31
  75.0 0.4 copy-done.6
  75.4 0.3 fusion.29
  76.0 0.5 copy-done.8
  77.0 0.4 copy-done.13
  77.5 0.3 copy.198
  77.8 0.4 fusion.127
  78.2 5.7 %collective-permute-start.5 = (bf16[3072,128]{1,0:T(8,128)(2,1)S(1)}, bf16[3072,128]{1,0:T(8,128)(2,1)S(1)}, u32[]{:S(2)}, u32[]{:S(2)}) collective-permute-start(bf16[3072,128]{1,0:T(8,128)(2,1)S(1)} %pad_maximum_fusion), channel_id=1, source_target_pairs={{4,0},{8,4},{12,8},{16,12},{20,16},{24,20},{28,24},{32,28},{36,32}... | collective-permute-start | bytes 2359304 | tf_op jit(solution)/shard_map/ppermute | solution.py:17
  84.5 0.7 copy-done.4
  85.5 0.7 copy-done.10
  86.2 0.3 copy.201
  86.8 0.4 copy-done.12
  87.1 0.7 fusion.25
  88.1 13.2 %collective-permute-done.5 = bf16[3072,128]{1,0:T(8,128)(2,1)S(1)} collective-permute-done((bf16[3072,128]{1,0:T(8,128)(2,1)S(1)}, bf16[3072,128]{1,0:T(8,128)(2,1)S(1)}, u32[]{:S(2)}, u32[]{:S(2)}) %collective-permute-start.5) | collective-permute-done | bytes 786464 | tf_op jit(solution)/shard_map/ppermute | solution.py:17
  101.5 1.9 %collective-permute-start.6 = (bf16[3072,128]{1,0:T(8,128)(2,1)S(1)}, bf16[3072,128]{1,0:T(8,128)(2,1)S(1)}, u32[]{:S(2)}, u32[]{:S(2)}) collective-permute-start(bf16[3072,128]{1,0:T(8,128)(2,1)S(1)} %pad_maximum_fusion.1), channel_id=1, source_target_pairs={{8,0},{12,4},{16,8},{20,12},{24,16},{28,20},{32,24},{36,28},{40,32... | collective-permute-start | bytes 2359304 | tf_op jit(solution)/shard_map/ppermute | solution.py:17
  103.7 0.9 copy.216
  104.5 0.9 copy.217
  105.6 15.8 %collective-permute-done.6 = bf16[3072,128]{1,0:T(8,128)(2,1)S(1)} collective-permute-done((bf16[3072,128]{1,0:T(8,128)(2,1)S(1)}, bf16[3072,128]{1,0:T(8,128)(2,1)S(1)}, u32[]{:S(2)}, u32[]{:S(2)}) %collective-permute-start.6) | collective-permute-done | bytes 786464 | tf_op jit(solution)/shard_map/ppermute | solution.py:17
  121.5 1.9 %collective-permute-start.7 = (bf16[8,128,128]{2,1,0:T(8,128)(2,1)S(1)}, bf16[8,128,128]{2,1,0:T(8,128)(2,1)S(1)}, u32[]{:S(2)}, u32[]{:S(2)}) collective-permute-start(bf16[8,128,128]{2,1,0:T(8,128)(2,1)S(1)} %get-tuple-element.36), channel_id=1, source_target_pairs={{16,0},{20,4},{24,8},{28,12},{32,16},{36,20},{40,24},{44,28},{48,3... | collective-permute-start | bytes 786440 | tf_op jit(solution)/shard_map/ppermute | solution.py:17
  123.5 8.7 %collective-permute-done.7 = bf16[8,128,128]{2,1,0:T(8,128)(2,1)S(1)} collective-permute-done((bf16[8,128,128]{2,1,0:T(8,128)(2,1)S(1)}, bf16[8,128,128]{2,1,0:T(8,128)(2,1)S(1)}, u32[]{:S(2)}, u32[]{:S(2)}) %collective-permute-start.7) | collective-permute-done | bytes 262176 | tf_op jit(solution)/shard_map/ppermute | solution.py:17
  132.3 1.9 %collective-permute-start.9 = (bf16[8,128,128]{2,1,0:T(8,128)(2,1)S(1)}, bf16[8,128,128]{2,1,0:T(8,128)(2,1)S(1)}, u32[]{:S(2)}, u32[]{:S(2)}) collective-permute-start(bf16[8,128,128]{2,1,0:T(8,128)(2,1)S(1)} %add_convert_fusion), channel_id=1, source_target_pairs={{36,0},{40,4},{44,8},{48,12},{52,16},{56,20},{60,24},{64,28},{68,3... | collective-permute-start | bytes 786440 | tf_op jit(solution)/shard_map/ppermute | solution.py:17
  134.2 1.9 %collective-permute-start.8 = (bf16[8,128,128]{2,1,0:T(8,128)(2,1)S(1)}, bf16[8,128,128]{2,1,0:T(8,128)(2,1)S(1)}, u32[]{:S(2)}, u32[]{:S(2)}) collective-permute-start(bf16[8,128,128]{2,1,0:T(8,128)(2,1)S(1)} %add_convert_fusion), channel_id=1, source_target_pairs={{4,0},{8,4},{12,8},{16,12},{20,16},{24,20},{28,24},{32,28},{36,32}... | collective-permute-start | bytes 786440 | tf_op jit(solution)/shard_map/ppermute | solution.py:17
  136.2 10.3 %collective-permute-done.9 = bf16[8,128,128]{2,1,0:T(8,128)(2,1)S(1)} collective-permute-done((bf16[8,128,128]{2,1,0:T(8,128)(2,1)S(1)}, bf16[8,128,128]{2,1,0:T(8,128)(2,1)S(1)}, u32[]{:S(2)}, u32[]{:S(2)}) %collective-permute-start.9) | collective-permute-done | bytes 262176 | tf_op jit(solution)/shard_map/ppermute | solution.py:17
  146.5 1.0 collective-permute-done.8
  147.5 0.8 fusion.27
  148.3 0.9 copy.218
  149.2 0.6 fusion.28
  149.8 0.9 copy.219
  (87 shorter events, 6.4 us)
Async XLA Ops:
  0.6 10.1 %copy-start.15 = (s32[64]{0:T(128)S(1)}, s32[64]{0:T(128)}, u32[]{:S(2)}) copy-start(s32[64]{0:T(128)} %param.10) | copy-start | bytes 772
  1.8 29.4 %copy-start.1 = (bf16[128,8,128]{2,1,0:T(8,128)(2,1)S(1)}, bf16[128,8,128]{2,1,0:T(8,128)(2,1)}, u32[]{:S(2)}) copy-start(bf16[128,8,128]{2,1,0:T(8,128)(2,1)} %param.6) | copy-start | bytes 786436
  1.8 29.4 %copy-start.3 = (bf16[128,8,128]{2,1,0:T(8,128)(2,1)S(1)}, bf16[128,8,128]{2,1,0:T(8,128)(2,1)}, u32[]{:S(2)}) copy-start(bf16[128,8,128]{2,1,0:T(8,128)(2,1)} %param.7) | copy-start | bytes 786436
  1.9 29.6 %collective-permute-start.1 = (bf16[2,128,8,128]{3,1,2,0:T(8,128)(2,1)S(1)}, bf16[2,128,8,128]{3,1,2,0:T(8,128)(2,1)S(1)}, u32[]{:S(2)}, u32[]{:S(2)}) collective-permute-start(bf16[2,128,8,128]{3,1,2,0:T(8,128)(2,1)S(1)} %pad_maximum_fusion.2), channel_id=1, source_target_pairs={{0,8},{4,12},{8,16},{12,20},{16,24},{20,28},{24,32},{28,36},{32,40... | collective-permute-start | bytes 1572872 | tf_op jit(solution)/shard_map/ppermute | solution.py:17
  6.7 25.2 %collective-permute-start = (bf16[2,128,8,128]{3,1,2,0:T(8,128)(2,1)S(1)}, bf16[2,128,8,128]{3,1,2,0:T(8,128)(2,1)S(1)}, u32[]{:S(2)}, u32[]{:S(2)}) collective-permute-start(bf16[2,128,8,128]{3,1,2,0:T(8,128)(2,1)S(1)} %pad_maximum_fusion.2), channel_id=1, source_target_pairs={{0,4},{4,8},{8,12},{12,16},{16,20},{20,24},{24,28},{28,32},{32,36}... | collective-permute-start | bytes 1572872 | tf_op jit(solution)/shard_map/ppermute | solution.py:17
  31.5 14.2 %copy-start.5 = (bf16[2,128,8,128]{3,1,2,0:T(8,128)(2,1)}, bf16[2,128,8,128]{3,1,2,0:T(8,128)(2,1)S(1)}, u32[]{:S(2)}) copy-start(bf16[2,128,8,128]{3,1,2,0:T(8,128)(2,1)S(1)} %collective-permute-done.1) | copy-start | bytes 1572868
  31.9 4.4 %copy-start.7 = (bf16[2,128,8,128]{3,1,2,0:T(8,128)(2,1)}, bf16[2,128,8,128]{3,1,2,0:T(8,128)(2,1)S(1)}, u32[]{:S(2)}) copy-start(bf16[2,128,8,128]{3,1,2,0:T(8,128)(2,1)S(1)} %collective-permute-done) | copy-start | bytes 1572868
  32.3 9.3 %collective-permute-start.2 = (bf16[8,128,128]{2,1,0:T(8,128)(2,1)S(1)}, bf16[8,128,128]{2,1,0:T(8,128)(2,1)S(1)}, u32[]{:S(2)}, u32[]{:S(2)}) collective-permute-start(bf16[8,128,128]{2,1,0:T(8,128)(2,1)S(1)} %get-tuple-element.72), channel_id=1, source_target_pairs={{0,8},{4,12},{8,16},{12,20},{16,24},{20,28},{24,32},{28,36},{32,40... | collective-permute-start | bytes 786440 | tf_op jit(solution)/shard_map/ppermute | solution.py:17
  36.3 1.0 copy-start
  36.3 1.9 %copy-start.2 = (bf16[128,8,128]{2,1,0:T(8,128)(2,1)S(1)}, bf16[128,8,128]{2,1,0:T(8,128)(2,1)}, u32[]{:S(2)}) copy-start(bf16[128,8,128]{2,1,0:T(8,128)(2,1)} %param.8) | copy-start | bytes 786436
  41.6 11.2 %collective-permute-start.3 = (bf16[8,128,128]{2,1,0:T(8,128)(2,1)S(1)}, bf16[8,128,128]{2,1,0:T(8,128)(2,1)S(1)}, u32[]{:S(2)}, u32[]{:S(2)}) collective-permute-start(bf16[8,128,128]{2,1,0:T(8,128)(2,1)S(1)} %fusion.50), channel_id=1, source_target_pairs={{0,16},{4,20},{8,24},{12,28},{16,32},{20,36},{24,40},{28,44},{32,4... | collective-permute-start | bytes 786440 | tf_op jit(solution)/shard_map/ppermute | solution.py:17
  53.0 8.8 %collective-permute-start.4 = (bf16[8,128,128]{2,1,0:T(8,128)(2,1)S(1)}, bf16[8,128,128]{2,1,0:T(8,128)(2,1)S(1)}, u32[]{:S(2)}, u32[]{:S(2)}) collective-permute-start(bf16[8,128,128]{2,1,0:T(8,128)(2,1)S(1)} %get-tuple-element.41), channel_id=1, source_target_pairs={{0,32},{4,36},{8,40},{12,44},{16,48},{20,52},{24,56},{28,60},{32,6... | collective-permute-start | bytes 786440 | tf_op jit(solution)/shard_map/ppermute | solution.py:17
  57.6 5.4 %copy-start.14 = (f32[8,128]{1,0:T(8,128)S(1)}, f32[8,128]{1,0:T(8,128)}, u32[]{:S(2)}) copy-start(f32[8,128]{1,0:T(8,128)} %param.9) | copy-start | bytes 12292
  61.8 0.7 copy-start.11
  74.4 1.0 copy-start.6
  75.4 1.0 copy-start.8
  76.5 0.9 copy-start.13
  78.2 23.1 %collective-permute-start.5 = (bf16[3072,128]{1,0:T(8,128)(2,1)S(1)}, bf16[3072,128]{1,0:T(8,128)(2,1)S(1)}, u32[]{:S(2)}, u32[]{:S(2)}) collective-permute-start(bf16[3072,128]{1,0:T(8,128)(2,1)S(1)} %pad_maximum_fusion), channel_id=1, source_target_pairs={{4,0},{8,4},{12,8},{16,12},{20,16},{24,20},{28,24},{32,28},{36,32}... | collective-permute-start | bytes 2359304 | tf_op jit(solution)/shard_map/ppermute | solution.py:17
  84.2 1.0 copy-start.4
  85.2 0.9 copy-start.10
  86.2 1.0 copy-start.12
  101.5 19.8 %collective-permute-start.6 = (bf16[3072,128]{1,0:T(8,128)(2,1)S(1)}, bf16[3072,128]{1,0:T(8,128)(2,1)S(1)}, u32[]{:S(2)}, u32[]{:S(2)}) collective-permute-start(bf16[3072,128]{1,0:T(8,128)(2,1)S(1)} %pad_maximum_fusion.1), channel_id=1, source_target_pairs={{8,0},{12,4},{16,8},{20,12},{24,16},{28,20},{32,24},{36,28},{40,32... | collective-permute-start | bytes 2359304 | tf_op jit(solution)/shard_map/ppermute | solution.py:17
  121.5 10.7 %collective-permute-start.7 = (bf16[8,128,128]{2,1,0:T(8,128)(2,1)S(1)}, bf16[8,128,128]{2,1,0:T(8,128)(2,1)S(1)}, u32[]{:S(2)}, u32[]{:S(2)}) collective-permute-start(bf16[8,128,128]{2,1,0:T(8,128)(2,1)S(1)} %get-tuple-element.36), channel_id=1, source_target_pairs={{16,0},{20,4},{24,8},{28,12},{32,16},{36,20},{40,24},{44,28},{48,3... | collective-permute-start | bytes 786440 | tf_op jit(solution)/shard_map/ppermute | solution.py:17
  132.3 14.2 %collective-permute-start.9 = (bf16[8,128,128]{2,1,0:T(8,128)(2,1)S(1)}, bf16[8,128,128]{2,1,0:T(8,128)(2,1)S(1)}, u32[]{:S(2)}, u32[]{:S(2)}) collective-permute-start(bf16[8,128,128]{2,1,0:T(8,128)(2,1)S(1)} %add_convert_fusion), channel_id=1, source_target_pairs={{36,0},{40,4},{44,8},{48,12},{52,16},{56,20},{60,24},{64,28},{68,3... | collective-permute-start | bytes 786440 | tf_op jit(solution)/shard_map/ppermute | solution.py:17
  134.2 13.3 %collective-permute-start.8 = (bf16[8,128,128]{2,1,0:T(8,128)(2,1)S(1)}, bf16[8,128,128]{2,1,0:T(8,128)(2,1)S(1)}, u32[]{:S(2)}, u32[]{:S(2)}) collective-permute-start(bf16[8,128,128]{2,1,0:T(8,128)(2,1)S(1)} %add_convert_fusion), channel_id=1, source_target_pairs={{4,0},{8,4},{12,8},{16,12},{20,16},{24,20},{28,24},{32,28},{36,32}... | collective-permute-start | bytes 786440 | tf_op jit(solution)/shard_map/ppermute | solution.py:17
  147.5 1.7 %copy-start.9 = (f32[128,8,128]{2,0,1:T(8,128)S(1)}, f32[128,8,128]{2,0,1:T(8,128)}, u32[]{:S(2)}) copy-start(f32[128,8,128]{2,0,1:T(8,128)} %convolution_bitcast_fusion) | copy-start | bytes 1572868

commit v5 on v3

--- a/solution.py
+++ b/solution.py
@@ -15,6 +15,10 @@
     devices = lax.axis_size(axis)
     pairs = [(i, i + by) for i in range(devices) if 0 <= i + by < devices]
     return lax.ppermute(x, axis, pairs)
+
+
+def send_state(x, axis, by):
+    return from_behind(x.astype(jnp.bfloat16), axis, by).astype(jnp.float32)
 
 
 def tile_state(keys_t, values_t, doc_lengths, start):
@@ -122,6 +126,22 @@
     keep_first = (own_doc == own_doc[0])[:, None, None]
     query_wide = queries.astype(jnp.float32)
     attend = (narrow("thd,uhd->htu", queries, keys) * same_tile).astype(jnp.bfloat16)
+    grad_wide = cotangent.astype(jnp.float32)
+    row_dot = jnp.sum(grad_wide * soft_out, axis=-1).T
+    query_soft = jnp.zeros((tile, heads, width), jnp.float32)
+    dscore_list = []
+    for position in range(SPAN + 1):
+        dprobs = narrow("thd,uhd->htu", cotangent, value_tiles[position])
+        dscores = (prob_list[position] * (dprobs - row_dot[..., None])).astype(jnp.bfloat16)
+        query_soft = query_soft + narrow("htu,uhd->thd", dscores, key_tiles[position]) * scale
+        dscore_list.append(dscores)
+    parts = [
+        key_terms(dscore_list[position], weight_list[position], queries, cotangent, scale)
+        for position in range(SPAN + 1)
+    ]
+    outgoing = [
+        jnp.stack(list(parts[SPAN - shift])).astype(jnp.bfloat16) for shift in range(1, SPAN + 1)
+    ]
     place = lax.axis_index("ctx")
     need = min(-(-MAXDOC // tile), lax.axis_size("ctx"))
     near_states = [
@@ -132,9 +152,15 @@
     near_spans = [(place - SPAN + position, place - SPAN + position) for position in range(SPAN)]
     incoming = fold_states(near_states, front_flags(doc_lengths, near_spans, tile))
     covered = SPAN
+    returned = None
     while covered < need:
         (flag,) = front_flags(doc_lengths, [(place - covered, place - 1)], tile)
-        incoming = incoming + (1.0 - flag) * from_behind(incoming, "ctx", covered)
+        if 2 * covered >= need:
+            incoming, outgoing = lax.optimization_barrier((incoming, outgoing))
+            returned = [
+                from_behind(outgoing[shift - 1], "ctx", -shift) for shift in range(1, SPAN + 1)
+            ]
+        incoming = incoming + (1.0 - flag) * send_state(incoming, "ctx", covered)
         covered *= 2
     linear_out = (
         narrow("htu,uhd->thd", attend, values)
@@ -143,21 +169,12 @@
     squares = lax.psum(jnp.sum(linear_out * linear_out, axis=(1, 2)), "head")
     inverse = lax.rsqrt(squares / features + norm_eps)
     mixed = (linear_out * inverse[:, None, None] * gain[None] + soft_out).astype(jnp.bfloat16)
-    grad_wide = cotangent.astype(jnp.float32)
     weighted = grad_wide * gain[None]
     projection = lax.psum(jnp.sum(weighted * linear_out, axis=(1, 2)), "head")
     inner = (
         inverse[:, None, None] * weighted
         - linear_out * (inverse**3 * projection / features)[:, None, None]
     ).astype(jnp.bfloat16)
-    row_dot = jnp.sum(grad_wide * soft_out, axis=-1).T
-    query_soft = jnp.zeros((tile, heads, width), jnp.float32)
-    dscore_list = []
-    for position in range(SPAN + 1):
-        dprobs = narrow("thd,uhd->htu", cotangent, value_tiles[position])
-        dscores = (prob_list[position] * (dprobs - row_dot[..., None])).astype(jnp.bfloat16)
-        query_soft = query_soft + narrow("htu,uhd->thd", dscores, key_tiles[position]) * scale
-        dscore_list.append(dscores)
     inner_wide = inner.astype(jnp.float32)
     back = (narrow("thd,uhd->htu", inner, values) * same_tile).astype(jnp.bfloat16)
     query_linear = (
@@ -167,16 +184,25 @@
     tile_sum = narrow(
         "thd,the->hde", jnp.where(keep_first, queries, jnp.zeros_like(queries)), inner
     )
+    key_soft, value_soft = parts[SPAN]
+    if returned is None:
+        returned = [
+            from_behind(outgoing[shift - 1], "ctx", -shift) for shift in range(1, SPAN + 1)
+        ]
+    tile_sum, returned = lax.optimization_barrier((tile_sum, returned))
+    for moved in returned:
+        key_soft = key_soft + moved[0].astype(jnp.float32)
+        value_soft = value_soft + moved[1].astype(jnp.float32)
     part = tile_sum
     covered = 1
     while 2 * covered < need:
         (flag,) = back_flags(doc_lengths, [(place, place + covered - 1)], tile)
-        part = part + (1.0 - flag) * from_behind(part, "ctx", -covered)
+        part = part + (1.0 - flag) * send_state(part, "ctx", -covered)
         covered *= 2
-    later = from_behind(part, "ctx", -1)
+    later = send_state(part, "ctx", -1)
     if covered < need:
         (flag,) = back_flags(doc_lengths, [(place + 1, place + covered)], tile)
-        later = later + (1.0 - flag) * from_behind(part, "ctx", -1 - covered)
+        later = later + (1.0 - flag) * send_state(part, "ctx", -1 - covered)
     key_linear = (
         narrow("htu,thd->uhd", back, queries)
         + wide("uhe,hde->uhd", values.astype(jnp.float32), later) * carried_next[:, None, None]
@@ -185,16 +211,6 @@
         narrow("htu,the->uhe", attend, inner)
         + wide("uhd,hde->uhe", keys.astype(jnp.float32), later) * carried_next[:, None, None]
     )
-    parts = [
-        key_terms(dscore_list[position], weight_list[position], queries, cotangent, scale)
-        for position in range(SPAN + 1)
-    ]
-    key_soft, value_soft = parts[SPAN]
-    for shift in range(1, SPAN + 1):
-        sent = jnp.stack([parts[SPAN - shift][0], parts[SPAN - shift][1]])
-        returned = from_behind(sent.astype(jnp.bfloat16), "ctx", -shift).astype(sent.dtype)
-        key_soft = key_soft + returned[0]
-        value_soft = value_soft + returned[1]
     query_grad = (query_linear + query_soft).astype(jnp.bfloat16)
     key_grad = (key_linear + key_soft).astype(jnp.bfloat16)
     value_grad = (value_linear + value_soft).astype(jnp.bfloat16)

time: 191 us -> 142 us (0.74)
  the two profiles are of different devices: /device:TPU:71 before, /device:TPU:103 now
where the time goes in v5:
time: 142 us
  waiting for transfers between devices  48.6 us (34%)
  starting transfers between devices  40.7 us (29%)
  matrix products  12.8 us (9%)
  local copies, waits for them, and re-layouts  12.4 us (9%)
  between operations  12 us (8%)
  blocking collectives  8.74 us (6%)
  other arithmetic  6.39 us (4%)
    ppermute x12, waiting for transfers between devices, from_behind(): return lax.ppermute(x, axis, pairs)  48.6 us
    ppermute x12, starting transfers between devices, from_behind(): return lax.ppermute(x, axis, pairs)  40.7 us
    dot_general x26, matrix products, narrow(): return jnp.einsum(form, left, right, preferred_element_type=jnp.float32)  10.5 us
    psum x1, blocking collectives, per_device(): squares = lax.psum(jnp.sum(linear_out * linear_out, axis=(1, 2)), 'head')  8.74 us
    unnamed x22, local copies, waits for them, and re-layouts  5.14 us
  transfers between devices with their start and end apart: 12, of which 9 were waited for; matrix products, arithmetic and copies ran while one was open for 15% of the time, Pallas kernels for 0%

profile of v5, /device:TPU:103, one launch (start us, length us, event | category | flops | bytes accessed | tf_op | source)
XLA Modules:
  0.0 141.6 jit_solution(5483367299329181403)
XLA Ops:
  0.6 1.1 copy_bitcast_fusion
  1.8 4.7 %collective-permute-start.1 = (bf16[2,128,8,128]{3,1,2,0:T(8,128)(2,1)S(1)}, bf16[2,128,8,128]{3,1,2,0:T(8,128)(2,1)S(1)}, u32[]{:S(2)}, u32[]{:S(2)}) collective-permute-start(bf16[2,128,8,128]{3,1,2,0:T(8,128)(2,1)S(1)} %pad_maximum_fusion), channel_id=1, source_target_pairs={{0,8},{4,12},{8,16},{12,20},{16,24},{20,28},{24,32},{28,36},{32,40... | collective-permute-start | bytes 1572872 | tf_op jit(solution)/shard_map/ppermute | solution.py:17
  6.5 4.0 %collective-permute-start = (bf16[2,128,8,128]{3,1,2,0:T(8,128)(2,1)S(1)}, bf16[2,128,8,128]{3,1,2,0:T(8,128)(2,1)S(1)}, u32[]{:S(2)}, u32[]{:S(2)}) collective-permute-start(bf16[2,128,8,128]{3,1,2,0:T(8,128)(2,1)S(1)} %pad_maximum_fusion), channel_id=1, source_target_pairs={{0,4},{4,8},{8,12},{12,16},{16,20},{20,24},{24,28},{28,32},{32,36}... | collective-permute-start | bytes 1572872 | tf_op jit(solution)/shard_map/ppermute | solution.py:17
  10.9 0.6 fusion.112
  13.5 0.3 fusion.109
  13.9 0.6 fusion.126
  14.4 0.6 fusion.121
  15.1 0.6 fusion.122
  15.7 0.6 fusion.123
  16.3 0.6 slice.87
  16.9 0.6 slice.94
  17.7 1.3 broadcast_compare_fusion.1
  19.1 0.6 fusion.124
  19.7 0.7 fusion.125
  20.3 0.6 fusion.120
  20.9 0.6 slice.92
  31.0 0.3 fusion.53
  31.3 0.3 fusion.128
  31.7 0.3 fusion.129
  32.3 0.6 copy-done
  33.4 0.7 copy-done.2
  34.1 0.3 convolution_bitcast_fusion.3
  34.4 0.4 convolution_multiply_fusion.7
  34.8 0.4 fusion.127
  35.2 3.1 %collective-permute-start.2 = (bf16[8,128,128]{2,1,0:T(8,128)(2,1)S(1)}, bf16[8,128,128]{2,1,0:T(8,128)(2,1)S(1)}, u32[]{:S(2)}, u32[]{:S(2)}) collective-permute-start(bf16[8,128,128]{2,1,0:T(8,128)(2,1)S(1)} %get-tuple-element.73), channel_id=1, source_target_pairs={{0,8},{4,12},{8,16},{12,20},{16,24},{20,28},{24,32},{28,36},{32,40... | collective-permute-start | bytes 786440 | tf_op jit(solution)/shard_map/ppermute | solution.py:17
  38.6 0.4 fusion.49
  39.0 0.3 fusion.33
  39.6 0.3 fusion.32
  40.1 0.9 pad_maximum_fusion.2
  41.3 3.2 %collective-permute-done.2 = bf16[8,128,128]{2,1,0:T(8,128)(2,1)S(1)} collective-permute-done((bf16[8,128,128]{2,1,0:T(8,128)(2,1)S(1)}, bf16[8,128,128]{2,1,0:T(8,128)(2,1)S(1)}, u32[]{:S(2)}, u32[]{:S(2)}) %collective-permute-start.2) | collective-permute-done | bytes 262176 | tf_op jit(solution)/shard_map/ppermute | solution.py:17
  44.5 4.0 %collective-permute-start.3 = (bf16[8,128,128]{2,1,0:T(8,128)(2,1)S(1)}, bf16[8,128,128]{2,1,0:T(8,128)(2,1)S(1)}, u32[]{:S(2)}, u32[]{:S(2)}) collective-permute-start(bf16[8,128,128]{2,1,0:T(8,128)(2,1)S(1)} %fusion.54), channel_id=1, source_target_pairs={{0,16},{4,20},{8,24},{12,28},{16,32},{20,36},{24,40},{28,44},{32,4... | collective-permute-start | bytes 786440 | tf_op jit(solution)/shard_map/ppermute | solution.py:17
  48.6 0.8 pad_maximum_fusion.1
  49.4 0.3 fusion.34
  49.7 6.0 %collective-permute-done.3 = bf16[8,128,128]{2,1,0:T(8,128)(2,1)S(1)} collective-permute-done((bf16[8,128,128]{2,1,0:T(8,128)(2,1)S(1)}, bf16[8,128,128]{2,1,0:T(8,128)(2,1)S(1)}, u32[]{:S(2)}, u32[]{:S(2)}) %collective-permute-start.3) | collective-permute-done | bytes 262176 | tf_op jit(solution)/shard_map/ppermute | solution.py:17
  55.9 2.7 %collective-permute-start.4 = (bf16[8,128,128]{2,1,0:T(8,128)(2,1)S(1)}, bf16[8,128,128]{2,1,0:T(8,128)(2,1)S(1)}, u32[]{:S(2)}, u32[]{:S(2)}) collective-permute-start(bf16[8,128,128]{2,1,0:T(8,128)(2,1)S(1)} %convert_element_type.227), channel_id=1, source_target_pairs={{0,32},{4,36},{8,40},{12,44},{16,48},{20,52},{24,56},{28,60},{32,6... | collective-permute-start | bytes 786440 | tf_op jit(solution)/shard_map/ppermute | solution.py:17
  58.6 1.1 fusion.14
  59.7 3.1 %collective-permute-start.5 = (bf16[2,128,8,128]{3,1,2,0:T(8,128)(2,1)}, bf16[2,128,8,128]{3,1,2,0:T(8,128)(2,1)}, u32[]{:S(2)}, u32[]{:S(2)}) collective-permute-start(bf16[2,128,8,128]{3,1,2,0:T(8,128)(2,1)} %pad_maximum_fusion.1), channel_id=1, source_target_pairs={{4,0},{8,4},{12,8},{16,12},{20,16},{24,20},{28,24},{32,28},{36,32}... | collective-permute-start | bytes 1572872 | tf_op jit(solution)/shard_map/ppermute | solution.py:17
  62.8 3.6 %collective-permute-start.6 = (bf16[2,128,8,128]{3,1,2,0:T(8,128)(2,1)}, bf16[2,128,8,128]{3,1,2,0:T(8,128)(2,1)}, u32[]{:S(2)}, u32[]{:S(2)}) collective-permute-start(bf16[2,128,8,128]{3,1,2,0:T(8,128)(2,1)} %pad_maximum_fusion.2), channel_id=1, source_target_pairs={{8,0},{12,4},{16,8},{20,12},{24,16},{28,20},{32,24},{36,28},{40,32... | collective-permute-start | bytes 1572872 | tf_op jit(solution)/shard_map/ppermute | solution.py:17
  66.4 0.5 fusion.30
  67.1 0.4 fusion.48
  67.5 8.7 %all-reduce = (f32[128]{0:T(128)S(1)}, f32[128]{0:T(128)S(1)}) all-reduce(f32[128]{0:T(128)S(1)} %get-tuple-element.29, f32[128]{0:T(128)S(1)} %get-tuple-element.28), channel_id=1, replica_groups=mesh['ctx'=64,'head'=4] {'head'}, use_global_device_ids=true, to_apply=%region_17.18 | all-reduce | flops 256 | bytes 2048 | tf_op jit(solution)/shard_map/psum | solution.py:169
  76.5 0.3 fusion.58
  76.9 2.4 %collective-permute-done.5 = bf16[2,128,8,128]{3,1,2,0:T(8,128)(2,1)} collective-permute-done((bf16[2,128,8,128]{3,1,2,0:T(8,128)(2,1)}, bf16[2,128,8,128]{3,1,2,0:T(8,128)(2,1)}, u32[]{:S(2)}, u32[]{:S(2)}) %collective-permute-start.5) | collective-permute-done | bytes 524320 | tf_op jit(solution)/shard_map/ppermute | solution.py:17
  79.3 3.8 %collective-permute-done.6 = bf16[2,128,8,128]{3,1,2,0:T(8,128)(2,1)} collective-permute-done((bf16[2,128,8,128]{3,1,2,0:T(8,128)(2,1)}, bf16[2,128,8,128]{3,1,2,0:T(8,128)(2,1)}, u32[]{:S(2)}, u32[]{:S(2)}) %collective-permute-start.6) | collective-permute-done | bytes 524320 | tf_op jit(solution)/shard_map/ppermute | solution.py:17
  83.1 6.2 %collective-permute-start.7 = (bf16[8,128,128]{2,1,0:T(8,128)(2,1)S(1)}, bf16[8,128,128]{2,1,0:T(8,128)(2,1)S(1)}, u32[]{:S(2)}, u32[]{:S(2)}) collective-permute-start(bf16[8,128,128]{2,1,0:T(8,128)(2,1)S(1)} %convert_element_type.238), channel_id=1, source_target_pairs={{4,0},{8,4},{12,8},{16,12},{20,16},{24,20},{28,24},{32,28},{36,32}... | collective-permute-start | bytes 786440 | tf_op jit(solution)/shard_map/ppermute | solution.py:17
  89.6 0.3 fusion.39
  89.9 4.3 %collective-permute-done.7 = bf16[8,128,128]{2,1,0:T(8,128)(2,1)S(1)} collective-permute-done((bf16[8,128,128]{2,1,0:T(8,128)(2,1)S(1)}, bf16[8,128,128]{2,1,0:T(8,128)(2,1)S(1)}, u32[]{:S(2)}, u32[]{:S(2)}) %collective-permute-start.7) | collective-permute-done | bytes 262176 | tf_op jit(solution)/shard_map/ppermute | solution.py:17
  94.3 2.4 %collective-permute-start.8 = (bf16[8,128,128]{2,1,0:T(8,128)(2,1)S(1)}, bf16[8,128,128]{2,1,0:T(8,128)(2,1)S(1)}, u32[]{:S(2)}, u32[]{:S(2)}) collective-permute-start(bf16[8,128,128]{2,1,0:T(8,128)(2,1)S(1)} %fusion.55), channel_id=1, source_target_pairs={{8,0},{12,4},{16,8},{20,12},{24,16},{28,20},{32,24},{36,28},{40,32... | collective-permute-start | bytes 786440 | tf_op jit(solution)/shard_map/ppermute | solution.py:17
  96.7 0.7 fusion.29
  97.4 9.6 %collective-permute-done.8 = bf16[8,128,128]{2,1,0:T(8,128)(2,1)S(1)} collective-permute-done((bf16[8,128,128]{2,1,0:T(8,128)(2,1)S(1)}, bf16[8,128,128]{2,1,0:T(8,128)(2,1)S(1)}, u32[]{:S(2)}, u32[]{:S(2)}) %collective-permute-start.8) | collective-permute-done | bytes 262176 | tf_op jit(solution)/shard_map/ppermute | solution.py:17
  107.1 1.9 %collective-permute-start.9 = (bf16[8,128,128]{2,1,0:T(8,128)(2,1)S(1)}, bf16[8,128,128]{2,1,0:T(8,128)(2,1)S(1)}, u32[]{:S(2)}, u32[]{:S(2)}) collective-permute-start(bf16[8,128,128]{2,1,0:T(8,128)(2,1)S(1)} %fusion.74), channel_id=1, source_target_pairs={{16,0},{20,4},{24,8},{28,12},{32,16},{36,20},{40,24},{44,28},{48,3... | collective-permute-start | bytes 786440 | tf_op jit(solution)/shard_map/ppermute | solution.py:17
  109.3 11.0 %collective-permute-done.9 = bf16[8,128,128]{2,1,0:T(8,128)(2,1)S(1)} collective-permute-done((bf16[8,128,128]{2,1,0:T(8,128)(2,1)S(1)}, bf16[8,128,128]{2,1,0:T(8,128)(2,1)S(1)}, u32[]{:S(2)}, u32[]{:S(2)}) %collective-permute-start.9) | collective-permute-done | bytes 262176 | tf_op jit(solution)/shard_map/ppermute | solution.py:17
  120.5 2.2 %collective-permute-start.11 = (bf16[8,128,128]{2,1,0:T(8,128)(2,1)S(1)}, bf16[8,128,128]{2,1,0:T(8,128)(2,1)S(1)}, u32[]{:S(2)}, u32[]{:S(2)}) collective-permute-start(bf16[8,128,128]{2,1,0:T(8,128)(2,1)S(1)} %add_convert_fusion), channel_id=1, source_target_pairs={{36,0},{40,4},{44,8},{48,12},{52,16},{56,20},{60,24},{64,28},{68,3... | collective-permute-start | bytes 786440 | tf_op jit(solution)/shard_map/ppermute | solution.py:17
  122.7 2.8 %collective-permute-start.10 = (bf16[8,128,128]{2,1,0:T(8,128)(2,1)S(1)}, bf16[8,128,128]{2,1,0:T(8,128)(2,1)S(1)}, u32[]{:S(2)}, u32[]{:S(2)}) collective-permute-start(bf16[8,128,128]{2,1,0:T(8,128)(2,1)S(1)} %add_convert_fusion), channel_id=1, source_target_pairs={{4,0},{8,4},{12,8},{16,12},{20,16},{24,20},{28,24},{32,28},{36,32}... | collective-permute-start | bytes 786440 | tf_op jit(solution)/shard_map/ppermute | solution.py:17
  125.8 0.9 copy.204
  126.6 0.9 copy.205
  127.7 5.5 %collective-permute-done.11 = bf16[8,128,128]{2,1,0:T(8,128)(2,1)S(1)} collective-permute-done((bf16[8,128,128]{2,1,0:T(8,128)(2,1)S(1)}, bf16[8,128,128]{2,1,0:T(8,128)(2,1)S(1)}, u32[]{:S(2)}, u32[]{:S(2)}) %collective-permute-start.11) | collective-permute-done | bytes 262176 | tf_op jit(solution)/shard_map/ppermute | solution.py:17
  133.2 2.8 %collective-permute-done.10 = bf16[8,128,128]{2,1,0:T(8,128)(2,1)S(1)} collective-permute-done((bf16[8,128,128]{2,1,0:T(8,128)(2,1)S(1)}, bf16[8,128,128]{2,1,0:T(8,128)(2,1)S(1)}, u32[]{:S(2)}, u32[]{:S(2)}) %collective-permute-start.10) | collective-permute-done | bytes 262176 | tf_op jit(solution)/shard_map/ppermute | solution.py:17
  136.1 0.5 fusion.26
  136.5 1.3 fusion.31
  137.8 0.7 fusion.28
  138.5 1.3 fusion.35
  139.8 0.9 copy.206
  140.7 0.9 copy.207
  (69 shorter events, 5.3 us)
Async XLA Ops:
  1.8 8.8 %copy-start.8 = (s32[64]{0:T(128)S(1)}, s32[64]{0:T(128)}, u32[]{:S(2)}) copy-start(s32[64]{0:T(128)} %param.10) | copy-start | bytes 772
  1.8 29.5 %collective-permute-start.1 = (bf16[2,128,8,128]{3,1,2,0:T(8,128)(2,1)S(1)}, bf16[2,128,8,128]{3,1,2,0:T(8,128)(2,1)S(1)}, u32[]{:S(2)}, u32[]{:S(2)}) collective-permute-start(bf16[2,128,8,128]{3,1,2,0:T(8,128)(2,1)S(1)} %pad_maximum_fusion), channel_id=1, source_target_pairs={{0,8},{4,12},{8,16},{12,20},{16,24},{20,28},{24,32},{28,36},{32,40... | collective-permute-start | bytes 1572872 | tf_op jit(solution)/shard_map/ppermute | solution.py:17
  6.5 25.1 %collective-permute-start = (bf16[2,128,8,128]{3,1,2,0:T(8,128)(2,1)S(1)}, bf16[2,128,8,128]{3,1,2,0:T(8,128)(2,1)S(1)}, u32[]{:S(2)}, u32[]{:S(2)}) collective-permute-start(bf16[2,128,8,128]{3,1,2,0:T(8,128)(2,1)S(1)} %pad_maximum_fusion), channel_id=1, source_target_pairs={{0,4},{4,8},{8,12},{12,16},{16,20},{20,24},{24,28},{28,32},{32,36}... | collective-permute-start | bytes 1572872 | tf_op jit(solution)/shard_map/ppermute | solution.py:17
  10.5 20.5 %copy-start.3 = (bf16[128,8,128]{2,1,0:T(8,128)(2,1)S(1)}, bf16[128,8,128]{2,1,0:T(8,128)(2,1)}, u32[]{:S(2)}) copy-start(bf16[128,8,128]{2,1,0:T(8,128)(2,1)} %param.7) | copy-start | bytes 786436
  10.5 20.5 %copy-start.1 = (bf16[128,8,128]{2,1,0:T(8,128)(2,1)S(1)}, bf16[128,8,128]{2,1,0:T(8,128)(2,1)}, u32[]{:S(2)}) copy-start(bf16[128,8,128]{2,1,0:T(8,128)(2,1)} %param.6) | copy-start | bytes 786436
  32.0 1.0 copy-start
  33.2 1.0 copy-start.2
  35.2 9.3 %collective-permute-start.2 = (bf16[8,128,128]{2,1,0:T(8,128)(2,1)S(1)}, bf16[8,128,128]{2,1,0:T(8,128)(2,1)S(1)}, u32[]{:S(2)}, u32[]{:S(2)}) collective-permute-start(bf16[8,128,128]{2,1,0:T(8,128)(2,1)S(1)} %get-tuple-element.73), channel_id=1, source_target_pairs={{0,8},{4,12},{8,16},{12,20},{16,24},{20,28},{24,32},{28,36},{32,40... | collective-permute-start | bytes 786440 | tf_op jit(solution)/shard_map/ppermute | solution.py:17
  44.5 11.2 %collective-permute-start.3 = (bf16[8,128,128]{2,1,0:T(8,128)(2,1)S(1)}, bf16[8,128,128]{2,1,0:T(8,128)(2,1)S(1)}, u32[]{:S(2)}, u32[]{:S(2)}) collective-permute-start(bf16[8,128,128]{2,1,0:T(8,128)(2,1)S(1)} %fusion.54), channel_id=1, source_target_pairs={{0,16},{4,20},{8,24},{12,28},{16,32},{20,36},{24,40},{28,44},{32,4... | collective-permute-start | bytes 786440 | tf_op jit(solution)/shard_map/ppermute | solution.py:17
  55.9 10.5 %collective-permute-start.4 = (bf16[8,128,128]{2,1,0:T(8,128)(2,1)S(1)}, bf16[8,128,128]{2,1,0:T(8,128)(2,1)S(1)}, u32[]{:S(2)}, u32[]{:S(2)}) collective-permute-start(bf16[8,128,128]{2,1,0:T(8,128)(2,1)S(1)} %convert_element_type.227), channel_id=1, source_target_pairs={{0,32},{4,36},{8,40},{12,44},{16,48},{20,52},{24,56},{28,60},{32,6... | collective-permute-start | bytes 786440 | tf_op jit(solution)/shard_map/ppermute | solution.py:17
  59.7 19.7 %collective-permute-start.5 = (bf16[2,128,8,128]{3,1,2,0:T(8,128)(2,1)}, bf16[2,128,8,128]{3,1,2,0:T(8,128)(2,1)}, u32[]{:S(2)}, u32[]{:S(2)}) collective-permute-start(bf16[2,128,8,128]{3,1,2,0:T(8,128)(2,1)} %pad_maximum_fusion.1), channel_id=1, source_target_pairs={{4,0},{8,4},{12,8},{16,12},{20,16},{24,20},{28,24},{32,28},{36,32}... | collective-permute-start | bytes 1572872 | tf_op jit(solution)/shard_map/ppermute | solution.py:17
  62.8 20.3 %collective-permute-start.6 = (bf16[2,128,8,128]{3,1,2,0:T(8,128)(2,1)}, bf16[2,128,8,128]{3,1,2,0:T(8,128)(2,1)}, u32[]{:S(2)}, u32[]{:S(2)}) collective-permute-start(bf16[2,128,8,128]{3,1,2,0:T(8,128)(2,1)} %pad_maximum_fusion.2), channel_id=1, source_target_pairs={{8,0},{12,4},{16,8},{20,12},{24,16},{28,20},{32,24},{36,28},{40,32... | collective-permute-start | bytes 1572872 | tf_op jit(solution)/shard_map/ppermute | solution.py:17
  66.4 0.7 copy-start.5
  66.4 0.7 copy-start.7
  76.9 12.5 %copy-start.4 = (f32[128,8,128]{2,0,1:T(8,128)S(1)}, f32[128,8,128]{2,0,1:T(8,128)}, u32[]{:S(2)}) copy-start(f32[128,8,128]{2,0,1:T(8,128)} %fusion.14) | copy-start | bytes 1572868
  83.1 11.1 %collective-permute-start.7 = (bf16[8,128,128]{2,1,0:T(8,128)(2,1)S(1)}, bf16[8,128,128]{2,1,0:T(8,128)(2,1)S(1)}, u32[]{:S(2)}, u32[]{:S(2)}) collective-permute-start(bf16[8,128,128]{2,1,0:T(8,128)(2,1)S(1)} %convert_element_type.238), channel_id=1, source_target_pairs={{4,0},{8,4},{12,8},{16,12},{20,16},{24,20},{28,24},{32,28},{36,32}... | collective-permute-start | bytes 786440 | tf_op jit(solution)/shard_map/ppermute | solution.py:17
  94.2 2.5 %copy-start.6 = (bf16[8,128,128]{2,1,0:T(8,128)(2,1)S(1)}, bf16[8,128,128]{2,1,0:T(8,128)(2,1)}, u32[]{:S(2)}) copy-start(bf16[8,128,128]{2,1,0:T(8,128)(2,1)} %copy-done.5) | copy-start | bytes 786436
  94.3 12.7 %collective-permute-start.8 = (bf16[8,128,128]{2,1,0:T(8,128)(2,1)S(1)}, bf16[8,128,128]{2,1,0:T(8,128)(2,1)S(1)}, u32[]{:S(2)}, u32[]{:S(2)}) collective-permute-start(bf16[8,128,128]{2,1,0:T(8,128)(2,1)S(1)} %fusion.55), channel_id=1, source_target_pairs={{8,0},{12,4},{16,8},{20,12},{24,16},{28,20},{32,24},{36,28},{40,32... | collective-permute-start | bytes 786440 | tf_op jit(solution)/shard_map/ppermute | solution.py:17
  107.1 13.2 %collective-permute-start.9 = (bf16[8,128,128]{2,1,0:T(8,128)(2,1)S(1)}, bf16[8,128,128]{2,1,0:T(8,128)(2,1)S(1)}, u32[]{:S(2)}, u32[]{:S(2)}) collective-permute-start(bf16[8,128,128]{2,1,0:T(8,128)(2,1)S(1)} %fusion.74), channel_id=1, source_target_pairs={{16,0},{20,4},{24,8},{28,12},{32,16},{36,20},{40,24},{44,28},{48,3... | collective-permute-start | bytes 786440 | tf_op jit(solution)/shard_map/ppermute | solution.py:17
  120.5 12.8 %collective-permute-start.11 = (bf16[8,128,128]{2,1,0:T(8,128)(2,1)S(1)}, bf16[8,128,128]{2,1,0:T(8,128)(2,1)S(1)}, u32[]{:S(2)}, u32[]{:S(2)}) collective-permute-start(bf16[8,128,128]{2,1,0:T(8,128)(2,1)S(1)} %add_convert_fusion), channel_id=1, source_target_pairs={{36,0},{40,4},{44,8},{48,12},{52,16},{56,20},{60,24},{64,28},{68,3... | collective-permute-start | bytes 786440 | tf_op jit(solution)/shard_map/ppermute | solution.py:17
  122.7 13.4 %collective-permute-start.10 = (bf16[8,128,128]{2,1,0:T(8,128)(2,1)S(1)}, bf16[8,128,128]{2,1,0:T(8,128)(2,1)S(1)}, u32[]{:S(2)}, u32[]{:S(2)}) collective-permute-start(bf16[8,128,128]{2,1,0:T(8,128)(2,1)S(1)} %add_convert_fusion), channel_id=1, source_target_pairs={{4,0},{8,4},{12,8},{16,12},{20,16},{24,20},{28,24},{32,28},{36,32}... | collective-permute-start | bytes 786440 | tf_op jit(solution)/shard_map/ppermute | solution.py:17

commit v6 on v5

--- a/solution.py
+++ b/solution.py
@@ -17,7 +17,9 @@
     return lax.ppermute(x, axis, pairs)
 
 
-def send_state(x, axis, by):
+def send_state(x, axis, by, exact=False):
+    if exact:
+        return from_behind(x, axis, by)
     return from_behind(x.astype(jnp.bfloat16), axis, by).astype(jnp.float32)
 
 
@@ -160,7 +162,9 @@
             returned = [
                 from_behind(outgoing[shift - 1], "ctx", -shift) for shift in range(1, SPAN + 1)
             ]
-        incoming = incoming + (1.0 - flag) * send_state(incoming, "ctx", covered)
+        incoming = incoming + (1.0 - flag) * send_state(
+            incoming, "ctx", covered, exact=2 * covered >= need
+        )
         covered *= 2
     linear_out = (
         narrow("htu,uhd->thd", attend, values)
@@ -199,10 +203,10 @@
         (flag,) = back_flags(doc_lengths, [(place, place + covered - 1)], tile)
         part = part + (1.0 - flag) * send_state(part, "ctx", -covered)
         covered *= 2
-    later = send_state(part, "ctx", -1)
+    later = send_state(part, "ctx", -1, exact=True)
     if covered < need:
         (flag,) = back_flags(doc_lengths, [(place + 1, place + covered)], tile)
-        later = later + (1.0 - flag) * send_state(part, "ctx", -1 - covered)
+        later = later + (1.0 - flag) * send_state(part, "ctx", -1 - covered, exact=True)
     key_linear = (
         narrow("htu,thd->uhd", back, queries)
         + wide("uhe,hde->uhd", values.astype(jnp.float32), later) * carried_next[:, None, None]

time: 142 us -> 159 us (1.12)
  the two profiles are of different devices: /device:TPU:103 before, /device:TPU:79 now
where the time goes in v6:
time: 159 us; the launch traced here: 158 us
  waiting for transfers between devices  60 us (38%)
  starting transfers between devices  45.7 us (29%)
  matrix products  14.9 us (9%)
  between operations  12.1 us (8%)
  local copies, waits for them, and re-layouts  11.4 us (7%)
  other arithmetic  7.29 us (5%)
  blocking collectives  6.65 us (4%)
    ppermute x12, waiting for transfers between devices, from_behind(): return lax.ppermute(x, axis, pairs)  60 us
    ppermute x12, starting transfers between devices, from_behind(): return lax.ppermute(x, axis, pairs)  45.7 us
    dot_general x26, matrix products, narrow(): return jnp.einsum(form, left, right, preferred_element_type=jnp.float32)  11.8 us
    psum x1, blocking collectives, per_device(): squares = lax.psum(jnp.sum(linear_out * linear_out, axis=(1, 2)), 'head')  6.65 us
    unnamed x26, local copies, waits for them, and re-layouts  4.18 us
  transfers between devices with their start and end apart: 12, of which 9 were waited for; matrix products, arithmetic and copies ran while one was open for 15% of the time, Pallas kernels for 0%

profile of v6, /device:TPU:79, one launch (start us, length us, event | category | flops | bytes accessed | tf_op | source)
XLA Modules:
  0.0 158.0 jit_solution(11116631868638000196)
XLA Ops:
  0.6 1.1 copy_bitcast_fusion
  1.9 3.6 %collective-permute-start.1 = (bf16[2,128,8,128]{3,1,2,0:T(8,128)(2,1)S(1)}, bf16[2,128,8,128]{3,1,2,0:T(8,128)(2,1)S(1)}, u32[]{:S(2)}, u32[]{:S(2)}) collective-permute-start(bf16[2,128,8,128]{3,1,2,0:T(8,128)(2,1)S(1)} %pad_maximum_fusion), channel_id=1, source_target_pairs={{0,8},{4,12},{8,16},{12,20},{16,24},{20,28},{24,32},{28,36},{32,40... | collective-permute-start | bytes 1572872 | tf_op jit(solution)/shard_map/ppermute | solution.py:17
  5.5 4.0 %collective-permute-start = (bf16[2,128,8,128]{3,1,2,0:T(8,128)(2,1)S(1)}, bf16[2,128,8,128]{3,1,2,0:T(8,128)(2,1)S(1)}, u32[]{:S(2)}, u32[]{:S(2)}) collective-permute-start(bf16[2,128,8,128]{3,1,2,0:T(8,128)(2,1)S(1)} %pad_maximum_fusion), channel_id=1, source_target_pairs={{0,4},{4,8},{8,12},{12,16},{16,20},{20,24},{24,28},{28,32},{32,36}... | collective-permute-start | bytes 1572872 | tf_op jit(solution)/shard_map/ppermute | solution.py:17
  9.8 0.6 fusion.108
  10.6 0.7 slice.94
  11.2 0.6 slice.87
  13.9 0.3 fusion.105
  14.2 0.6 fusion.122
  14.8 0.6 fusion.121
  15.4 0.6 fusion.120
  16.1 0.3 fusion.53
  16.4 1.3 broadcast_compare_fusion.1
  17.7 0.6 fusion.119
  18.3 0.6 fusion.118
  18.9 0.6 fusion.117
  19.5 0.6 slice.92
  23.6 0.3 fusion.125
  24.0 0.3 fusion.124
  24.6 0.3 convolution_bitcast_fusion.3
  24.9 0.6 copy-done
  26.0 0.4 convolution_multiply_fusion.7
  26.4 0.4 fusion.123
  26.7 3.1 %collective-permute-start.2 = (bf16[8,128,128]{2,1,0:T(8,128)(2,1)S(1)}, bf16[8,128,128]{2,1,0:T(8,128)(2,1)S(1)}, u32[]{:S(2)}, u32[]{:S(2)}) collective-permute-start(bf16[8,128,128]{2,1,0:T(8,128)(2,1)S(1)} %get-tuple-element.73), channel_id=1, source_target_pairs={{0,8},{4,12},{8,16},{12,20},{16,24},{20,28},{24,32},{28,36},{32,40... | collective-permute-start | bytes 786440 | tf_op jit(solution)/shard_map/ppermute | solution.py:17
  30.2 1.1 fusion.49
  31.3 0.3 fusion.33
  31.8 0.9 pad_maximum_fusion.1
  32.7 0.3 fusion.34
  33.0 3.3 %collective-permute-done.2 = bf16[8,128,128]{2,1,0:T(8,128)(2,1)S(1)} collective-permute-done((bf16[8,128,128]{2,1,0:T(8,128)(2,1)S(1)}, bf16[8,128,128]{2,1,0:T(8,128)(2,1)S(1)}, u32[]{:S(2)}, u32[]{:S(2)}) %collective-permute-start.2) | collective-permute-done | bytes 262176 | tf_op jit(solution)/shard_map/ppermute | solution.py:17
  36.4 4.7 %collective-permute-start.3 = (bf16[8,128,128]{2,1,0:T(8,128)(2,1)S(1)}, bf16[8,128,128]{2,1,0:T(8,128)(2,1)S(1)}, u32[]{:S(2)}, u32[]{:S(2)}) collective-permute-start(bf16[8,128,128]{2,1,0:T(8,128)(2,1)S(1)} %fusion.54), channel_id=1, source_target_pairs={{0,16},{4,20},{8,24},{12,28},{16,32},{20,36},{24,40},{28,44},{32,4... | collective-permute-start | bytes 786440 | tf_op jit(solution)/shard_map/ppermute | solution.py:17
  41.3 0.8 pad_maximum_fusion.2
  42.2 4.4 %collective-permute-done.3 = bf16[8,128,128]{2,1,0:T(8,128)(2,1)S(1)} collective-permute-done((bf16[8,128,128]{2,1,0:T(8,128)(2,1)S(1)}, bf16[8,128,128]{2,1,0:T(8,128)(2,1)S(1)}, u32[]{:S(2)}, u32[]{:S(2)}) %collective-permute-start.3) | collective-permute-done | bytes 262176 | tf_op jit(solution)/shard_map/ppermute | solution.py:17
  46.7 3.8 %collective-permute-start.4 = (f32[8,128,128]{2,1,0:T(8,128)S(1)}, f32[8,128,128]{2,1,0:T(8,128)S(1)}, u32[]{:S(2)}, u32[]{:S(2)}) collective-permute-start(f32[8,128,128]{2,1,0:T(8,128)S(1)} %multiply_add_fusion.5), channel_id=1, source_target_pairs={{0,32},{4,36},{8,40},{12,44},{16,48},{20,52},{24,56},{28,60},{32,6... | collective-permute-start | bytes 1572872 | tf_op jit(solution)/shard_map/ppermute | solution.py:17
  50.5 0.6 fusion.116
  57.4 1.1 fusion.63
  58.5 1.0 fusion.35
  59.5 4.8 %collective-permute-start.5 = (bf16[2,128,8,128]{3,1,2,0:T(8,128)(2,1)}, bf16[2,128,8,128]{3,1,2,0:T(8,128)(2,1)}, u32[]{:S(2)}, u32[]{:S(2)}) collective-permute-start(bf16[2,128,8,128]{3,1,2,0:T(8,128)(2,1)} %pad_maximum_fusion.1), channel_id=1, source_target_pairs={{4,0},{8,4},{12,8},{16,12},{20,16},{24,20},{28,24},{32,28},{36,32}... | collective-permute-start | bytes 1572872 | tf_op jit(solution)/shard_map/ppermute | solution.py:17
  64.3 3.7 %collective-permute-start.6 = (bf16[2,128,8,128]{3,1,2,0:T(8,128)(2,1)}, bf16[2,128,8,128]{3,1,2,0:T(8,128)(2,1)}, u32[]{:S(2)}, u32[]{:S(2)}) collective-permute-start(bf16[2,128,8,128]{3,1,2,0:T(8,128)(2,1)} %pad_maximum_fusion.2), channel_id=1, source_target_pairs={{8,0},{12,4},{16,8},{20,12},{24,16},{28,20},{32,24},{36,28},{40,32... | collective-permute-start | bytes 1572872 | tf_op jit(solution)/shard_map/ppermute | solution.py:17
  68.1 1.4 fusion.48
  69.5 6.6 %all-reduce = (f32[128]{0:T(128)S(1)}, f32[128]{0:T(128)S(1)}) all-reduce(f32[128]{0:T(128)S(1)} %get-tuple-element.29, f32[128]{0:T(128)S(1)} %get-tuple-element.28), channel_id=1, replica_groups=mesh['ctx'=64,'head'=4] {'head'}, use_global_device_ids=true, to_apply=%region_17.18 | all-reduce | flops 256 | bytes 2048 | tf_op jit(solution)/shard_map/psum | solution.py:173
  76.1 1.3 fusion.47
  77.4 0.3 fusion.56
  77.8 4.5 %collective-permute-done.5 = bf16[2,128,8,128]{3,1,2,0:T(8,128)(2,1)} collective-permute-done((bf16[2,128,8,128]{3,1,2,0:T(8,128)(2,1)}, bf16[2,128,8,128]{3,1,2,0:T(8,128)(2,1)}, u32[]{:S(2)}, u32[]{:S(2)}) %collective-permute-start.5) | collective-permute-done | bytes 524320 | tf_op jit(solution)/shard_map/ppermute | solution.py:17
  82.3 3.8 %collective-permute-done.6 = bf16[2,128,8,128]{3,1,2,0:T(8,128)(2,1)} collective-permute-done((bf16[2,128,8,128]{3,1,2,0:T(8,128)(2,1)}, bf16[2,128,8,128]{3,1,2,0:T(8,128)(2,1)}, u32[]{:S(2)}, u32[]{:S(2)}) %collective-permute-start.6) | collective-permute-done | bytes 524320 | tf_op jit(solution)/shard_map/ppermute | solution.py:17
  86.1 6.2 %collective-permute-start.7 = (bf16[8,128,128]{2,1,0:T(8,128)(2,1)S(1)}, bf16[8,128,128]{2,1,0:T(8,128)(2,1)S(1)}, u32[]{:S(2)}, u32[]{:S(2)}) collective-permute-start(bf16[8,128,128]{2,1,0:T(8,128)(2,1)S(1)} %convert_element_type.220), channel_id=1, source_target_pairs={{4,0},{8,4},{12,8},{16,12},{20,16},{24,20},{28,24},{32,28},{36,32}... | collective-permute-start | bytes 786440 | tf_op jit(solution)/shard_map/ppermute | solution.py:17
  92.6 3.3 %collective-permute-done.7 = bf16[8,128,128]{2,1,0:T(8,128)(2,1)S(1)} collective-permute-done((bf16[8,128,128]{2,1,0:T(8,128)(2,1)S(1)}, bf16[8,128,128]{2,1,0:T(8,128)(2,1)S(1)}, u32[]{:S(2)}, u32[]{:S(2)}) %collective-permute-start.7) | collective-permute-done | bytes 262176 | tf_op jit(solution)/shard_map/ppermute | solution.py:17
  96.0 3.7 %collective-permute-start.8 = (bf16[8,128,128]{2,1,0:T(8,128)(2,1)S(1)}, bf16[8,128,128]{2,1,0:T(8,128)(2,1)S(1)}, u32[]{:S(2)}, u32[]{:S(2)}) collective-permute-start(bf16[8,128,128]{2,1,0:T(8,128)(2,1)S(1)} %fusion.55), channel_id=1, source_target_pairs={{8,0},{12,4},{16,8},{20,12},{24,16},{28,20},{32,24},{36,28},{40,32... | collective-permute-start | bytes 786440 | tf_op jit(solution)/shard_map/ppermute | solution.py:17
  99.7 0.3 fusion.39
  100.3 7.3 %collective-permute-done.8 = bf16[8,128,128]{2,1,0:T(8,128)(2,1)S(1)} collective-permute-done((bf16[8,128,128]{2,1,0:T(8,128)(2,1)S(1)}, bf16[8,128,128]{2,1,0:T(8,128)(2,1)S(1)}, u32[]{:S(2)}, u32[]{:S(2)}) %collective-permute-start.8) | collective-permute-done | bytes 262176 | tf_op jit(solution)/shard_map/ppermute | solution.py:17
  107.7 2.1 %collective-permute-start.9 = (bf16[8,128,128]{2,1,0:T(8,128)(2,1)S(1)}, bf16[8,128,128]{2,1,0:T(8,128)(2,1)S(1)}, u32[]{:S(2)}, u32[]{:S(2)}) collective-permute-start(bf16[8,128,128]{2,1,0:T(8,128)(2,1)S(1)} %fusion.70), channel_id=1, source_target_pairs={{16,0},{20,4},{24,8},{28,12},{32,16},{36,20},{40,24},{44,28},{48,3... | collective-permute-start | bytes 786440 | tf_op jit(solution)/shard_map/ppermute | solution.py:17
  109.8 0.7 fusion.28
  110.5 8.4 %collective-permute-done.9 = bf16[8,128,128]{2,1,0:T(8,128)(2,1)S(1)} collective-permute-done((bf16[8,128,128]{2,1,0:T(8,128)(2,1)S(1)}, bf16[8,128,128]{2,1,0:T(8,128)(2,1)S(1)}, u32[]{:S(2)}, u32[]{:S(2)}) %collective-permute-start.9) | collective-permute-done | bytes 262176 | tf_op jit(solution)/shard_map/ppermute | solution.py:17
  119.1 3.9 %collective-permute-start.10 = (f32[8,128,128]{2,1,0:T(8,128)S(1)}, f32[8,128,128]{2,1,0:T(8,128)S(1)}, u32[]{:S(2)}, u32[]{:S(2)}) collective-permute-start(f32[8,128,128]{2,1,0:T(8,128)S(1)} %multiply_add_fusion.1), channel_id=1, source_target_pairs={{4,0},{8,4},{12,8},{16,12},{20,16},{24,20},{28,24},{32,28},{36,32}... | collective-permute-start | bytes 1572872 | tf_op jit(solution)/shard_map/ppermute | solution.py:17
  123.0 2.1 %collective-permute-start.11 = (f32[8,128,128]{2,1,0:T(8,128)S(1)}, f32[8,128,128]{2,1,0:T(8,128)S(1)}, u32[]{:S(2)}, u32[]{:S(2)}) collective-permute-start(f32[8,128,128]{2,1,0:T(8,128)S(1)} %multiply_add_fusion.1), channel_id=1, source_target_pairs={{36,0},{40,4},{44,8},{48,12},{52,16},{56,20},{60,24},{64,28},{68,3... | collective-permute-start | bytes 1572872 | tf_op jit(solution)/shard_map/ppermute | solution.py:17
  125.1 0.3 fusion.31
  125.4 0.9 copy.204
  126.3 0.9 copy.205
  127.6 8.3 %collective-permute-done.10 = f32[8,128,128]{2,1,0:T(8,128)S(1)} collective-permute-done((f32[8,128,128]{2,1,0:T(8,128)S(1)}, f32[8,128,128]{2,1,0:T(8,128)S(1)}, u32[]{:S(2)}, u32[]{:S(2)}) %collective-permute-start.10) | collective-permute-done | bytes 524320 | tf_op jit(solution)/shard_map/ppermute | solution.py:17
  135.9 16.7 %collective-permute-done.11 = f32[8,128,128]{2,1,0:T(8,128)S(1)} collective-permute-done((f32[8,128,128]{2,1,0:T(8,128)S(1)}, f32[8,128,128]{2,1,0:T(8,128)S(1)}, u32[]{:S(2)}, u32[]{:S(2)}) %collective-permute-start.11) | collective-permute-done | bytes 524320 | tf_op jit(solution)/shard_map/ppermute | solution.py:17
  152.6 0.7 fusion.26
  153.2 1.3 fusion.36
  154.5 0.9 copy.206
  155.4 0.4 fusion.24
  155.8 1.3 fusion.32
  157.1 0.9 copy.207
  (72 shorter events, 4.7 us)
Async XLA Ops:
  1.8 7.7 %copy-start.10 = (s32[64]{0:T(128)S(1)}, s32[64]{0:T(128)}, u32[]{:S(2)}) copy-start(s32[64]{0:T(128)} %param.10) | copy-start | bytes 772
  1.8 14.3 %copy-start.3 = (bf16[128,8,128]{2,1,0:T(8,128)(2,1)S(1)}, bf16[128,8,128]{2,1,0:T(8,128)(2,1)}, u32[]{:S(2)}) copy-start(bf16[128,8,128]{2,1,0:T(8,128)(2,1)} %param.7) | copy-start | bytes 786436
  1.8 14.2 %copy-start.1 = (bf16[128,8,128]{2,1,0:T(8,128)(2,1)S(1)}, bf16[128,8,128]{2,1,0:T(8,128)(2,1)}, u32[]{:S(2)}) copy-start(bf16[128,8,128]{2,1,0:T(8,128)(2,1)} %param.6) | copy-start | bytes 786436
  1.9 22.1 %collective-permute-start.1 = (bf16[2,128,8,128]{3,1,2,0:T(8,128)(2,1)S(1)}, bf16[2,128,8,128]{3,1,2,0:T(8,128)(2,1)S(1)}, u32[]{:S(2)}, u32[]{:S(2)}) collective-permute-start(bf16[2,128,8,128]{3,1,2,0:T(8,128)(2,1)S(1)} %pad_maximum_fusion), channel_id=1, source_target_pairs={{0,8},{4,12},{8,16},{12,20},{16,24},{20,28},{24,32},{28,36},{32,40... | collective-permute-start | bytes 1572872 | tf_op jit(solution)/shard_map/ppermute | solution.py:17
  5.5 18.2 %collective-permute-start = (bf16[2,128,8,128]{3,1,2,0:T(8,128)(2,1)S(1)}, bf16[2,128,8,128]{3,1,2,0:T(8,128)(2,1)S(1)}, u32[]{:S(2)}, u32[]{:S(2)}) collective-permute-start(bf16[2,128,8,128]{3,1,2,0:T(8,128)(2,1)S(1)} %pad_maximum_fusion), channel_id=1, source_target_pairs={{0,4},{4,8},{8,12},{12,16},{16,20},{20,24},{24,28},{28,32},{32,36}... | collective-permute-start | bytes 1572872 | tf_op jit(solution)/shard_map/ppermute | solution.py:17
  16.1 7.3 %copy-start.2 = (bf16[128,8,128]{2,1,0:T(8,128)(2,1)S(1)}, bf16[128,8,128]{2,1,0:T(8,128)(2,1)}, u32[]{:S(2)}) copy-start(bf16[128,8,128]{2,1,0:T(8,128)(2,1)} %param.8) | copy-start | bytes 786436
  24.6 1.0 copy-start
  26.7 9.6 %collective-permute-start.2 = (bf16[8,128,128]{2,1,0:T(8,128)(2,1)S(1)}, bf16[8,128,128]{2,1,0:T(8,128)(2,1)S(1)}, u32[]{:S(2)}, u32[]{:S(2)}) collective-permute-start(bf16[8,128,128]{2,1,0:T(8,128)(2,1)S(1)} %get-tuple-element.73), channel_id=1, source_target_pairs={{0,8},{4,12},{8,16},{12,20},{16,24},{20,28},{24,32},{28,36},{32,40... | collective-permute-start | bytes 786440 | tf_op jit(solution)/shard_map/ppermute | solution.py:17
  36.4 10.2 %collective-permute-start.3 = (bf16[8,128,128]{2,1,0:T(8,128)(2,1)S(1)}, bf16[8,128,128]{2,1,0:T(8,128)(2,1)S(1)}, u32[]{:S(2)}, u32[]{:S(2)}) collective-permute-start(bf16[8,128,128]{2,1,0:T(8,128)(2,1)S(1)} %fusion.54), channel_id=1, source_target_pairs={{0,16},{4,20},{8,24},{12,28},{16,32},{20,36},{24,40},{28,44},{32,4... | collective-permute-start | bytes 786440 | tf_op jit(solution)/shard_map/ppermute | solution.py:17
  46.7 21.4 %collective-permute-start.4 = (f32[8,128,128]{2,1,0:T(8,128)S(1)}, f32[8,128,128]{2,1,0:T(8,128)S(1)}, u32[]{:S(2)}, u32[]{:S(2)}) collective-permute-start(f32[8,128,128]{2,1,0:T(8,128)S(1)} %multiply_add_fusion.5), channel_id=1, source_target_pairs={{0,32},{4,36},{8,40},{12,44},{16,48},{20,52},{24,56},{28,60},{32,6... | collective-permute-start | bytes 1572872 | tf_op jit(solution)/shard_map/ppermute | solution.py:17
  58.5 9.6 %copy-start.9 = (f32[8,128]{1,0:T(8,128)S(1)}, f32[8,128]{1,0:T(8,128)}, u32[]{:S(2)}) copy-start(f32[8,128]{1,0:T(8,128)} %param.9) | copy-start | bytes 12292
  59.5 22.8 %collective-permute-start.5 = (bf16[2,128,8,128]{3,1,2,0:T(8,128)(2,1)}, bf16[2,128,8,128]{3,1,2,0:T(8,128)(2,1)}, u32[]{:S(2)}, u32[]{:S(2)}) collective-permute-start(bf16[2,128,8,128]{3,1,2,0:T(8,128)(2,1)} %pad_maximum_fusion.1), channel_id=1, source_target_pairs={{4,0},{8,4},{12,8},{16,12},{20,16},{24,20},{28,24},{32,28},{36,32}... | collective-permute-start | bytes 1572872 | tf_op jit(solution)/shard_map/ppermute | solution.py:17
  64.3 21.8 %collective-permute-start.6 = (bf16[2,128,8,128]{3,1,2,0:T(8,128)(2,1)}, bf16[2,128,8,128]{3,1,2,0:T(8,128)(2,1)}, u32[]{:S(2)}, u32[]{:S(2)}) collective-permute-start(bf16[2,128,8,128]{3,1,2,0:T(8,128)(2,1)} %pad_maximum_fusion.2), channel_id=1, source_target_pairs={{8,0},{12,4},{16,8},{20,12},{24,16},{28,20},{32,24},{36,28},{40,32... | collective-permute-start | bytes 1572872 | tf_op jit(solution)/shard_map/ppermute | solution.py:17
  68.1 1.4 copy-start.6
  68.1 8.0 %copy-start.4 = (f32[128,8,128]{2,0,1:T(8,128)S(1)}, f32[128,8,128]{2,0,1:T(8,128)}, u32[]{:S(2)}) copy-start(f32[128,8,128]{2,0,1:T(8,128)} %get-tuple-element.82) | copy-start | bytes 1572868
  77.8 14.5 %copy-start.5 = (f32[8,128,128]{1,2,0:T(8,128)S(1)}, f32[8,128,128]{1,2,0:T(8,128)}, u32[]{:S(2)}) copy-start(f32[8,128,128]{1,2,0:T(8,128)} %fusion.63) | copy-start | bytes 1572868
  86.1 9.8 %collective-permute-start.7 = (bf16[8,128,128]{2,1,0:T(8,128)(2,1)S(1)}, bf16[8,128,128]{2,1,0:T(8,128)(2,1)S(1)}, u32[]{:S(2)}, u32[]{:S(2)}) collective-permute-start(bf16[8,128,128]{2,1,0:T(8,128)(2,1)S(1)} %convert_element_type.220), channel_id=1, source_target_pairs={{4,0},{8,4},{12,8},{16,12},{20,16},{24,20},{28,24},{32,28},{36,32}... | collective-permute-start | bytes 786440 | tf_op jit(solution)/shard_map/ppermute | solution.py:17
  96.0 11.6 %collective-permute-start.8 = (bf16[8,128,128]{2,1,0:T(8,128)(2,1)S(1)}, bf16[8,128,128]{2,1,0:T(8,128)(2,1)S(1)}, u32[]{:S(2)}, u32[]{:S(2)}) collective-permute-start(bf16[8,128,128]{2,1,0:T(8,128)(2,1)S(1)} %fusion.55), channel_id=1, source_target_pairs={{8,0},{12,4},{16,8},{20,12},{24,16},{28,20},{32,24},{36,28},{40,32... | collective-permute-start | bytes 786440 | tf_op jit(solution)/shard_map/ppermute | solution.py:17
  107.6 2.2 %copy-start.7 = (f32[8,128,128]{2,1,0:T(8,128)S(1)}, f32[8,128,128]{2,1,0:T(8,128)}, u32[]{:S(2)}) copy-start(f32[8,128,128]{2,1,0:T(8,128)} %copy-done.6) | copy-start | bytes 1572868
  107.7 11.2 %collective-permute-start.9 = (bf16[8,128,128]{2,1,0:T(8,128)(2,1)S(1)}, bf16[8,128,128]{2,1,0:T(8,128)(2,1)S(1)}, u32[]{:S(2)}, u32[]{:S(2)}) collective-permute-start(bf16[8,128,128]{2,1,0:T(8,128)(2,1)S(1)} %fusion.70), channel_id=1, source_target_pairs={{16,0},{20,4},{24,8},{28,12},{32,16},{36,20},{40,24},{44,28},{48,3... | collective-permute-start | bytes 786440 | tf_op jit(solution)/shard_map/ppermute | solution.py:17
  118.9 6.2 %copy-start.8 = (bf16[8,128,128]{1,2,0:T(8,128)(2,1)S(1)}, bf16[8,128,128]{1,2,0:T(8,128)(2,1)}, u32[]{:S(2)}) copy-start(bf16[8,128,128]{1,2,0:T(8,128)(2,1)} %fusion.35) | copy-start | bytes 786436
  119.1 16.8 %collective-permute-start.10 = (f32[8,128,128]{2,1,0:T(8,128)S(1)}, f32[8,128,128]{2,1,0:T(8,128)S(1)}, u32[]{:S(2)}, u32[]{:S(2)}) collective-permute-start(f32[8,128,128]{2,1,0:T(8,128)S(1)} %multiply_add_fusion.1), channel_id=1, source_target_pairs={{4,0},{8,4},{12,8},{16,12},{20,16},{24,20},{28,24},{32,28},{36,32}... | collective-permute-start | bytes 1572872 | tf_op jit(solution)/shard_map/ppermute | solution.py:17
  123.0 29.6 %collective-permute-start.11 = (f32[8,128,128]{2,1,0:T(8,128)S(1)}, f32[8,128,128]{2,1,0:T(8,128)S(1)}, u32[]{:S(2)}, u32[]{:S(2)}) collective-permute-start(f32[8,128,128]{2,1,0:T(8,128)S(1)} %multiply_add_fusion.1), channel_id=1, source_target_pairs={{36,0},{40,4},{44,8},{48,12},{52,16},{56,20},{60,24},{64,28},{68,3... | collective-permute-start | bytes 1572872 | tf_op jit(solution)/shard_map/ppermute | solution.py:17

commit v7 on v5

--- a/solution.py
+++ b/solution.py
@@ -90,6 +90,8 @@
     prev_doc = one_doc(doc_lengths, base - 1)
     next_doc = one_doc(doc_lengths, base + tile)
     pair = jnp.stack([keys, values])
+    asks = jnp.stack([queries, cotangent])
+    later_asks = [from_behind(asks, "ctx", -shift) for shift in range(1, SPAN + 1)]
     arrived = [from_behind(pair, "ctx", shift) for shift in range(SPAN, 0, -1)]
     key_tiles = [piece[0] for piece in arrived] + [keys]
     value_tiles = [piece[1] for piece in arrived] + [values]
@@ -135,13 +137,11 @@
         dscores = (prob_list[position] * (dprobs - row_dot[..., None])).astype(jnp.bfloat16)
         query_soft = query_soft + narrow("htu,uhd->thd", dscores, key_tiles[position]) * scale
         dscore_list.append(dscores)
-    parts = [
-        key_terms(dscore_list[position], weight_list[position], queries, cotangent, scale)
-        for position in range(SPAN + 1)
-    ]
-    outgoing = [
-        jnp.stack(list(parts[SPAN - shift])).astype(jnp.bfloat16) for shift in range(1, SPAN + 1)
-    ]
+    key_soft, value_soft = key_terms(
+        dscore_list[SPAN], weight_list[SPAN], queries, cotangent, scale
+    )
+    stats = jnp.stack([log_total, row_dot])
+    later_stats = [from_behind(stats, "ctx", -shift) for shift in range(1, SPAN + 1)]
     place = lax.axis_index("ctx")
     need = min(-(-MAXDOC // tile), lax.axis_size("ctx"))
     near_states = [
@@ -152,14 +152,8 @@
     near_spans = [(place - SPAN + position, place - SPAN + position) for position in range(SPAN)]
     incoming = fold_states(near_states, front_flags(doc_lengths, near_spans, tile))
     covered = SPAN
-    returned = None
     while covered < need:
         (flag,) = front_flags(doc_lengths, [(place - covered, place - 1)], tile)
-        if 2 * covered >= need:
-            incoming, outgoing = lax.optimization_barrier((incoming, outgoing))
-            returned = [
-                from_behind(outgoing[shift - 1], "ctx", -shift) for shift in range(1, SPAN + 1)
-            ]
         incoming = incoming + (1.0 - flag) * send_state(incoming, "ctx", covered)
         covered *= 2
     linear_out = (
@@ -184,15 +178,29 @@
     tile_sum = narrow(
         "thd,the->hde", jnp.where(keep_first, queries, jnp.zeros_like(queries)), inner
     )
-    key_soft, value_soft = parts[SPAN]
-    if returned is None:
-        returned = [
-            from_behind(outgoing[shift - 1], "ctx", -shift) for shift in range(1, SPAN + 1)
-        ]
-    tile_sum, returned = lax.optimization_barrier((tile_sum, returned))
-    for moved in returned:
-        key_soft = key_soft + moved[0].astype(jnp.float32)
-        value_soft = value_soft + moved[1].astype(jnp.float32)
+    tile_sum, later_asks, later_stats = lax.optimization_barrier(
+        (tile_sum, later_asks, later_stats)
+    )
+    total_len = lax.axis_size("ctx") * tile
+    for shift in range(1, SPAN + 1):
+        query_t = later_asks[shift - 1][0]
+        grad_t = later_asks[shift - 1][1]
+        lse_t = later_stats[shift - 1][0]
+        dot_t = later_stats[shift - 1][1]
+        query_pos = own_pos + shift * tile
+        query_doc = doc_index(doc_lengths, query_pos)
+        mask = (
+            (query_doc[:, None] == own_doc[None, :])
+            & (own_pos[None, :] <= query_pos[:, None])
+            & (query_pos[:, None] < total_len)
+        )
+        probs = jnp.exp(masked_scores(query_t, keys, mask, scale) - lse_t[..., None])
+        weights = probs.astype(jnp.bfloat16)
+        dprobs = narrow("thd,uhd->htu", grad_t, values)
+        dscores = (probs * (dprobs - dot_t[..., None])).astype(jnp.bfloat16)
+        key_part, value_part = key_terms(dscores, weights, query_t, grad_t, scale)
+        key_soft = key_soft + key_part
+        value_soft = value_soft + value_part
     part = tile_sum
     covered = 1
     while 2 * covered < need:

time: 142 us -> 172 us (1.21)
  matrix products: 12.8 us -> 27.4 us
  local copies, waits for them, and re-layouts: 12.4 us -> 19.5 us
  other arithmetic: 6.39 us -> 11.6 us
  starting transfers between devices: 40.7 us -> 45.7 us
  waiting for transfers between devices: 48.6 us -> 46 us
    dot_general x26, matrix products: 10.5 us -> 25.2 us  [narrow(): return jnp.einsum(form, left, right, preferred_element_type=jnp.float32)]
    ppermute x12 -> x14, starting transfers between devices: 40.7 us -> 45.7 us  [from_behind(): return lax.ppermute(x, axis, pairs)]
    unnamed x22 -> x59, local copies, waits for them, and re-layouts: 5.14 us -> 9.38 us
    ppermute x12 -> x14, waiting for transfers between devices: 48.6 us -> 46 us  [from_behind(): return lax.ppermute(x, axis, pairs)]
    convert_element_type x1, other arithmetic: 0.25 us -> 2 us  [per_device(): inner = (inverse[:, None, None] * weighted - linear_out * (inverse ** 3 *...]
  transfers between devices with their start and end apart: 12 -> 14, of which waited for: 9 -> 8; matrix products, arithmetic and copies ran while one was open for 15% -> 26% of each run, Pallas kernels for 0% -> 0%
where the time goes in v7:
time: 172 us; the launch traced here: 171 us
  waiting for transfers between devices  46 us (27%)
  starting transfers between devices  45.7 us (27%)
  matrix products  27.4 us (16%)
  local copies, waits for them, and re-layouts  19.5 us (11%)
  between operations  11.9 us (7%)
  other arithmetic  11.6 us (7%)
  blocking collectives  8.73 us (5%)
    ppermute x14, waiting for transfers between devices, from_behind(): return lax.ppermute(x, axis, pairs)  46 us
    ppermute x14, starting transfers between devices, from_behind(): return lax.ppermute(x, axis, pairs)  45.7 us
    dot_general x26, matrix products, narrow(): return jnp.einsum(form, left, right, preferred_element_type=jnp.float32)  25.2 us
    unnamed x59, local copies, waits for them, and re-layouts  9.38 us
    psum x1, blocking collectives, per_device(): squares = lax.psum(jnp.sum(linear_out * linear_out, axis=(1, 2)), 'head')  8.73 us
  transfers between devices with their start and end apart: 14, of which 8 were waited for; matrix products, arithmetic and copies ran while one was open for 26% of the time, Pallas kernels for 0%

profile of v7, /device:TPU:103, one launch (start us, length us, event | category | flops | bytes accessed | tf_op | source)
XLA Modules:
  0.0 170.8 jit_solution(14894607655779315375)
XLA Ops:
  0.6 1.1 copy_bitcast_fusion.1
  1.8 0.9 pad_maximum_fusion
  2.6 4.7 %collective-permute-start.1 = (bf16[2,128,8,128]{3,1,2,0:T(8,128)(2,1)}, bf16[2,128,8,128]{3,1,2,0:T(8,128)(2,1)S(1)}, u32[]{:S(2)}, u32[]{:S(2)}) collective-permute-start(bf16[2,128,8,128]{3,1,2,0:T(8,128)(2,1)} %pad_maximum_fusion), channel_id=1, source_target_pairs={{0,8},{4,12},{8,16},{12,20},{16,24},{20,28},{24,32},{28,36},{32,40... | collective-permute-start | bytes 1572872 | tf_op jit(solution)/shard_map/ppermute | solution.py:17
  7.3 4.0 %collective-permute-start = (bf16[2,128,8,128]{3,1,2,0:T(8,128)(2,1)}, bf16[2,128,8,128]{3,1,2,0:T(8,128)(2,1)S(1)}, u32[]{:S(2)}, u32[]{:S(2)}) collective-permute-start(bf16[2,128,8,128]{3,1,2,0:T(8,128)(2,1)} %pad_maximum_fusion), channel_id=1, source_target_pairs={{0,4},{4,8},{8,12},{12,16},{16,20},{20,24},{24,28},{28,32},{32,36}... | collective-permute-start | bytes 1572872 | tf_op jit(solution)/shard_map/ppermute | solution.py:17
  11.4 0.9 pad_maximum_fusion.1
  12.3 1.9 %collective-permute-start.5 = (bf16[2,128,8,128]{3,1,2,0:T(8,128)(2,1)}, bf16[2,128,8,128]{3,1,2,0:T(8,128)(2,1)}, u32[]{:S(2)}, u32[]{:S(2)}) collective-permute-start(bf16[2,128,8,128]{3,1,2,0:T(8,128)(2,1)} %pad_maximum_fusion.1), channel_id=1, source_target_pairs={{4,0},{8,4},{12,8},{16,12},{20,16},{24,20},{28,24},{32,28},{36,32}... | collective-permute-start | bytes 1572872 | tf_op jit(solution)/shard_map/ppermute | solution.py:17
  14.2 2.2 %collective-permute-start.6 = (bf16[2,128,8,128]{3,1,2,0:T(8,128)(2,1)}, bf16[2,128,8,128]{3,1,2,0:T(8,128)(2,1)}, u32[]{:S(2)}, u32[]{:S(2)}) collective-permute-start(bf16[2,128,8,128]{3,1,2,0:T(8,128)(2,1)} %pad_maximum_fusion.1), channel_id=1, source_target_pairs={{8,0},{12,4},{16,8},{20,12},{24,16},{28,20},{32,24},{36,28},{40,32... | collective-permute-start | bytes 1572872 | tf_op jit(solution)/shard_map/ppermute | solution.py:17
  16.4 0.6 copy-done.23
  17.4 0.6 fusion.158
  19.1 1.1 broadcast_compare_fusion.3
  20.8 1.1 broadcast_compare_fusion.4
  22.6 0.7 fusion.177
  25.1 0.6 fusion.175
  25.8 0.6 fusion.174
  26.9 0.7 and_and_fusion
  28.3 0.6 fusion.172
  29.5 0.9 copy.189
  41.1 1.1 fusion.31
  42.3 1.2 copy.182
  45.0 6.4 %collective-permute-start.2 = (bf16[8,128,128]{2,1,0:T(8,128)(2,1)S(1)}, bf16[8,128,128]{2,1,0:T(8,128)(2,1)S(1)}, u32[]{:S(2)}, u32[]{:S(2)}) collective-permute-start(bf16[8,128,128]{2,1,0:T(8,128)(2,1)S(1)} %get-tuple-element.82), channel_id=1, source_target_pairs={{0,8},{4,12},{8,16},{12,20},{16,24},{20,28},{24,32},{28,36},{32,40... | collective-permute-start | bytes 786440 | tf_op jit(solution)/shard_map/ppermute | solution.py:17
  51.9 4.3 %collective-permute-done.2 = bf16[8,128,128]{2,1,0:T(8,128)(2,1)S(1)} collective-permute-done((bf16[8,128,128]{2,1,0:T(8,128)(2,1)S(1)}, bf16[8,128,128]{2,1,0:T(8,128)(2,1)S(1)}, u32[]{:S(2)}, u32[]{:S(2)}) %collective-permute-start.2) | collective-permute-done | bytes 262176 | tf_op jit(solution)/shard_map/ppermute | solution.py:17
  56.3 2.6 %collective-permute-start.3 = (bf16[8,128,128]{2,1,0:T(8,128)(2,1)S(1)}, bf16[8,128,128]{2,1,0:T(8,128)(2,1)S(1)}, u32[]{:S(2)}, u32[]{:S(2)}) collective-permute-start(bf16[8,128,128]{2,1,0:T(8,128)(2,1)S(1)} %fusion.61), channel_id=1, source_target_pairs={{0,16},{4,20},{8,24},{12,28},{16,32},{20,36},{24,40},{28,44},{32,4... | collective-permute-start | bytes 786440 | tf_op jit(solution)/shard_map/ppermute | solution.py:17
  59.5 6.2 %collective-permute-done.3 = bf16[8,128,128]{2,1,0:T(8,128)(2,1)S(1)} collective-permute-done((bf16[8,128,128]{2,1,0:T(8,128)(2,1)S(1)}, bf16[8,128,128]{2,1,0:T(8,128)(2,1)S(1)}, u32[]{:S(2)}, u32[]{:S(2)}) %collective-permute-start.3) | collective-permute-done | bytes 262176 | tf_op jit(solution)/shard_map/ppermute | solution.py:17
  65.9 1.9 %collective-permute-start.4 = (bf16[8,128,128]{2,1,0:T(8,128)(2,1)S(1)}, bf16[8,128,128]{2,1,0:T(8,128)(2,1)S(1)}, u32[]{:S(2)}, u32[]{:S(2)}) collective-permute-start(bf16[8,128,128]{2,1,0:T(8,128)(2,1)S(1)} %get-tuple-element.49), channel_id=1, source_target_pairs={{0,32},{4,36},{8,40},{12,44},{16,48},{20,52},{24,56},{28,60},{32,6... | collective-permute-start | bytes 786440 | tf_op jit(solution)/shard_map/ppermute | solution.py:17
  68.1 4.9 %collective-permute-done.4 = bf16[8,128,128]{2,1,0:T(8,128)(2,1)S(1)} collective-permute-done((bf16[8,128,128]{2,1,0:T(8,128)(2,1)S(1)}, bf16[8,128,128]{2,1,0:T(8,128)(2,1)S(1)}, u32[]{:S(2)}, u32[]{:S(2)}) %collective-permute-start.4) | collective-permute-done | bytes 262176 | tf_op jit(solution)/shard_map/ppermute | solution.py:17
  73.0 0.6 fusion.38
  74.1 1.2 fusion.53
  75.9 5.7 %collective-permute-start.7 = (f32[2,8,128]{2,1,0:T(8,128)}, f32[2,8,128]{2,1,0:T(8,128)}, u32[]{:S(2)}, u32[]{:S(2)}) collective-permute-start(f32[2,8,128]{2,1,0:T(8,128)} %pad_maximum_fusion.2), channel_id=1, source_target_pairs={{4,0},{8,4},{12,8},{16,12},{20,16},{24,20},{28,24},{32,28},{36,32}... | collective-permute-start | bytes 24584 | tf_op jit(solution)/shard_map/ppermute | solution.py:17
  81.5 4.3 %collective-permute-start.8 = (f32[2,8,128]{2,1,0:T(8,128)}, f32[2,8,128]{2,1,0:T(8,128)}, u32[]{:S(2)}, u32[]{:S(2)}) collective-permute-start(f32[2,8,128]{2,1,0:T(8,128)} %pad_maximum_fusion.2), channel_id=1, source_target_pairs={{8,0},{12,4},{16,8},{20,12},{24,16},{28,20},{32,24},{36,28},{40,32... | collective-permute-start | bytes 24584 | tf_op jit(solution)/shard_map/ppermute | solution.py:17
  85.9 8.7 %all-reduce = (f32[128]{0:T(128)S(1)}, f32[128]{0:T(128)S(1)}) all-reduce(f32[128]{0:T(128)S(1)} %get-tuple-element.27, f32[128]{0:T(128)S(1)} %get-tuple-element.26), channel_id=1, replica_groups=mesh['ctx'=64,'head'=4] {'head'}, use_global_device_ids=true, to_apply=%region_10.11 | all-reduce | flops 256 | bytes 2048 | tf_op jit(solution)/shard_map/psum | solution.py:163
  94.6 2.0 %fusion.52 = (bf16[128,8,128]{0,2,1:T(8,128)(2,1)S(1)}, bf16[128,8,128]{0,2,1:T(8,128)(2,1)}) fusion(bf16[128,8,128]{0,2,1:T(8,128)(2,1)S(1)} %copy-done.9, f32[128,8,128]{0,2,1:T(8,128)} %get-tuple-element.86, f32[128]{0:T(128)S(1)} %get-tuple-element.74, f32[8,128]{1,0:T(8,128)S(1)} %copy-done.19, f32[128]{0:T(128)S(1)} %get-tuple-element.75, ...), kind=kLoop, calls=%fused_computation.83 | loop fusion | flops 1310720 | bytes 1840128 | tf_op jit(solution)/shard_map/convert_element_type | solution.py:171
  96.8 1.1 fusion.132
  97.9 1.0 fusion.43
  99.0 0.6 copy-done.24
  100.0 2.3 %fusion.48 = f32[8,128,128]{2,1,0:T(8,128)} fusion(f32[8,128,128]{1,2,0:T(8,128)S(1)} %copy.182, f32[8,128]{1,0:T(8,128)S(1)} %bitcast.192, f32[8,128]{1,0:T(8,128)S(1)} %log_add_fusion, pred[128,128]{0,1:T(8,128)(4,1)S(1)} %get-tuple-element.59, bf16[2,128,8,128]{3,1,2,0:T(8,128)(2,1)} %copy-done.4, bf16[128,8,128]{2,1,0:T(8,128)(2,1)S(1)} %copy-done.2), kind=kOutput, calls=%fused_computation.77 | convolution fusion | flops 67764224 | bytes 1859584 | tf_op jit(solution)/shard_map/htu,uhd->thd/dot_general | solution.py:59
  102.3 2.5 %fusion.26 = f32[128,8,128]{0,2,1:T(8,128)} fusion(f32[8,128,128]{2,1,0:T(8,128)} %fusion.48, f32[8,128,128]{1,2,0:T(8,128)S(1)} %copy.179, f32[8,128]{1,0:T(8,128)S(1)} %bitcast.193, f32[8,128]{1,0:T(8,128)S(1)} %log_add_fusion, pred[128,128]{0,1:T(8,128)(4,1)S(1)} %get-tuple-element.60, bf16[2,128,8,128]{3,1,2,0:T(8,128)(2,1)} %copy-done.3, ...), kind=kOutput, calls=%fused_computation.45 | convolution fusion | flops 68026368 | bytes 2383872 | tf_op jit(solution)/shard_map/htu,uhd->thd/dot_general | solution.py:59
  104.8 1.5 fusion.21
  106.8 1.0 convolution_bitcast_fusion.5
  108.1 0.7 copy-done.18
  109.0 0.7 copy-done.15
  109.7 0.9 copy.246
  110.6 0.9 copy.247
  111.5 4.2 %collective-permute-start.9 = (bf16[8,128,128]{2,1,0:T(8,128)(2,1)S(1)}, bf16[8,128,128]{2,1,0:T(8,128)(2,1)S(1)}, u32[]{:S(2)}, u32[]{:S(2)}) collective-permute-start(bf16[8,128,128]{2,1,0:T(8,128)(2,1)S(1)} %convert_element_type.230), channel_id=1, source_target_pairs={{4,0},{8,4},{12,8},{16,12},{20,16},{24,20},{28,24},{32,28},{36,32}... | collective-permute-start | bytes 786440 | tf_op jit(solution)/shard_map/ppermute | solution.py:17
  115.8 0.7 slice_bitcast_fusion.20
  116.5 1.3 fusion.18
  117.7 8.1 %collective-permute-done.9 = bf16[8,128,128]{2,1,0:T(8,128)(2,1)S(1)} collective-permute-done((bf16[8,128,128]{2,1,0:T(8,128)(2,1)S(1)}, bf16[8,128,128]{2,1,0:T(8,128)(2,1)S(1)}, u32[]{:S(2)}, u32[]{:S(2)}) %collective-permute-start.9) | collective-permute-done | bytes 262176 | tf_op jit(solution)/shard_map/ppermute | solution.py:17
  125.9 0.8 fusion.62
  126.6 1.9 %collective-permute-start.10 = (bf16[8,128,128]{2,1,0:T(8,128)(2,1)}, bf16[8,128,128]{2,1,0:T(8,128)(2,1)S(1)}, u32[]{:S(2)}, u32[]{:S(2)}) collective-permute-start(bf16[8,128,128]{2,1,0:T(8,128)(2,1)} %fusion.62), channel_id=1, source_target_pairs={{8,0},{12,4},{16,8},{20,12},{24,16},{28,20},{32,24},{36,28},{40,32... | collective-permute-start | bytes 786440 | tf_op jit(solution)/shard_map/ppermute | solution.py:17
  128.6 2.3 %fusion.10 = f32[128,8,128]{2,0,1:T(8,128)} fusion(f32[128,8,128]{2,0,1:T(8,128)S(1)} %fusion.19, f32[8,128,128]{1,2,0:T(8,128)S(1)} %fusion.18, f32[8,128]{1,0:T(8,128)S(1)} %get-tuple-element.55, bf16[2,128,8,128]{3,1,2,0:T(8,128)(2,1)} %collective-permute-done.5, bf16[128,8,128]{2,1,0:T(8,128)(2,1)S(1)} %copy-done), kind=kOutput, calls=%fused_computation.19 | convolution fusion | flops 67764224 | bytes 2363392 | tf_op jit(solution)/shard_map/htu,thd->uhd/dot_general | solution.py:59
  130.9 6.4 %collective-permute-done.10 = bf16[8,128,128]{2,1,0:T(8,128)(2,1)S(1)} collective-permute-done((bf16[8,128,128]{2,1,0:T(8,128)(2,1)}, bf16[8,128,128]{2,1,0:T(8,128)(2,1)S(1)}, u32[]{:S(2)}, u32[]{:S(2)}) %collective-permute-start.10) | collective-permute-done | bytes 262176 | tf_op jit(solution)/shard_map/ppermute | solution.py:17
  137.4 2.1 %collective-permute-start.11 = (bf16[8,128,128]{2,1,0:T(8,128)(2,1)S(1)}, bf16[8,128,128]{2,1,0:T(8,128)(2,1)S(1)}, u32[]{:S(2)}, u32[]{:S(2)}) collective-permute-start(bf16[8,128,128]{2,1,0:T(8,128)(2,1)S(1)} %fusion.121), channel_id=1, source_target_pairs={{16,0},{20,4},{24,8},{28,12},{32,16},{36,20},{40,24},{44,28},{48,3... | collective-permute-start | bytes 786440 | tf_op jit(solution)/shard_map/ppermute | solution.py:17
  139.5 0.7 slice_bitcast_fusion.18
  140.2 1.2 convolution_bitcast_fusion.1
  141.3 6.9 %collective-permute-done.11 = bf16[8,128,128]{2,1,0:T(8,128)(2,1)S(1)} collective-permute-done((bf16[8,128,128]{2,1,0:T(8,128)(2,1)S(1)}, bf16[8,128,128]{2,1,0:T(8,128)(2,1)S(1)}, u32[]{:S(2)}, u32[]{:S(2)}) %collective-permute-start.11) | collective-permute-done | bytes 262176 | tf_op jit(solution)/shard_map/ppermute | solution.py:17
  148.5 1.9 %collective-permute-start.13 = (bf16[8,128,128]{2,1,0:T(8,128)(2,1)S(1)}, bf16[8,128,128]{2,1,0:T(8,128)(2,1)S(1)}, u32[]{:S(2)}, u32[]{:S(2)}) collective-permute-start(bf16[8,128,128]{2,1,0:T(8,128)(2,1)S(1)} %add_convert_fusion), channel_id=1, source_target_pairs={{36,0},{40,4},{44,8},{48,12},{52,16},{56,20},{60,24},{64,28},{68,3... | collective-permute-start | bytes 786440 | tf_op jit(solution)/shard_map/ppermute | solution.py:17
  150.4 1.9 %collective-permute-start.12 = (bf16[8,128,128]{2,1,0:T(8,128)(2,1)S(1)}, bf16[8,128,128]{2,1,0:T(8,128)(2,1)S(1)}, u32[]{:S(2)}, u32[]{:S(2)}) collective-permute-start(bf16[8,128,128]{2,1,0:T(8,128)(2,1)S(1)} %add_convert_fusion), channel_id=1, source_target_pairs={{4,0},{8,4},{12,8},{16,12},{20,16},{24,20},{28,24},{32,28},{36,32}... | collective-permute-start | bytes 786440 | tf_op jit(solution)/shard_map/ppermute | solution.py:17
  152.3 1.3 fusion.14
  153.6 1.4 convolution_bitcast_fusion
  155.0 7.9 %collective-permute-done.13 = bf16[8,128,128]{2,1,0:T(8,128)(2,1)S(1)} collective-permute-done((bf16[8,128,128]{2,1,0:T(8,128)(2,1)S(1)}, bf16[8,128,128]{2,1,0:T(8,128)(2,1)S(1)}, u32[]{:S(2)}, u32[]{:S(2)}) %collective-permute-start.13) | collective-permute-done | bytes 262176 | tf_op jit(solution)/shard_map/ppermute | solution.py:17
  162.9 1.2 collective-permute-done.12
  164.1 0.7 fusion.36
  164.8 2.5 %fusion.39 = bf16[128,8,128]{2,0,1:T(8,128)(2,1)} fusion(f32[128,8,128]{2,0,1:T(8,128)S(1)} %fusion.36, f32[128,8,128]{2,0,1:T(8,128)} %fusion.10, f32[8,128,128]{1,2,0:T(8,128)} %copy-done.12, f32[8,128]{1,0:T(8,128)S(1)} %get-tuple-element.53, bf16[2,128,8,128]{3,1,2,0:T(8,128)(2,1)} %collective-permute-done.6, bf16[128,8,128]{2,1,0:T(8,128)(2,1)S(1)} %copy-done), kind=kOutput, calls=%fused_computation.68 | convolution fusion | flops 68026368 | bytes 2625536 | tf_op jit(solution)/shard_map/htu,thd->uhd/dot_general | solution.py:59
  167.3 1.9 %copy.248 = bf16[128,8,128]{2,1,0:T(8,128)(2,1)} copy(bf16[128,8,128]{2,0,1:T(8,128)(2,1)} %fusion.39) | data formatting | bytes 524288
  169.9 0.9 copy.249
  (120 shorter events, 13.1 us)
Async XLA Ops:
  1.8 9.5 %copy-start.1 = (bf16[128,8,128]{2,1,0:T(8,128)(2,1)S(1)}, bf16[128,8,128]{2,1,0:T(8,128)(2,1)}, u32[]{:S(2)}) copy-start(bf16[128,8,128]{2,1,0:T(8,128)(2,1)} %param.6) | copy-start | bytes 786436
  1.8 9.5 %copy-start.2 = (bf16[128,8,128]{2,1,0:T(8,128)(2,1)S(1)}, bf16[128,8,128]{2,1,0:T(8,128)(2,1)}, u32[]{:S(2)}) copy-start(bf16[128,8,128]{2,1,0:T(8,128)(2,1)} %param.11) | copy-start | bytes 786436
  2.6 38.0 %collective-permute-start.1 = (bf16[2,128,8,128]{3,1,2,0:T(8,128)(2,1)}, bf16[2,128,8,128]{3,1,2,0:T(8,128)(2,1)S(1)}, u32[]{:S(2)}, u32[]{:S(2)}) collective-permute-start(bf16[2,128,8,128]{3,1,2,0:T(8,128)(2,1)} %pad_maximum_fusion), channel_id=1, source_target_pairs={{0,8},{4,12},{8,16},{12,20},{16,24},{20,28},{24,32},{28,36},{32,40... | collective-permute-start | bytes 1572872 | tf_op jit(solution)/shard_map/ppermute | solution.py:17
  7.3 33.8 %collective-permute-start = (bf16[2,128,8,128]{3,1,2,0:T(8,128)(2,1)}, bf16[2,128,8,128]{3,1,2,0:T(8,128)(2,1)S(1)}, u32[]{:S(2)}, u32[]{:S(2)}) collective-permute-start(bf16[2,128,8,128]{3,1,2,0:T(8,128)(2,1)} %pad_maximum_fusion), channel_id=1, source_target_pairs={{0,4},{4,8},{8,12},{12,16},{16,20},{20,24},{24,28},{28,32},{32,36}... | collective-permute-start | bytes 1572872 | tf_op jit(solution)/shard_map/ppermute | solution.py:17
  12.3 99.2 %collective-permute-start.5 = (bf16[2,128,8,128]{3,1,2,0:T(8,128)(2,1)}, bf16[2,128,8,128]{3,1,2,0:T(8,128)(2,1)}, u32[]{:S(2)}, u32[]{:S(2)}) collective-permute-start(bf16[2,128,8,128]{3,1,2,0:T(8,128)(2,1)} %pad_maximum_fusion.1), channel_id=1, source_target_pairs={{4,0},{8,4},{12,8},{16,12},{20,16},{24,20},{28,24},{32,28},{36,32}... | collective-permute-start | bytes 1572872 | tf_op jit(solution)/shard_map/ppermute | solution.py:17
  14.2 97.3 %collective-permute-start.6 = (bf16[2,128,8,128]{3,1,2,0:T(8,128)(2,1)}, bf16[2,128,8,128]{3,1,2,0:T(8,128)(2,1)}, u32[]{:S(2)}, u32[]{:S(2)}) collective-permute-start(bf16[2,128,8,128]{3,1,2,0:T(8,128)(2,1)} %pad_maximum_fusion.1), channel_id=1, source_target_pairs={{8,0},{12,4},{16,8},{20,12},{24,16},{28,20},{32,24},{36,28},{40,32... | collective-permute-start | bytes 1572872 | tf_op jit(solution)/shard_map/ppermute | solution.py:17
  16.4 0.7 copy-start.23
  26.9 46.1 %copy-start.21 = (f32[128]{0:T(128)}, f32[128]{0:T(128)S(1)}, u32[]{:S(2)}) copy-start(f32[128]{0:T(128)S(1)} %get-tuple-element.66) | copy-start | bytes 1540
  29.5 10.8 %copy-start.7 = (bf16[128,8,128]{2,1,0:T(8,128)(2,1)S(1)}, bf16[128,8,128]{2,1,0:T(8,128)(2,1)}, u32[]{:S(2)}) copy-start(bf16[128,8,128]{2,1,0:T(8,128)(2,1)} %param.7) | copy-start | bytes 786436
  40.6 27.2 %copy-start.3 = (bf16[2,128,8,128]{3,1,2,0:T(8,128)(2,1)}, bf16[2,128,8,128]{3,1,2,0:T(8,128)(2,1)S(1)}, u32[]{:S(2)}) copy-start(bf16[2,128,8,128]{3,1,2,0:T(8,128)(2,1)S(1)} %collective-permute-done.1) | copy-start | bytes 1572868
  41.1 18.1 %copy-start.4 = (bf16[2,128,8,128]{3,1,2,0:T(8,128)(2,1)}, bf16[2,128,8,128]{3,1,2,0:T(8,128)(2,1)S(1)}, u32[]{:S(2)}) copy-start(bf16[2,128,8,128]{3,1,2,0:T(8,128)(2,1)S(1)} %collective-permute-done) | copy-start | bytes 1572868
  43.5 0.6 copy-start.25
  44.1 0.6 copy-start.26
  45.0 11.2 %collective-permute-start.2 = (bf16[8,128,128]{2,1,0:T(8,128)(2,1)S(1)}, bf16[8,128,128]{2,1,0:T(8,128)(2,1)S(1)}, u32[]{:S(2)}, u32[]{:S(2)}) collective-permute-start(bf16[8,128,128]{2,1,0:T(8,128)(2,1)S(1)} %get-tuple-element.82), channel_id=1, source_target_pairs={{0,8},{4,12},{8,16},{12,20},{16,24},{20,28},{24,32},{28,36},{32,40... | collective-permute-start | bytes 786440 | tf_op jit(solution)/shard_map/ppermute | solution.py:17
  56.2 2.7 %copy-start = (bf16[128,8,128]{2,1,0:T(8,128)(2,1)S(1)}, bf16[128,8,128]{2,1,0:T(8,128)(2,1)}, u32[]{:S(2)}) copy-start(bf16[128,8,128]{2,1,0:T(8,128)(2,1)} %param.8) | copy-start | bytes 786436
  56.3 9.5 %collective-permute-start.3 = (bf16[8,128,128]{2,1,0:T(8,128)(2,1)S(1)}, bf16[8,128,128]{2,1,0:T(8,128)(2,1)S(1)}, u32[]{:S(2)}, u32[]{:S(2)}) collective-permute-start(bf16[8,128,128]{2,1,0:T(8,128)(2,1)S(1)} %fusion.61), channel_id=1, source_target_pairs={{0,16},{4,20},{8,24},{12,28},{16,32},{20,36},{24,40},{28,44},{32,4... | collective-permute-start | bytes 786440 | tf_op jit(solution)/shard_map/ppermute | solution.py:17
  65.9 7.1 %copy-start.5 = (f32[8,128,128]{2,1,0:T(8,128)}, f32[8,128,128]{2,1,0:T(8,128)S(1)}, u32[]{:S(2)}) copy-start(f32[8,128,128]{2,1,0:T(8,128)S(1)} %get-tuple-element.50) | copy-start | bytes 1572868
  65.9 7.1 %collective-permute-start.4 = (bf16[8,128,128]{2,1,0:T(8,128)(2,1)S(1)}, bf16[8,128,128]{2,1,0:T(8,128)(2,1)S(1)}, u32[]{:S(2)}, u32[]{:S(2)}) collective-permute-start(bf16[8,128,128]{2,1,0:T(8,128)(2,1)S(1)} %get-tuple-element.49), channel_id=1, source_target_pairs={{0,32},{4,36},{8,40},{12,44},{16,48},{20,52},{24,56},{28,60},{32,6... | collective-permute-start | bytes 786440 | tf_op jit(solution)/shard_map/ppermute | solution.py:17
  73.0 0.7 copy-start.16
  73.0 1.0 copy-start.9
  73.0 1.0 copy-start.19
  75.9 35.6 %collective-permute-start.7 = (f32[2,8,128]{2,1,0:T(8,128)}, f32[2,8,128]{2,1,0:T(8,128)}, u32[]{:S(2)}, u32[]{:S(2)}) collective-permute-start(f32[2,8,128]{2,1,0:T(8,128)} %pad_maximum_fusion.2), channel_id=1, source_target_pairs={{4,0},{8,4},{12,8},{16,12},{20,16},{24,20},{28,24},{32,28},{36,32}... | collective-permute-start | bytes 24584 | tf_op jit(solution)/shard_map/ppermute | solution.py:17
  81.5 29.9 %collective-permute-start.8 = (f32[2,8,128]{2,1,0:T(8,128)}, f32[2,8,128]{2,1,0:T(8,128)}, u32[]{:S(2)}, u32[]{:S(2)}) collective-permute-start(f32[2,8,128]{2,1,0:T(8,128)} %pad_maximum_fusion.2), channel_id=1, source_target_pairs={{8,0},{12,4},{16,8},{20,12},{24,16},{28,20},{32,24},{36,28},{40,32... | collective-permute-start | bytes 24584 | tf_op jit(solution)/shard_map/ppermute | solution.py:17
  99.0 0.6 copy-start.24
  102.3 2.5 %copy-start.8 = (bf16[128,8,128]{2,1,0:T(8,128)(2,1)S(1)}, bf16[128,8,128]{2,1,0:T(8,128)(2,1)}, u32[]{:S(2)}) copy-start(bf16[128,8,128]{2,1,0:T(8,128)(2,1)} %param.7) | copy-start | bytes 786436
  104.8 1.5 copy-start.6
  104.8 1.5 copy-start.17
  104.8 1.5 copy-start.22
  107.8 0.9 copy-start.18
  108.7 0.9 copy-start.15
  111.5 4.9 %copy-start.20 = (pred[128,128]{0,1:T(8,128)(4,1)S(1)}, pred[128,128]{0,1:T(8,128)(4,1)}, u32[]{:S(2)}) copy-start(pred[128,128]{0,1:T(8,128)(4,1)} %get-tuple-element.62) | copy-start | bytes 49156
  111.5 14.3 %collective-permute-start.9 = (bf16[8,128,128]{2,1,0:T(8,128)(2,1)S(1)}, bf16[8,128,128]{2,1,0:T(8,128)(2,1)S(1)}, u32[]{:S(2)}, u32[]{:S(2)}) collective-permute-start(bf16[8,128,128]{2,1,0:T(8,128)(2,1)S(1)} %convert_element_type.230), channel_id=1, source_target_pairs={{4,0},{8,4},{12,8},{16,12},{20,16},{24,20},{28,24},{32,28},{36,32}... | collective-permute-start | bytes 786440 | tf_op jit(solution)/shard_map/ppermute | solution.py:17
  117.7 10.8 %copy-start.13 = (f32[8,128,128]{1,2,0:T(8,128)}, f32[8,128,128]{1,2,0:T(8,128)S(1)}, u32[]{:S(2)}) copy-start(f32[8,128,128]{1,2,0:T(8,128)S(1)} %fusion.18) | copy-start | bytes 1572868
  126.6 10.6 %collective-permute-start.10 = (bf16[8,128,128]{2,1,0:T(8,128)(2,1)}, bf16[8,128,128]{2,1,0:T(8,128)(2,1)S(1)}, u32[]{:S(2)}, u32[]{:S(2)}) collective-permute-start(bf16[8,128,128]{2,1,0:T(8,128)(2,1)} %fusion.62), channel_id=1, source_target_pairs={{8,0},{12,4},{16,8},{20,12},{24,16},{28,20},{32,24},{36,28},{40,32... | collective-permute-start | bytes 786440 | tf_op jit(solution)/shard_map/ppermute | solution.py:17
  137.3 2.9 %copy-start.14 = (f32[8,128,128]{1,2,0:T(8,128)S(1)}, f32[8,128,128]{1,2,0:T(8,128)}, u32[]{:S(2)}) copy-start(f32[8,128,128]{1,2,0:T(8,128)} %copy-done.13) | copy-start | bytes 1572868
  137.4 10.9 %collective-permute-start.11 = (bf16[8,128,128]{2,1,0:T(8,128)(2,1)S(1)}, bf16[8,128,128]{2,1,0:T(8,128)(2,1)S(1)}, u32[]{:S(2)}, u32[]{:S(2)}) collective-permute-start(bf16[8,128,128]{2,1,0:T(8,128)(2,1)S(1)} %fusion.121), channel_id=1, source_target_pairs={{16,0},{20,4},{24,8},{28,12},{32,16},{36,20},{40,24},{44,28},{48,3... | collective-permute-start | bytes 786440 | tf_op jit(solution)/shard_map/ppermute | solution.py:17
  148.5 14.4 %collective-permute-start.13 = (bf16[8,128,128]{2,1,0:T(8,128)(2,1)S(1)}, bf16[8,128,128]{2,1,0:T(8,128)(2,1)S(1)}, u32[]{:S(2)}, u32[]{:S(2)}) collective-permute-start(bf16[8,128,128]{2,1,0:T(8,128)(2,1)S(1)} %add_convert_fusion), channel_id=1, source_target_pairs={{36,0},{40,4},{44,8},{48,12},{52,16},{56,20},{60,24},{64,28},{68,3... | collective-permute-start | bytes 786440 | tf_op jit(solution)/shard_map/ppermute | solution.py:17
  150.4 13.7 %collective-permute-start.12 = (bf16[8,128,128]{2,1,0:T(8,128)(2,1)S(1)}, bf16[8,128,128]{2,1,0:T(8,128)(2,1)S(1)}, u32[]{:S(2)}, u32[]{:S(2)}) collective-permute-start(bf16[8,128,128]{2,1,0:T(8,128)(2,1)S(1)} %add_convert_fusion), channel_id=1, source_target_pairs={{4,0},{8,4},{12,8},{16,12},{20,16},{24,20},{28,24},{32,28},{36,32}... | collective-permute-start | bytes 786440 | tf_op jit(solution)/shard_map/ppermute | solution.py:17
  153.6 10.5 %copy-start.12 = (f32[8,128,128]{1,2,0:T(8,128)}, f32[8,128,128]{1,2,0:T(8,128)S(1)}, u32[]{:S(2)}) copy-start(f32[8,128,128]{1,2,0:T(8,128)S(1)} %fusion.14) | copy-start | bytes 1572868
  153.6 10.5 %copy-start.11 = (f32[128,8,128]{2,0,1:T(8,128)S(1)}, f32[128,8,128]{2,0,1:T(8,128)}, u32[]{:S(2)}) copy-start(f32[128,8,128]{2,0,1:T(8,128)} %convolution_bitcast_fusion.5) | copy-start | bytes 1572868
  167.3 1.9 %copy-start.10 = (f32[8,128,128]{1,2,0:T(8,128)S(1)}, f32[8,128,128]{1,2,0:T(8,128)}, u32[]{:S(2)}) copy-start(f32[8,128,128]{1,2,0:T(8,128)} %fusion.132) | copy-start | bytes 1572868

commit v8 on v5

--- a/solution.py
+++ b/solution.py
@@ -189,16 +189,18 @@
         returned = [
             from_behind(outgoing[shift - 1], "ctx", -shift) for shift in range(1, SPAN + 1)
         ]
-    tile_sum, returned = lax.optimization_barrier((tile_sum, returned))
-    for moved in returned:
-        key_soft = key_soft + moved[0].astype(jnp.float32)
-        value_soft = value_soft + moved[1].astype(jnp.float32)
     part = tile_sum
     covered = 1
     while 2 * covered < need:
         (flag,) = back_flags(doc_lengths, [(place, place + covered - 1)], tile)
-        part = part + (1.0 - flag) * send_state(part, "ctx", -covered)
+        received = send_state(part, "ctx", -covered)
+        if covered == 1:
+            received, returned = lax.optimization_barrier((received, returned))
+        part = part + (1.0 - flag) * received
         covered *= 2
+    for moved in returned:
+        key_soft = key_soft + moved[0].astype(jnp.float32)
+        value_soft = value_soft + moved[1].astype(jnp.float32)
     later = send_state(part, "ctx", -1)
     if covered < need:
         (flag,) = back_flags(doc_lengths, [(place + 1, place + covered)], tile)

time: 142 us -> 136 us (0.958)
  waiting for transfers between devices: 48.6 us -> 45.4 us
  starting transfers between devices: 40.7 us -> 37.9 us
    ppermute x12, waiting for transfers between devices: 48.6 us -> 45.4 us  [from_behind(): return lax.ppermute(x, axis, pairs)]
    ppermute x12, starting transfers between devices: 40.7 us -> 37.9 us  [from_behind(): return lax.ppermute(x, axis, pairs)]
  transfers between devices with their start and end apart: 12 -> 12, of which waited for: 9 -> 7; matrix products, arithmetic and copies ran while one was open for 15% -> 15% of each run, Pallas kernels for 0% -> 0%
where the time goes in v8:
time: 136 us
  waiting for transfers between devices  45.4 us (33%)
  starting transfers between devices  37.9 us (28%)
  matrix products  12.8 us (9%)
  local copies, waits for them, and re-layouts  12.4 us (9%)
  between operations  12 us (9%)
  blocking collectives  8.74 us (6%)
  other arithmetic  6.31 us (5%)
    ppermute x12, waiting for transfers between devices, from_behind(): return lax.ppermute(x, axis, pairs)  45.4 us
    ppermute x12, starting transfers between devices, from_behind(): return lax.ppermute(x, axis, pairs)  37.9 us
    dot_general x26, matrix products, narrow(): return jnp.einsum(form, left, right, preferred_element_type=jnp.float32)  10.5 us
    psum x1, blocking collectives, per_device(): squares = lax.psum(jnp.sum(linear_out * linear_out, axis=(1, 2)), 'head')  8.74 us
    unnamed x22, local copies, waits for them, and re-layouts  5.14 us
  transfers between devices with their start and end apart: 12, of which 7 were waited for; matrix products, arithmetic and copies ran while one was open for 15% of the time, Pallas kernels for 0%

profile of v8, /device:TPU:103, one launch (start us, length us, event | category | flops | bytes accessed | tf_op | source)
XLA Modules:
  0.0 135.6 jit_solution(13899424035800755872)
XLA Ops:
  0.6 1.1 copy_bitcast_fusion
  1.8 4.7 %collective-permute-start.1 = (bf16[2,128,8,128]{3,1,2,0:T(8,128)(2,1)S(1)}, bf16[2,128,8,128]{3,1,2,0:T(8,128)(2,1)S(1)}, u32[]{:S(2)}, u32[]{:S(2)}) collective-permute-start(bf16[2,128,8,128]{3,1,2,0:T(8,128)(2,1)S(1)} %pad_maximum_fusion), channel_id=1, source_target_pairs={{0,8},{4,12},{8,16},{12,20},{16,24},{20,28},{24,32},{28,36},{32,40... | collective-permute-start | bytes 1572872 | tf_op jit(solution)/shard_map/ppermute | solution.py:17
  6.5 4.0 %collective-permute-start = (bf16[2,128,8,128]{3,1,2,0:T(8,128)(2,1)S(1)}, bf16[2,128,8,128]{3,1,2,0:T(8,128)(2,1)S(1)}, u32[]{:S(2)}, u32[]{:S(2)}) collective-permute-start(bf16[2,128,8,128]{3,1,2,0:T(8,128)(2,1)S(1)} %pad_maximum_fusion), channel_id=1, source_target_pairs={{0,4},{4,8},{8,12},{12,16},{16,20},{20,24},{24,28},{28,32},{32,36}... | collective-permute-start | bytes 1572872 | tf_op jit(solution)/shard_map/ppermute | solution.py:17
  10.9 0.6 fusion.111
  13.5 0.3 fusion.108
  13.9 0.6 fusion.126
  14.4 0.6 fusion.121
  15.1 0.6 fusion.122
  15.7 0.6 fusion.123
  16.3 0.6 slice.87
  16.9 0.6 slice.94
  17.7 1.3 broadcast_compare_fusion.1
  19.1 0.6 fusion.124
  19.7 0.7 fusion.125
  20.3 0.6 fusion.120
  20.9 0.6 slice.92
  31.0 0.3 fusion.53
  31.3 0.3 fusion.128
  31.6 0.3 fusion.129
  32.3 0.6 copy-done
  33.4 0.7 copy-done.2
  34.1 0.3 convolution_bitcast_fusion.3
  34.4 0.4 convolution_multiply_fusion.7
  34.8 0.4 fusion.127
  35.1 3.1 %collective-permute-start.2 = (bf16[8,128,128]{2,1,0:T(8,128)(2,1)S(1)}, bf16[8,128,128]{2,1,0:T(8,128)(2,1)S(1)}, u32[]{:S(2)}, u32[]{:S(2)}) collective-permute-start(bf16[8,128,128]{2,1,0:T(8,128)(2,1)S(1)} %get-tuple-element.75), channel_id=1, source_target_pairs={{0,8},{4,12},{8,16},{12,20},{16,24},{20,28},{24,32},{28,36},{32,40... | collective-permute-start | bytes 786440 | tf_op jit(solution)/shard_map/ppermute | solution.py:17
  38.3 0.3 fusion.68
  38.6 0.4 fusion.49
  39.0 0.3 fusion.33
  39.6 0.3 fusion.32
  40.1 0.9 pad_maximum_fusion.2
  41.3 3.2 %collective-permute-done.2 = bf16[8,128,128]{2,1,0:T(8,128)(2,1)S(1)} collective-permute-done((bf16[8,128,128]{2,1,0:T(8,128)(2,1)S(1)}, bf16[8,128,128]{2,1,0:T(8,128)(2,1)S(1)}, u32[]{:S(2)}, u32[]{:S(2)}) %collective-permute-start.2) | collective-permute-done | bytes 262176 | tf_op jit(solution)/shard_map/ppermute | solution.py:17
  44.5 4.0 %collective-permute-start.3 = (bf16[8,128,128]{2,1,0:T(8,128)(2,1)S(1)}, bf16[8,128,128]{2,1,0:T(8,128)(2,1)S(1)}, u32[]{:S(2)}, u32[]{:S(2)}) collective-permute-start(bf16[8,128,128]{2,1,0:T(8,128)(2,1)S(1)} %fusion.54), channel_id=1, source_target_pairs={{0,16},{4,20},{8,24},{12,28},{16,32},{20,36},{24,40},{28,44},{32,4... | collective-permute-start | bytes 786440 | tf_op jit(solution)/shard_map/ppermute | solution.py:17
  48.6 0.9 pad_maximum_fusion.1
  49.4 0.3 fusion.34
  49.8 6.0 %collective-permute-done.3 = bf16[8,128,128]{2,1,0:T(8,128)(2,1)S(1)} collective-permute-done((bf16[8,128,128]{2,1,0:T(8,128)(2,1)S(1)}, bf16[8,128,128]{2,1,0:T(8,128)(2,1)S(1)}, u32[]{:S(2)}, u32[]{:S(2)}) %collective-permute-start.3) | collective-permute-done | bytes 262176 | tf_op jit(solution)/shard_map/ppermute | solution.py:17
  55.9 2.6 %collective-permute-start.4 = (bf16[8,128,128]{2,1,0:T(8,128)(2,1)S(1)}, bf16[8,128,128]{2,1,0:T(8,128)(2,1)S(1)}, u32[]{:S(2)}, u32[]{:S(2)}) collective-permute-start(bf16[8,128,128]{2,1,0:T(8,128)(2,1)S(1)} %convert_element_type.227), channel_id=1, source_target_pairs={{0,32},{4,36},{8,40},{12,44},{16,48},{20,52},{24,56},{28,60},{32,6... | collective-permute-start | bytes 786440 | tf_op jit(solution)/shard_map/ppermute | solution.py:17
  58.5 1.1 fusion.14
  59.6 3.1 %collective-permute-start.6 = (bf16[2,128,8,128]{3,1,2,0:T(8,128)(2,1)}, bf16[2,128,8,128]{3,1,2,0:T(8,128)(2,1)}, u32[]{:S(2)}, u32[]{:S(2)}) collective-permute-start(bf16[2,128,8,128]{3,1,2,0:T(8,128)(2,1)} %pad_maximum_fusion.1), channel_id=1, source_target_pairs={{4,0},{8,4},{12,8},{16,12},{20,16},{24,20},{28,24},{32,28},{36,32}... | collective-permute-start | bytes 1572872 | tf_op jit(solution)/shard_map/ppermute | solution.py:17
  62.7 3.6 %collective-permute-start.7 = (bf16[2,128,8,128]{3,1,2,0:T(8,128)(2,1)}, bf16[2,128,8,128]{3,1,2,0:T(8,128)(2,1)}, u32[]{:S(2)}, u32[]{:S(2)}) collective-permute-start(bf16[2,128,8,128]{3,1,2,0:T(8,128)(2,1)} %pad_maximum_fusion.2), channel_id=1, source_target_pairs={{8,0},{12,4},{16,8},{20,12},{24,16},{28,20},{32,24},{36,28},{40,32... | collective-permute-start | bytes 1572872 | tf_op jit(solution)/shard_map/ppermute | solution.py:17
  66.4 0.5 fusion.30
  67.1 0.4 fusion.48
  67.5 8.7 %all-reduce = (f32[128]{0:T(128)S(1)}, f32[128]{0:T(128)S(1)}) all-reduce(f32[128]{0:T(128)S(1)} %get-tuple-element.29, f32[128]{0:T(128)S(1)} %get-tuple-element.28), channel_id=1, replica_groups=mesh['ctx'=64,'head'=4] {'head'}, use_global_device_ids=true, to_apply=%region_17.18 | all-reduce | flops 256 | bytes 2048 | tf_op jit(solution)/shard_map/psum | solution.py:169
  76.5 0.4 fusion.130
  76.9 4.9 %collective-permute-start.5 = (bf16[8,128,128]{2,1,0:T(8,128)(2,1)S(1)}, bf16[8,128,128]{2,1,0:T(8,128)(2,1)S(1)}, u32[]{:S(2)}, u32[]{:S(2)}) collective-permute-start(bf16[8,128,128]{2,1,0:T(8,128)(2,1)S(1)} %get-tuple-element.86), channel_id=1, source_target_pairs={{4,0},{8,4},{12,8},{16,12},{20,16},{24,20},{28,24},{32,28},{36,32}... | collective-permute-start | bytes 786440 | tf_op jit(solution)/shard_map/ppermute | solution.py:17
  82.1 0.3 fusion.39
  82.4 10.4 %collective-permute-done.5 = bf16[8,128,128]{2,1,0:T(8,128)(2,1)S(1)} collective-permute-done((bf16[8,128,128]{2,1,0:T(8,128)(2,1)S(1)}, bf16[8,128,128]{2,1,0:T(8,128)(2,1)S(1)}, u32[]{:S(2)}, u32[]{:S(2)}) %collective-permute-start.5) | collective-permute-done | bytes 262176 | tf_op jit(solution)/shard_map/ppermute | solution.py:17
  92.9 1.9 %collective-permute-start.8 = (bf16[8,128,128]{2,1,0:T(8,128)(2,1)S(1)}, bf16[8,128,128]{2,1,0:T(8,128)(2,1)S(1)}, u32[]{:S(2)}, u32[]{:S(2)}) collective-permute-start(bf16[8,128,128]{2,1,0:T(8,128)(2,1)S(1)} %get-tuple-element.47), channel_id=1, source_target_pairs={{8,0},{12,4},{16,8},{20,12},{24,16},{28,20},{32,24},{36,28},{40,32... | collective-permute-start | bytes 786440 | tf_op jit(solution)/shard_map/ppermute | solution.py:17
  94.8 0.7 fusion.29
  95.5 7.8 %collective-permute-done.8 = bf16[8,128,128]{2,1,0:T(8,128)(2,1)S(1)} collective-permute-done((bf16[8,128,128]{2,1,0:T(8,128)(2,1)S(1)}, bf16[8,128,128]{2,1,0:T(8,128)(2,1)S(1)}, u32[]{:S(2)}, u32[]{:S(2)}) %collective-permute-start.8) | collective-permute-done | bytes 262176 | tf_op jit(solution)/shard_map/ppermute | solution.py:17
  103.4 1.9 %collective-permute-start.9 = (bf16[8,128,128]{2,1,0:T(8,128)(2,1)S(1)}, bf16[8,128,128]{2,1,0:T(8,128)(2,1)S(1)}, u32[]{:S(2)}, u32[]{:S(2)}) collective-permute-start(bf16[8,128,128]{2,1,0:T(8,128)(2,1)S(1)} %fusion.55), channel_id=1, source_target_pairs={{16,0},{20,4},{24,8},{28,12},{32,16},{36,20},{40,24},{44,28},{48,3... | collective-permute-start | bytes 786440 | tf_op jit(solution)/shard_map/ppermute | solution.py:17
  105.3 0.3 fusion.36
  105.6 8.5 %collective-permute-done.9 = bf16[8,128,128]{2,1,0:T(8,128)(2,1)S(1)} collective-permute-done((bf16[8,128,128]{2,1,0:T(8,128)(2,1)S(1)}, bf16[8,128,128]{2,1,0:T(8,128)(2,1)S(1)}, u32[]{:S(2)}, u32[]{:S(2)}) %collective-permute-start.9) | collective-permute-done | bytes 262176 | tf_op jit(solution)/shard_map/ppermute | solution.py:17
  114.2 1.9 %collective-permute-start.11 = (bf16[8,128,128]{2,1,0:T(8,128)(2,1)S(1)}, bf16[8,128,128]{2,1,0:T(8,128)(2,1)S(1)}, u32[]{:S(2)}, u32[]{:S(2)}) collective-permute-start(bf16[8,128,128]{2,1,0:T(8,128)(2,1)S(1)} %add_convert_fusion), channel_id=1, source_target_pairs={{36,0},{40,4},{44,8},{48,12},{52,16},{56,20},{60,24},{64,28},{68,3... | collective-permute-start | bytes 786440 | tf_op jit(solution)/shard_map/ppermute | solution.py:17
  116.2 2.1 %collective-permute-start.10 = (bf16[8,128,128]{2,1,0:T(8,128)(2,1)S(1)}, bf16[8,128,128]{2,1,0:T(8,128)(2,1)S(1)}, u32[]{:S(2)}, u32[]{:S(2)}) collective-permute-start(bf16[8,128,128]{2,1,0:T(8,128)(2,1)S(1)} %add_convert_fusion), channel_id=1, source_target_pairs={{4,0},{8,4},{12,8},{16,12},{20,16},{24,20},{28,24},{32,28},{36,32}... | collective-permute-start | bytes 786440 | tf_op jit(solution)/shard_map/ppermute | solution.py:17
  118.5 0.9 copy.204
  119.4 0.9 copy.205
  120.5 7.3 %collective-permute-done.11 = bf16[8,128,128]{2,1,0:T(8,128)(2,1)S(1)} collective-permute-done((bf16[8,128,128]{2,1,0:T(8,128)(2,1)S(1)}, bf16[8,128,128]{2,1,0:T(8,128)(2,1)S(1)}, u32[]{:S(2)}, u32[]{:S(2)}) %collective-permute-start.11) | collective-permute-done | bytes 262176 | tf_op jit(solution)/shard_map/ppermute | solution.py:17
  127.7 2.3 %collective-permute-done.10 = bf16[8,128,128]{2,1,0:T(8,128)(2,1)S(1)} collective-permute-done((bf16[8,128,128]{2,1,0:T(8,128)(2,1)S(1)}, bf16[8,128,128]{2,1,0:T(8,128)(2,1)S(1)}, u32[]{:S(2)}, u32[]{:S(2)}) %collective-permute-start.10) | collective-permute-done | bytes 262176 | tf_op jit(solution)/shard_map/ppermute | solution.py:17
  130.0 0.5 fusion.26
  130.5 1.3 fusion.31
  131.8 0.7 fusion.28
  132.5 1.3 fusion.35
  133.8 0.9 copy.206
  134.7 0.9 copy.207
  (69 shorter events, 4.6 us)
Async XLA Ops:
  1.8 8.8 %copy-start.8 = (s32[64]{0:T(128)S(1)}, s32[64]{0:T(128)}, u32[]{:S(2)}) copy-start(s32[64]{0:T(128)} %param.10) | copy-start | bytes 772
  1.8 29.5 %collective-permute-start.1 = (bf16[2,128,8,128]{3,1,2,0:T(8,128)(2,1)S(1)}, bf16[2,128,8,128]{3,1,2,0:T(8,128)(2,1)S(1)}, u32[]{:S(2)}, u32[]{:S(2)}) collective-permute-start(bf16[2,128,8,128]{3,1,2,0:T(8,128)(2,1)S(1)} %pad_maximum_fusion), channel_id=1, source_target_pairs={{0,8},{4,12},{8,16},{12,20},{16,24},{20,28},{24,32},{28,36},{32,40... | collective-permute-start | bytes 1572872 | tf_op jit(solution)/shard_map/ppermute | solution.py:17
  6.5 25.1 %collective-permute-start = (bf16[2,128,8,128]{3,1,2,0:T(8,128)(2,1)S(1)}, bf16[2,128,8,128]{3,1,2,0:T(8,128)(2,1)S(1)}, u32[]{:S(2)}, u32[]{:S(2)}) collective-permute-start(bf16[2,128,8,128]{3,1,2,0:T(8,128)(2,1)S(1)} %pad_maximum_fusion), channel_id=1, source_target_pairs={{0,4},{4,8},{8,12},{12,16},{16,20},{20,24},{24,28},{28,32},{32,36}... | collective-permute-start | bytes 1572872 | tf_op jit(solution)/shard_map/ppermute | solution.py:17
  10.5 20.5 %copy-start.3 = (bf16[128,8,128]{2,1,0:T(8,128)(2,1)S(1)}, bf16[128,8,128]{2,1,0:T(8,128)(2,1)}, u32[]{:S(2)}) copy-start(bf16[128,8,128]{2,1,0:T(8,128)(2,1)} %param.7) | copy-start | bytes 786436
  10.5 20.5 %copy-start.1 = (bf16[128,8,128]{2,1,0:T(8,128)(2,1)S(1)}, bf16[128,8,128]{2,1,0:T(8,128)(2,1)}, u32[]{:S(2)}) copy-start(bf16[128,8,128]{2,1,0:T(8,128)(2,1)} %param.6) | copy-start | bytes 786436
  32.0 1.0 copy-start
  33.2 1.0 copy-start.2
  35.1 9.3 %collective-permute-start.2 = (bf16[8,128,128]{2,1,0:T(8,128)(2,1)S(1)}, bf16[8,128,128]{2,1,0:T(8,128)(2,1)S(1)}, u32[]{:S(2)}, u32[]{:S(2)}) collective-permute-start(bf16[8,128,128]{2,1,0:T(8,128)(2,1)S(1)} %get-tuple-element.75), channel_id=1, source_target_pairs={{0,8},{4,12},{8,16},{12,20},{16,24},{20,28},{24,32},{28,36},{32,40... | collective-permute-start | bytes 786440 | tf_op jit(solution)/shard_map/ppermute | solution.py:17
  44.5 11.2 %collective-permute-start.3 = (bf16[8,128,128]{2,1,0:T(8,128)(2,1)S(1)}, bf16[8,128,128]{2,1,0:T(8,128)(2,1)S(1)}, u32[]{:S(2)}, u32[]{:S(2)}) collective-permute-start(bf16[8,128,128]{2,1,0:T(8,128)(2,1)S(1)} %fusion.54), channel_id=1, source_target_pairs={{0,16},{4,20},{8,24},{12,28},{16,32},{20,36},{24,40},{28,44},{32,4... | collective-permute-start | bytes 786440 | tf_op jit(solution)/shard_map/ppermute | solution.py:17
  55.9 10.5 %collective-permute-start.4 = (bf16[8,128,128]{2,1,0:T(8,128)(2,1)S(1)}, bf16[8,128,128]{2,1,0:T(8,128)(2,1)S(1)}, u32[]{:S(2)}, u32[]{:S(2)}) collective-permute-start(bf16[8,128,128]{2,1,0:T(8,128)(2,1)S(1)} %convert_element_type.227), channel_id=1, source_target_pairs={{0,32},{4,36},{8,40},{12,44},{16,48},{20,52},{24,56},{28,60},{32,6... | collective-permute-start | bytes 786440 | tf_op jit(solution)/shard_map/ppermute | solution.py:17
  59.6 33.1 %collective-permute-start.6 = (bf16[2,128,8,128]{3,1,2,0:T(8,128)(2,1)}, bf16[2,128,8,128]{3,1,2,0:T(8,128)(2,1)}, u32[]{:S(2)}, u32[]{:S(2)}) collective-permute-start(bf16[2,128,8,128]{3,1,2,0:T(8,128)(2,1)} %pad_maximum_fusion.1), channel_id=1, source_target_pairs={{4,0},{8,4},{12,8},{16,12},{20,16},{24,20},{28,24},{32,28},{36,32}... | collective-permute-start | bytes 1572872 | tf_op jit(solution)/shard_map/ppermute | solution.py:17
  62.7 30.0 %collective-permute-start.7 = (bf16[2,128,8,128]{3,1,2,0:T(8,128)(2,1)}, bf16[2,128,8,128]{3,1,2,0:T(8,128)(2,1)}, u32[]{:S(2)}, u32[]{:S(2)}) collective-permute-start(bf16[2,128,8,128]{3,1,2,0:T(8,128)(2,1)} %pad_maximum_fusion.2), channel_id=1, source_target_pairs={{8,0},{12,4},{16,8},{20,12},{24,16},{28,20},{32,24},{36,28},{40,32... | collective-permute-start | bytes 1572872 | tf_op jit(solution)/shard_map/ppermute | solution.py:17
  66.3 0.7 copy-start.5
  66.4 0.7 copy-start.7
  76.5 5.3 %copy-start.4 = (f32[128,8,128]{2,0,1:T(8,128)S(1)}, f32[128,8,128]{2,0,1:T(8,128)}, u32[]{:S(2)}) copy-start(f32[128,8,128]{2,0,1:T(8,128)} %fusion.14) | copy-start | bytes 1572868
  76.9 15.8 %collective-permute-start.5 = (bf16[8,128,128]{2,1,0:T(8,128)(2,1)S(1)}, bf16[8,128,128]{2,1,0:T(8,128)(2,1)S(1)}, u32[]{:S(2)}, u32[]{:S(2)}) collective-permute-start(bf16[8,128,128]{2,1,0:T(8,128)(2,1)S(1)} %get-tuple-element.86), channel_id=1, source_target_pairs={{4,0},{8,4},{12,8},{16,12},{20,16},{24,20},{28,24},{32,28},{36,32}... | collective-permute-start | bytes 786440 | tf_op jit(solution)/shard_map/ppermute | solution.py:17
  92.8 2.0 %copy-start.6 = (bf16[8,128,128]{2,1,0:T(8,128)(2,1)S(1)}, bf16[8,128,128]{2,1,0:T(8,128)(2,1)}, u32[]{:S(2)}) copy-start(bf16[8,128,128]{2,1,0:T(8,128)(2,1)} %copy-done.5) | copy-start | bytes 786436
  92.9 10.4 %collective-permute-start.8 = (bf16[8,128,128]{2,1,0:T(8,128)(2,1)S(1)}, bf16[8,128,128]{2,1,0:T(8,128)(2,1)S(1)}, u32[]{:S(2)}, u32[]{:S(2)}) collective-permute-start(bf16[8,128,128]{2,1,0:T(8,128)(2,1)S(1)} %get-tuple-element.47), channel_id=1, source_target_pairs={{8,0},{12,4},{16,8},{20,12},{24,16},{28,20},{32,24},{36,28},{40,32... | collective-permute-start | bytes 786440 | tf_op jit(solution)/shard_map/ppermute | solution.py:17
  103.4 10.7 %collective-permute-start.9 = (bf16[8,128,128]{2,1,0:T(8,128)(2,1)S(1)}, bf16[8,128,128]{2,1,0:T(8,128)(2,1)S(1)}, u32[]{:S(2)}, u32[]{:S(2)}) collective-permute-start(bf16[8,128,128]{2,1,0:T(8,128)(2,1)S(1)} %fusion.55), channel_id=1, source_target_pairs={{16,0},{20,4},{24,8},{28,12},{32,16},{36,20},{40,24},{44,28},{48,3... | collective-permute-start | bytes 786440 | tf_op jit(solution)/shard_map/ppermute | solution.py:17
  114.2 13.5 %collective-permute-start.11 = (bf16[8,128,128]{2,1,0:T(8,128)(2,1)S(1)}, bf16[8,128,128]{2,1,0:T(8,128)(2,1)S(1)}, u32[]{:S(2)}, u32[]{:S(2)}) collective-permute-start(bf16[8,128,128]{2,1,0:T(8,128)(2,1)S(1)} %add_convert_fusion), channel_id=1, source_target_pairs={{36,0},{40,4},{44,8},{48,12},{52,16},{56,20},{60,24},{64,28},{68,3... | collective-permute-start | bytes 786440 | tf_op jit(solution)/shard_map/ppermute | solution.py:17
  116.2 13.9 %collective-permute-start.10 = (bf16[8,128,128]{2,1,0:T(8,128)(2,1)S(1)}, bf16[8,128,128]{2,1,0:T(8,128)(2,1)S(1)}, u32[]{:S(2)}, u32[]{:S(2)}) collective-permute-start(bf16[8,128,128]{2,1,0:T(8,128)(2,1)S(1)} %add_convert_fusion), channel_id=1, source_target_pairs={{4,0},{8,4},{12,8},{16,12},{20,16},{24,20},{28,24},{32,28},{36,32}... | collective-permute-start | bytes 786440 | tf_op jit(solution)/shard_map/ppermute | solution.py:17

commit v9 on v8

--- a/solution.py
+++ b/solution.py
@@ -15,6 +15,23 @@
     devices = lax.axis_size(axis)
     pairs = [(i, i + by) for i in range(devices) if 0 <= i + by < devices]
     return lax.ppermute(x, axis, pairs)
+
+
+def relay(x, axis, by, sources):
+    devices = lax.axis_size(axis)
+    return lax.ppermute(x, axis, [(i, i + by) for i in sources if 0 <= i + by < devices])
+
+
+def window_tiles(pair, axis):
+    devices = lax.axis_size(axis)
+    if SPAN != 2 or devices % 2:
+        return [from_behind(pair, axis, shift) for shift in range(SPAN, 0, -1)]
+    even = range(0, devices, 2)
+    one_back = from_behind(pair, axis, 1)
+    from_even = relay(pair, axis, 2, even)
+    relayed = relay(one_back, axis, 1, even)
+    two_back = jnp.where(lax.axis_index(axis) % 2 == 0, from_even, relayed)
+    return [two_back, one_back]
 
 
 def send_state(x, axis, by):
@@ -90,7 +107,7 @@
     prev_doc = one_doc(doc_lengths, base - 1)
     next_doc = one_doc(doc_lengths, base + tile)
     pair = jnp.stack([keys, values])
-    arrived = [from_behind(pair, "ctx", shift) for shift in range(SPAN, 0, -1)]
+    arrived = window_tiles(pair, "ctx")
     key_tiles = [piece[0] for piece in arrived] + [keys]
     value_tiles = [piece[1] for piece in arrived] + [values]
     masks = []

time: 136 us -> 138 us (1.015)
  starting transfers between devices: 37.9 us -> 40.6 us
  waiting for transfers between devices: 45.4 us -> 43.7 us
    ppermute x0 -> x2, starting transfers between devices: none -> 2.12 us  [relay(): lax.ppermute(x, axis, [(i, i + by) for i in sources if 0 <= i + by < devi...]
    ppermute x12 -> x11, waiting for transfers between devices: 45.4 us -> 43.7 us  [from_behind(): return lax.ppermute(x, axis, pairs)]
    ppermute x12 -> x11, starting transfers between devices: 37.9 us -> 38.4 us  [from_behind(): return lax.ppermute(x, axis, pairs)]
    unnamed x22 -> x20, local copies, waits for them, and re-layouts: 5.14 us -> 5.08 us
  transfers between devices with their start and end apart: 12 -> 13, of which waited for: 7 -> 7; matrix products, arithmetic and copies ran while one was open for 15% -> 16% of each run, Pallas kernels for 0% -> 0%
where the time goes in v9:
time: 138 us; the launch traced here: 137 us
  waiting for transfers between devices  43.7 us (32%)
  starting transfers between devices  40.6 us (29%)
  matrix products  12.7 us (9%)
  local copies, waits for them, and re-layouts  12.3 us (9%)
  between operations  12 us (9%)
  blocking collectives  8.68 us (6%)
  other arithmetic  7.39 us (5%)
    ppermute x11, waiting for transfers between devices, from_behind(): return lax.ppermute(x, axis, pairs)  43.7 us
    ppermute x11, starting transfers between devices, from_behind(): return lax.ppermute(x, axis, pairs)  38.4 us
    dot_general x26, matrix products, narrow(): return jnp.einsum(form, left, right, preferred_element_type=jnp.float32)  10.3 us
    psum x1, blocking collectives, per_device(): squares = lax.psum(jnp.sum(linear_out * linear_out, axis=(1, 2)), 'head')  8.68 us
    unnamed x20, local copies, waits for them, and re-layouts  5.08 us
  transfers between devices with their start and end apart: 13, of which 7 were waited for; matrix products, arithmetic and copies ran while one was open for 16% of the time, Pallas kernels for 0%

profile of v9, /device:TPU:103, one launch (start us, length us, event | category | flops | bytes accessed | tf_op | source)
XLA Modules:
  0.0 137.4 jit_solution(14457188083295278480)
XLA Ops:
  0.6 1.1 copy_bitcast_fusion
  1.9 0.8 collective-permute-start.1
  2.7 7.9 %collective-permute-start = (bf16[2,128,8,128]{3,1,2,0:T(8,128)(2,1)S(1)}, bf16[2,128,8,128]{3,1,2,0:T(8,128)(2,1)S(1)}, u32[]{:S(2)}, u32[]{:S(2)}) collective-permute-start(bf16[2,128,8,128]{3,1,2,0:T(8,128)(2,1)S(1)} %pad_maximum_fusion), channel_id=1, source_target_pairs={{0,4},{4,8},{8,12},{12,16},{16,20},{20,24},{24,28},{28,32},{32,36}... | collective-permute-start | bytes 1572872 | tf_op jit(solution)/shard_map/ppermute | solution.py:17
  11.0 0.6 fusion.113
  13.6 0.3 fusion.110
  14.0 0.6 fusion.128
  14.6 0.6 fusion.123
  15.2 0.6 fusion.124
  15.8 0.6 fusion.125
  16.4 0.6 fusion.126
  17.1 0.6 slice.94
  17.7 0.6 slice.87
  18.3 1.3 broadcast_compare_fusion.1
  19.6 0.7 fusion.127
  20.5 0.3 fusion.54
  20.8 1.3 collective-permute-start.2
  22.1 0.6 fusion.122
  22.7 0.6 slice.92
  32.8 0.4 fusion.64
  33.1 0.3 fusion.131
  33.5 0.3 fusion.130
  34.1 0.6 copy-done
  35.3 0.4 fusion.129
  35.6 3.1 %collective-permute-start.3 = (bf16[8,128,128]{2,1,0:T(8,128)(2,1)S(1)}, bf16[8,128,128]{2,1,0:T(8,128)(2,1)S(1)}, u32[]{:S(2)}, u32[]{:S(2)}) collective-permute-start(bf16[8,128,128]{2,1,0:T(8,128)(2,1)S(1)} %get-tuple-element.75), channel_id=1, source_target_pairs={{0,8},{4,12},{8,16},{12,20},{16,24},{20,28},{24,32},{28,36},{32,40... | collective-permute-start | bytes 786440 | tf_op jit(solution)/shard_map/ppermute | solution.py:17
  39.1 0.3 fusion.18
  39.4 0.6 copy-done.2
  40.0 0.4 fusion.50
  40.4 0.3 fusion.34
  41.0 0.3 fusion.33
  41.5 0.9 pad_maximum_fusion.2
  42.7 1.6 %collective-permute-done.3 = bf16[8,128,128]{2,1,0:T(8,128)(2,1)S(1)} collective-permute-done((bf16[8,128,128]{2,1,0:T(8,128)(2,1)S(1)}, bf16[8,128,128]{2,1,0:T(8,128)(2,1)S(1)}, u32[]{:S(2)}, u32[]{:S(2)}) %collective-permute-start.3) | collective-permute-done | bytes 262176 | tf_op jit(solution)/shard_map/ppermute | solution.py:17
  44.3 2.7 %collective-permute-start.4 = (bf16[8,128,128]{2,1,0:T(8,128)(2,1)S(1)}, bf16[8,128,128]{2,1,0:T(8,128)(2,1)S(1)}, u32[]{:S(2)}, u32[]{:S(2)}) collective-permute-start(bf16[8,128,128]{2,1,0:T(8,128)(2,1)S(1)} %fusion.55), channel_id=1, source_target_pairs={{0,16},{4,20},{8,24},{12,28},{16,32},{20,36},{24,40},{28,44},{32,4... | collective-permute-start | bytes 786440 | tf_op jit(solution)/shard_map/ppermute | solution.py:17
  47.0 0.9 pad_maximum_fusion.1
  47.8 0.3 fusion.35
  48.1 5.3 %collective-permute-done.4 = bf16[8,128,128]{2,1,0:T(8,128)(2,1)S(1)} collective-permute-done((bf16[8,128,128]{2,1,0:T(8,128)(2,1)S(1)}, bf16[8,128,128]{2,1,0:T(8,128)(2,1)S(1)}, u32[]{:S(2)}, u32[]{:S(2)}) %collective-permute-start.4) | collective-permute-done | bytes 262176 | tf_op jit(solution)/shard_map/ppermute | solution.py:17
  53.5 2.8 %collective-permute-start.5 = (bf16[8,128,128]{2,1,0:T(8,128)(2,1)S(1)}, bf16[8,128,128]{2,1,0:T(8,128)(2,1)S(1)}, u32[]{:S(2)}, u32[]{:S(2)}) collective-permute-start(bf16[8,128,128]{2,1,0:T(8,128)(2,1)S(1)} %convert_element_type.227), channel_id=1, source_target_pairs={{0,32},{4,36},{8,40},{12,44},{16,48},{20,52},{24,56},{28,60},{32,6... | collective-permute-start | bytes 786440 | tf_op jit(solution)/shard_map/ppermute | solution.py:17
  56.7 5.0 %collective-permute-start.7 = (bf16[2,128,8,128]{3,1,2,0:T(8,128)(2,1)}, bf16[2,128,8,128]{3,1,2,0:T(8,128)(2,1)}, u32[]{:S(2)}, u32[]{:S(2)}) collective-permute-start(bf16[2,128,8,128]{3,1,2,0:T(8,128)(2,1)} %pad_maximum_fusion.1), channel_id=1, source_target_pairs={{4,0},{8,4},{12,8},{16,12},{20,16},{24,20},{28,24},{32,28},{36,32}... | collective-permute-start | bytes 1572872 | tf_op jit(solution)/shard_map/ppermute | solution.py:17
  61.7 4.8 %collective-permute-start.8 = (bf16[2,128,8,128]{3,1,2,0:T(8,128)(2,1)}, bf16[2,128,8,128]{3,1,2,0:T(8,128)(2,1)}, u32[]{:S(2)}, u32[]{:S(2)}) collective-permute-start(bf16[2,128,8,128]{3,1,2,0:T(8,128)(2,1)} %pad_maximum_fusion.2), channel_id=1, source_target_pairs={{8,0},{12,4},{16,8},{20,12},{24,16},{28,20},{32,24},{36,28},{40,32... | collective-permute-start | bytes 1572872 | tf_op jit(solution)/shard_map/ppermute | solution.py:17
  66.5 0.5 fusion.31
  67.2 1.1 fusion.49
  68.3 8.7 %all-reduce = (f32[128]{0:T(128)S(1)}, f32[128]{0:T(128)S(1)}) all-reduce(f32[128]{0:T(128)S(1)} %get-tuple-element.29, f32[128]{0:T(128)S(1)} %get-tuple-element.28), channel_id=1, replica_groups=mesh['ctx'=64,'head'=4] {'head'}, use_global_device_ids=true, to_apply=%region_17.18 | all-reduce | flops 256 | bytes 2048 | tf_op jit(solution)/shard_map/psum | solution.py:186
  77.0 1.3 fusion.48
  78.3 0.4 fusion.132
  78.7 4.2 %collective-permute-start.6 = (bf16[8,128,128]{2,1,0:T(8,128)(2,1)S(1)}, bf16[8,128,128]{2,1,0:T(8,128)(2,1)S(1)}, u32[]{:S(2)}, u32[]{:S(2)}) collective-permute-start(bf16[8,128,128]{2,1,0:T(8,128)(2,1)S(1)} %get-tuple-element.86), channel_id=1, source_target_pairs={{4,0},{8,4},{12,8},{16,12},{20,16},{24,20},{28,24},{32,28},{36,32}... | collective-permute-start | bytes 786440 | tf_op jit(solution)/shard_map/ppermute | solution.py:17
  83.2 0.3 fusion.40
  83.5 11.7 %collective-permute-done.6 = bf16[8,128,128]{2,1,0:T(8,128)(2,1)S(1)} collective-permute-done((bf16[8,128,128]{2,1,0:T(8,128)(2,1)S(1)}, bf16[8,128,128]{2,1,0:T(8,128)(2,1)S(1)}, u32[]{:S(2)}, u32[]{:S(2)}) %collective-permute-start.6) | collective-permute-done | bytes 262176 | tf_op jit(solution)/shard_map/ppermute | solution.py:17
  95.4 1.9 %collective-permute-start.9 = (bf16[8,128,128]{2,1,0:T(8,128)(2,1)S(1)}, bf16[8,128,128]{2,1,0:T(8,128)(2,1)S(1)}, u32[]{:S(2)}, u32[]{:S(2)}) collective-permute-start(bf16[8,128,128]{2,1,0:T(8,128)(2,1)S(1)} %get-tuple-element.47), channel_id=1, source_target_pairs={{8,0},{12,4},{16,8},{20,12},{24,16},{28,20},{32,24},{36,28},{40,32... | collective-permute-start | bytes 786440 | tf_op jit(solution)/shard_map/ppermute | solution.py:17
  97.3 0.7 fusion.30
  98.0 7.8 %collective-permute-done.9 = bf16[8,128,128]{2,1,0:T(8,128)(2,1)S(1)} collective-permute-done((bf16[8,128,128]{2,1,0:T(8,128)(2,1)S(1)}, bf16[8,128,128]{2,1,0:T(8,128)(2,1)S(1)}, u32[]{:S(2)}, u32[]{:S(2)}) %collective-permute-start.9) | collective-permute-done | bytes 262176 | tf_op jit(solution)/shard_map/ppermute | solution.py:17
  105.9 1.9 %collective-permute-start.10 = (bf16[8,128,128]{2,1,0:T(8,128)(2,1)S(1)}, bf16[8,128,128]{2,1,0:T(8,128)(2,1)S(1)}, u32[]{:S(2)}, u32[]{:S(2)}) collective-permute-start(bf16[8,128,128]{2,1,0:T(8,128)(2,1)S(1)} %fusion.56), channel_id=1, source_target_pairs={{16,0},{20,4},{24,8},{28,12},{32,16},{36,20},{40,24},{44,28},{48,3... | collective-permute-start | bytes 786440 | tf_op jit(solution)/shard_map/ppermute | solution.py:17
  107.8 0.3 fusion.37
  108.1 8.5 %collective-permute-done.10 = bf16[8,128,128]{2,1,0:T(8,128)(2,1)S(1)} collective-permute-done((bf16[8,128,128]{2,1,0:T(8,128)(2,1)S(1)}, bf16[8,128,128]{2,1,0:T(8,128)(2,1)S(1)}, u32[]{:S(2)}, u32[]{:S(2)}) %collective-permute-start.10) | collective-permute-done | bytes 262176 | tf_op jit(solution)/shard_map/ppermute | solution.py:17
  116.7 1.9 %collective-permute-start.12 = (bf16[8,128,128]{2,1,0:T(8,128)(2,1)S(1)}, bf16[8,128,128]{2,1,0:T(8,128)(2,1)S(1)}, u32[]{:S(2)}, u32[]{:S(2)}) collective-permute-start(bf16[8,128,128]{2,1,0:T(8,128)(2,1)S(1)} %add_convert_fusion), channel_id=1, source_target_pairs={{36,0},{40,4},{44,8},{48,12},{52,16},{56,20},{60,24},{64,28},{68,3... | collective-permute-start | bytes 786440 | tf_op jit(solution)/shard_map/ppermute | solution.py:17
  118.7 2.1 %collective-permute-start.11 = (bf16[8,128,128]{2,1,0:T(8,128)(2,1)S(1)}, bf16[8,128,128]{2,1,0:T(8,128)(2,1)S(1)}, u32[]{:S(2)}, u32[]{:S(2)}) collective-permute-start(bf16[8,128,128]{2,1,0:T(8,128)(2,1)S(1)} %add_convert_fusion), channel_id=1, source_target_pairs={{4,0},{8,4},{12,8},{16,12},{20,16},{24,20},{28,24},{32,28},{36,32}... | collective-permute-start | bytes 786440 | tf_op jit(solution)/shard_map/ppermute | solution.py:17
  121.0 0.9 copy.204
  121.9 0.9 copy.205
  123.0 6.2 %collective-permute-done.12 = bf16[8,128,128]{2,1,0:T(8,128)(2,1)S(1)} collective-permute-done((bf16[8,128,128]{2,1,0:T(8,128)(2,1)S(1)}, bf16[8,128,128]{2,1,0:T(8,128)(2,1)S(1)}, u32[]{:S(2)}, u32[]{:S(2)}) %collective-permute-start.12) | collective-permute-done | bytes 262176 | tf_op jit(solution)/shard_map/ppermute | solution.py:17
  129.1 2.7 %collective-permute-done.11 = bf16[8,128,128]{2,1,0:T(8,128)(2,1)S(1)} collective-permute-done((bf16[8,128,128]{2,1,0:T(8,128)(2,1)S(1)}, bf16[8,128,128]{2,1,0:T(8,128)(2,1)S(1)}, u32[]{:S(2)}, u32[]{:S(2)}) %collective-permute-start.11) | collective-permute-done | bytes 262176 | tf_op jit(solution)/shard_map/ppermute | solution.py:17
  131.8 0.5 fusion.27
  132.3 1.3 fusion.32
  133.6 0.7 fusion.29
  134.3 1.3 fusion.36
  135.6 0.9 copy.206
  136.5 0.9 copy.207
  (70 shorter events, 5.0 us)
Async XLA Ops:
  1.8 8.9 %copy-start.7 = (s32[64]{0:T(128)S(1)}, s32[64]{0:T(128)}, u32[]{:S(2)}) copy-start(s32[64]{0:T(128)} %param.10) | copy-start | bytes 772
  1.8 18.7 %copy-start.3 = (bf16[128,8,128]{2,1,0:T(8,128)(2,1)S(1)}, bf16[128,8,128]{2,1,0:T(8,128)(2,1)}, u32[]{:S(2)}) copy-start(bf16[128,8,128]{2,1,0:T(8,128)(2,1)} %param.7) | copy-start | bytes 786436
  1.8 18.6 %copy-start.1 = (bf16[128,8,128]{2,1,0:T(8,128)(2,1)S(1)}, bf16[128,8,128]{2,1,0:T(8,128)(2,1)}, u32[]{:S(2)}) copy-start(bf16[128,8,128]{2,1,0:T(8,128)(2,1)} %param.6) | copy-start | bytes 786436
  1.9 31.6 %collective-permute-start.1 = (bf16[2,128,8,128]{3,1,2,0:T(8,128)(2,1)S(1)}, bf16[2,128,8,128]{3,1,2,0:T(8,128)(2,1)S(1)}, u32[]{:S(2)}, u32[]{:S(2)}) collective-permute-start(bf16[2,128,8,128]{3,1,2,0:T(8,128)(2,1)S(1)} %pad_maximum_fusion), channel_id=1, source_target_pairs={{0,8},{8,16},{16,24},{24,32},{32,40},{40,48},{48,56},{56,64},{64,7... | collective-permute-start | bytes 1572872 | tf_op jit(solution)/shard_map/ppermute | solution.py:22
  2.7 18.1 %collective-permute-start = (bf16[2,128,8,128]{3,1,2,0:T(8,128)(2,1)S(1)}, bf16[2,128,8,128]{3,1,2,0:T(8,128)(2,1)S(1)}, u32[]{:S(2)}, u32[]{:S(2)}) collective-permute-start(bf16[2,128,8,128]{3,1,2,0:T(8,128)(2,1)S(1)} %pad_maximum_fusion), channel_id=1, source_target_pairs={{0,4},{4,8},{8,12},{12,16},{16,20},{20,24},{24,28},{28,32},{32,36}... | collective-permute-start | bytes 1572872 | tf_op jit(solution)/shard_map/ppermute | solution.py:17
  20.8 12.6 %collective-permute-start.2 = (bf16[2,128,8,128]{3,1,2,0:T(8,128)(2,1)S(1)}, bf16[2,128,8,128]{3,1,2,0:T(8,128)(2,1)S(1)}, u32[]{:S(2)}, u32[]{:S(2)}) collective-permute-start(bf16[2,128,8,128]{3,1,2,0:T(8,128)(2,1)S(1)} %collective-permute-done), channel_id=1, source_target_pairs={{0,4},{8,12},{16,20},{24,28},{32,36},{40,44},{48,52},{56,60},{64,6... | collective-permute-start | bytes 1572872 | tf_op jit(solution)/shard_map/ppermute | solution.py:22
  33.8 1.0 copy-start
  35.6 8.6 %collective-permute-start.3 = (bf16[8,128,128]{2,1,0:T(8,128)(2,1)S(1)}, bf16[8,128,128]{2,1,0:T(8,128)(2,1)S(1)}, u32[]{:S(2)}, u32[]{:S(2)}) collective-permute-start(bf16[8,128,128]{2,1,0:T(8,128)(2,1)S(1)} %get-tuple-element.75), channel_id=1, source_target_pairs={{0,8},{4,12},{8,16},{12,20},{16,24},{20,28},{24,32},{28,36},{32,40... | collective-permute-start | bytes 786440 | tf_op jit(solution)/shard_map/ppermute | solution.py:17
  39.1 1.0 copy-start.2
  44.3 9.1 %collective-permute-start.4 = (bf16[8,128,128]{2,1,0:T(8,128)(2,1)S(1)}, bf16[8,128,128]{2,1,0:T(8,128)(2,1)S(1)}, u32[]{:S(2)}, u32[]{:S(2)}) collective-permute-start(bf16[8,128,128]{2,1,0:T(8,128)(2,1)S(1)} %fusion.55), channel_id=1, source_target_pairs={{0,16},{4,20},{8,24},{12,28},{16,32},{20,36},{24,40},{28,44},{32,4... | collective-permute-start | bytes 786440 | tf_op jit(solution)/shard_map/ppermute | solution.py:17
  53.5 13.0 %collective-permute-start.5 = (bf16[8,128,128]{2,1,0:T(8,128)(2,1)S(1)}, bf16[8,128,128]{2,1,0:T(8,128)(2,1)S(1)}, u32[]{:S(2)}, u32[]{:S(2)}) collective-permute-start(bf16[8,128,128]{2,1,0:T(8,128)(2,1)S(1)} %convert_element_type.227), channel_id=1, source_target_pairs={{0,32},{4,36},{8,40},{12,44},{16,48},{20,52},{24,56},{28,60},{32,6... | collective-permute-start | bytes 786440 | tf_op jit(solution)/shard_map/ppermute | solution.py:17
  56.7 38.6 %collective-permute-start.7 = (bf16[2,128,8,128]{3,1,2,0:T(8,128)(2,1)}, bf16[2,128,8,128]{3,1,2,0:T(8,128)(2,1)}, u32[]{:S(2)}, u32[]{:S(2)}) collective-permute-start(bf16[2,128,8,128]{3,1,2,0:T(8,128)(2,1)} %pad_maximum_fusion.1), channel_id=1, source_target_pairs={{4,0},{8,4},{12,8},{16,12},{20,16},{24,20},{28,24},{32,28},{36,32}... | collective-permute-start | bytes 1572872 | tf_op jit(solution)/shard_map/ppermute | solution.py:17
  61.7 33.5 %collective-permute-start.8 = (bf16[2,128,8,128]{3,1,2,0:T(8,128)(2,1)}, bf16[2,128,8,128]{3,1,2,0:T(8,128)(2,1)}, u32[]{:S(2)}, u32[]{:S(2)}) collective-permute-start(bf16[2,128,8,128]{3,1,2,0:T(8,128)(2,1)} %pad_maximum_fusion.2), channel_id=1, source_target_pairs={{8,0},{12,4},{16,8},{20,12},{24,16},{28,20},{32,24},{36,28},{40,32... | collective-permute-start | bytes 1572872 | tf_op jit(solution)/shard_map/ppermute | solution.py:17
  66.5 0.7 copy-start.4
  66.5 0.7 copy-start.6
  78.7 16.5 %collective-permute-start.6 = (bf16[8,128,128]{2,1,0:T(8,128)(2,1)S(1)}, bf16[8,128,128]{2,1,0:T(8,128)(2,1)S(1)}, u32[]{:S(2)}, u32[]{:S(2)}) collective-permute-start(bf16[8,128,128]{2,1,0:T(8,128)(2,1)S(1)} %get-tuple-element.86), channel_id=1, source_target_pairs={{4,0},{8,4},{12,8},{16,12},{20,16},{24,20},{28,24},{32,28},{36,32}... | collective-permute-start | bytes 786440 | tf_op jit(solution)/shard_map/ppermute | solution.py:17
  95.3 2.0 %copy-start.5 = (bf16[8,128,128]{2,1,0:T(8,128)(2,1)S(1)}, bf16[8,128,128]{2,1,0:T(8,128)(2,1)}, u32[]{:S(2)}) copy-start(bf16[8,128,128]{2,1,0:T(8,128)(2,1)} %copy-done.4) | copy-start | bytes 786436
  95.4 10.4 %collective-permute-start.9 = (bf16[8,128,128]{2,1,0:T(8,128)(2,1)S(1)}, bf16[8,128,128]{2,1,0:T(8,128)(2,1)S(1)}, u32[]{:S(2)}, u32[]{:S(2)}) collective-permute-start(bf16[8,128,128]{2,1,0:T(8,128)(2,1)S(1)} %get-tuple-element.47), channel_id=1, source_target_pairs={{8,0},{12,4},{16,8},{20,12},{24,16},{28,20},{32,24},{36,28},{40,32... | collective-permute-start | bytes 786440 | tf_op jit(solution)/shard_map/ppermute | solution.py:17
  105.9 10.7 %collective-permute-start.10 = (bf16[8,128,128]{2,1,0:T(8,128)(2,1)S(1)}, bf16[8,128,128]{2,1,0:T(8,128)(2,1)S(1)}, u32[]{:S(2)}, u32[]{:S(2)}) collective-permute-start(bf16[8,128,128]{2,1,0:T(8,128)(2,1)S(1)} %fusion.56), channel_id=1, source_target_pairs={{16,0},{20,4},{24,8},{28,12},{32,16},{36,20},{40,24},{44,28},{48,3... | collective-permute-start | bytes 786440 | tf_op jit(solution)/shard_map/ppermute | solution.py:17
  116.7 12.4 %collective-permute-start.12 = (bf16[8,128,128]{2,1,0:T(8,128)(2,1)S(1)}, bf16[8,128,128]{2,1,0:T(8,128)(2,1)S(1)}, u32[]{:S(2)}, u32[]{:S(2)}) collective-permute-start(bf16[8,128,128]{2,1,0:T(8,128)(2,1)S(1)} %add_convert_fusion), channel_id=1, source_target_pairs={{36,0},{40,4},{44,8},{48,12},{52,16},{56,20},{60,24},{64,28},{68,3... | collective-permute-start | bytes 786440 | tf_op jit(solution)/shard_map/ppermute | solution.py:17
  118.7 13.2 %collective-permute-start.11 = (bf16[8,128,128]{2,1,0:T(8,128)(2,1)S(1)}, bf16[8,128,128]{2,1,0:T(8,128)(2,1)S(1)}, u32[]{:S(2)}, u32[]{:S(2)}) collective-permute-start(bf16[8,128,128]{2,1,0:T(8,128)(2,1)S(1)} %add_convert_fusion), channel_id=1, source_target_pairs={{4,0},{8,4},{12,8},{16,12},{20,16},{24,20},{28,24},{32,28},{36,32}... | collective-permute-start | bytes 786440 | tf_op jit(solution)/shard_map/ppermute | solution.py:17

commit v10 on v8

--- a/solution.py
+++ b/solution.py
@@ -166,11 +166,16 @@
         narrow("htu,uhd->thd", attend, values)
         + wide("thd,hde->the", query_wide, incoming) * carried_prev[:, None, None]
     )
-    squares = lax.psum(jnp.sum(linear_out * linear_out, axis=(1, 2)), "head")
+    weighted = cotangent.astype(jnp.float32) * gain[None]
+    squares, projection = lax.psum(
+        jnp.stack([
+            jnp.sum(linear_out * linear_out, axis=(1, 2)),
+            jnp.sum(weighted * linear_out, axis=(1, 2)),
+        ]),
+        "head",
+    )
     inverse = lax.rsqrt(squares / features + norm_eps)
     mixed = (linear_out * inverse[:, None, None] * gain[None] + soft_out).astype(jnp.bfloat16)
-    weighted = grad_wide * gain[None]
-    projection = lax.psum(jnp.sum(weighted * linear_out, axis=(1, 2)), "head")
     inner = (
         inverse[:, None, None] * weighted
         - linear_out * (inverse**3 * projection / features)[:, None, None]

time: 136 us -> 136 us (level)
  no operation moved by 1% of the time
where the time goes in v10:
time: 136 us
  waiting for transfers between devices  45.4 us (33%)
  starting transfers between devices  37.9 us (28%)
  matrix products  12.8 us (9%)
  local copies, waits for them, and re-layouts  12.4 us (9%)
  between operations  12 us (9%)
  blocking collectives  8.74 us (6%)
  other arithmetic  6.32 us (5%)
    ppermute x12, waiting for transfers between devices, from_behind(): return lax.ppermute(x, axis, pairs)  45.4 us
    ppermute x12, starting transfers between devices, from_behind(): return lax.ppermute(x, axis, pairs)  37.9 us
    dot_general x26, matrix products, narrow(): return jnp.einsum(form, left, right, preferred_element_type=jnp.float32)  10.5 us
    psum x1, blocking collectives, per_device(): lax.psum(jnp.stack([jnp.sum(linear_out * linear_out, axis=(1, 2)), jnp.su...  8.74 us
    unnamed x22, local copies, waits for them, and re-layouts  5.14 us
  transfers between devices with their start and end apart: 12, of which 7 were waited for; matrix products, arithmetic and copies ran while one was open for 15% of the time, Pallas kernels for 0%

profile of v10, /device:TPU:103, one launch (start us, length us, event | category | flops | bytes accessed | tf_op | source)
XLA Modules:
  0.0 135.6 jit_solution(5013973241469704528)
XLA Ops:
  0.6 1.1 copy_bitcast_fusion
  1.8 4.7 %collective-permute-start.1 = (bf16[2,128,8,128]{3,1,2,0:T(8,128)(2,1)S(1)}, bf16[2,128,8,128]{3,1,2,0:T(8,128)(2,1)S(1)}, u32[]{:S(2)}, u32[]{:S(2)}) collective-permute-start(bf16[2,128,8,128]{3,1,2,0:T(8,128)(2,1)S(1)} %pad_maximum_fusion), channel_id=1, source_target_pairs={{0,8},{4,12},{8,16},{12,20},{16,24},{20,28},{24,32},{28,36},{32,40... | collective-permute-start | bytes 1572872 | tf_op jit(solution)/shard_map/ppermute | solution.py:17
  6.5 4.0 %collective-permute-start = (bf16[2,128,8,128]{3,1,2,0:T(8,128)(2,1)S(1)}, bf16[2,128,8,128]{3,1,2,0:T(8,128)(2,1)S(1)}, u32[]{:S(2)}, u32[]{:S(2)}) collective-permute-start(bf16[2,128,8,128]{3,1,2,0:T(8,128)(2,1)S(1)} %pad_maximum_fusion), channel_id=1, source_target_pairs={{0,4},{4,8},{8,12},{12,16},{16,20},{20,24},{24,28},{28,32},{32,36}... | collective-permute-start | bytes 1572872 | tf_op jit(solution)/shard_map/ppermute | solution.py:17
  10.9 0.6 fusion.111
  13.5 0.3 fusion.108
  13.9 0.6 fusion.126
  14.4 0.6 fusion.121
  15.1 0.6 fusion.122
  15.7 0.6 fusion.123
  16.3 0.6 slice.87
  16.9 0.6 slice.94
  17.7 1.3 broadcast_compare_fusion.1
  19.1 0.6 fusion.124
  19.7 0.7 fusion.125
  20.3 0.6 fusion.120
  20.9 0.6 slice.92
  31.0 0.3 fusion.53
  31.3 0.3 fusion.128
  31.6 0.3 fusion.129
  32.3 0.6 copy-done
  33.4 0.7 copy-done.2
  34.1 0.3 convolution_bitcast_fusion.3
  34.4 0.4 convolution_multiply_fusion.7
  34.8 0.4 fusion.127
  35.1 3.1 %collective-permute-start.2 = (bf16[8,128,128]{2,1,0:T(8,128)(2,1)S(1)}, bf16[8,128,128]{2,1,0:T(8,128)(2,1)S(1)}, u32[]{:S(2)}, u32[]{:S(2)}) collective-permute-start(bf16[8,128,128]{2,1,0:T(8,128)(2,1)S(1)} %get-tuple-element.71), channel_id=1, source_target_pairs={{0,8},{4,12},{8,16},{12,20},{16,24},{20,28},{24,32},{28,36},{32,40... | collective-permute-start | bytes 786440 | tf_op jit(solution)/shard_map/ppermute | solution.py:17
  38.3 0.3 fusion.68
  38.6 0.4 fusion.49
  39.0 0.3 fusion.33
  39.6 0.3 fusion.32
  40.1 0.9 pad_maximum_fusion.2
  41.3 3.2 %collective-permute-done.2 = bf16[8,128,128]{2,1,0:T(8,128)(2,1)S(1)} collective-permute-done((bf16[8,128,128]{2,1,0:T(8,128)(2,1)S(1)}, bf16[8,128,128]{2,1,0:T(8,128)(2,1)S(1)}, u32[]{:S(2)}, u32[]{:S(2)}) %collective-permute-start.2) | collective-permute-done | bytes 262176 | tf_op jit(solution)/shard_map/ppermute | solution.py:17
  44.5 4.0 %collective-permute-start.3 = (bf16[8,128,128]{2,1,0:T(8,128)(2,1)S(1)}, bf16[8,128,128]{2,1,0:T(8,128)(2,1)S(1)}, u32[]{:S(2)}, u32[]{:S(2)}) collective-permute-start(bf16[8,128,128]{2,1,0:T(8,128)(2,1)S(1)} %fusion.54), channel_id=1, source_target_pairs={{0,16},{4,20},{8,24},{12,28},{16,32},{20,36},{24,40},{28,44},{32,4... | collective-permute-start | bytes 786440 | tf_op jit(solution)/shard_map/ppermute | solution.py:17
  48.6 0.9 pad_maximum_fusion.1
  49.4 0.3 fusion.34
  49.8 6.0 %collective-permute-done.3 = bf16[8,128,128]{2,1,0:T(8,128)(2,1)S(1)} collective-permute-done((bf16[8,128,128]{2,1,0:T(8,128)(2,1)S(1)}, bf16[8,128,128]{2,1,0:T(8,128)(2,1)S(1)}, u32[]{:S(2)}, u32[]{:S(2)}) %collective-permute-start.3) | collective-permute-done | bytes 262176 | tf_op jit(solution)/shard_map/ppermute | solution.py:17
  55.9 2.6 %collective-permute-start.4 = (bf16[8,128,128]{2,1,0:T(8,128)(2,1)S(1)}, bf16[8,128,128]{2,1,0:T(8,128)(2,1)S(1)}, u32[]{:S(2)}, u32[]{:S(2)}) collective-permute-start(bf16[8,128,128]{2,1,0:T(8,128)(2,1)S(1)} %convert_element_type.228), channel_id=1, source_target_pairs={{0,32},{4,36},{8,40},{12,44},{16,48},{20,52},{24,56},{28,60},{32,6... | collective-permute-start | bytes 786440 | tf_op jit(solution)/shard_map/ppermute | solution.py:17
  58.5 1.1 fusion.14
  59.6 3.1 %collective-permute-start.6 = (bf16[2,128,8,128]{3,1,2,0:T(8,128)(2,1)}, bf16[2,128,8,128]{3,1,2,0:T(8,128)(2,1)}, u32[]{:S(2)}, u32[]{:S(2)}) collective-permute-start(bf16[2,128,8,128]{3,1,2,0:T(8,128)(2,1)} %pad_maximum_fusion.1), channel_id=1, source_target_pairs={{4,0},{8,4},{12,8},{16,12},{20,16},{24,20},{28,24},{32,28},{36,32}... | collective-permute-start | bytes 1572872 | tf_op jit(solution)/shard_map/ppermute | solution.py:17
  62.7 3.6 %collective-permute-start.7 = (bf16[2,128,8,128]{3,1,2,0:T(8,128)(2,1)}, bf16[2,128,8,128]{3,1,2,0:T(8,128)(2,1)}, u32[]{:S(2)}, u32[]{:S(2)}) collective-permute-start(bf16[2,128,8,128]{3,1,2,0:T(8,128)(2,1)} %pad_maximum_fusion.2), channel_id=1, source_target_pairs={{8,0},{12,4},{16,8},{20,12},{24,16},{28,20},{32,24},{36,28},{40,32... | collective-permute-start | bytes 1572872 | tf_op jit(solution)/shard_map/ppermute | solution.py:17
  66.4 0.5 fusion.30
  67.1 0.4 multiply_reduce_fusion
  67.5 8.7 %psum.7 = f32[2,128]{1,0:T(2,128)S(1)} all-reduce(f32[2,128]{1,0:T(2,128)S(1)} %pad_maximum_fusion.3), channel_id=1, replica_groups=mesh['ctx'=64,'head'=4] {'head'}, use_global_device_ids=true, to_apply=%region_18.19 | all-reduce | flops 256 | bytes 2048 | tf_op jit(solution)/shard_map/psum | solution.py:170
  76.5 0.4 fusion.130
  76.9 4.9 %collective-permute-start.5 = (bf16[8,128,128]{2,1,0:T(8,128)(2,1)S(1)}, bf16[8,128,128]{2,1,0:T(8,128)(2,1)S(1)}, u32[]{:S(2)}, u32[]{:S(2)}) collective-permute-start(bf16[8,128,128]{2,1,0:T(8,128)(2,1)S(1)} %get-tuple-element.82), channel_id=1, source_target_pairs={{4,0},{8,4},{12,8},{16,12},{20,16},{24,20},{28,24},{32,28},{36,32}... | collective-permute-start | bytes 786440 | tf_op jit(solution)/shard_map/ppermute | solution.py:17
  82.1 0.3 fusion.39
  82.4 10.4 %collective-permute-done.5 = bf16[8,128,128]{2,1,0:T(8,128)(2,1)S(1)} collective-permute-done((bf16[8,128,128]{2,1,0:T(8,128)(2,1)S(1)}, bf16[8,128,128]{2,1,0:T(8,128)(2,1)S(1)}, u32[]{:S(2)}, u32[]{:S(2)}) %collective-permute-start.5) | collective-permute-done | bytes 262176 | tf_op jit(solution)/shard_map/ppermute | solution.py:17
  92.9 1.9 %collective-permute-start.8 = (bf16[8,128,128]{2,1,0:T(8,128)(2,1)S(1)}, bf16[8,128,128]{2,1,0:T(8,128)(2,1)S(1)}, u32[]{:S(2)}, u32[]{:S(2)}) collective-permute-start(bf16[8,128,128]{2,1,0:T(8,128)(2,1)S(1)} %get-tuple-element.45), channel_id=1, source_target_pairs={{8,0},{12,4},{16,8},{20,12},{24,16},{28,20},{32,24},{36,28},{40,32... | collective-permute-start | bytes 786440 | tf_op jit(solution)/shard_map/ppermute | solution.py:17
  94.8 0.7 fusion.29
  95.5 7.8 %collective-permute-done.8 = bf16[8,128,128]{2,1,0:T(8,128)(2,1)S(1)} collective-permute-done((bf16[8,128,128]{2,1,0:T(8,128)(2,1)S(1)}, bf16[8,128,128]{2,1,0:T(8,128)(2,1)S(1)}, u32[]{:S(2)}, u32[]{:S(2)}) %collective-permute-start.8) | collective-permute-done | bytes 262176 | tf_op jit(solution)/shard_map/ppermute | solution.py:17
  103.4 1.9 %collective-permute-start.9 = (bf16[8,128,128]{2,1,0:T(8,128)(2,1)S(1)}, bf16[8,128,128]{2,1,0:T(8,128)(2,1)S(1)}, u32[]{:S(2)}, u32[]{:S(2)}) collective-permute-start(bf16[8,128,128]{2,1,0:T(8,128)(2,1)S(1)} %fusion.55), channel_id=1, source_target_pairs={{16,0},{20,4},{24,8},{28,12},{32,16},{36,20},{40,24},{44,28},{48,3... | collective-permute-start | bytes 786440 | tf_op jit(solution)/shard_map/ppermute | solution.py:17
  105.3 0.3 fusion.36
  105.6 8.5 %collective-permute-done.9 = bf16[8,128,128]{2,1,0:T(8,128)(2,1)S(1)} collective-permute-done((bf16[8,128,128]{2,1,0:T(8,128)(2,1)S(1)}, bf16[8,128,128]{2,1,0:T(8,128)(2,1)S(1)}, u32[]{:S(2)}, u32[]{:S(2)}) %collective-permute-start.9) | collective-permute-done | bytes 262176 | tf_op jit(solution)/shard_map/ppermute | solution.py:17
  114.3 1.9 %collective-permute-start.11 = (bf16[8,128,128]{2,1,0:T(8,128)(2,1)S(1)}, bf16[8,128,128]{2,1,0:T(8,128)(2,1)S(1)}, u32[]{:S(2)}, u32[]{:S(2)}) collective-permute-start(bf16[8,128,128]{2,1,0:T(8,128)(2,1)S(1)} %add_convert_fusion), channel_id=1, source_target_pairs={{36,0},{40,4},{44,8},{48,12},{52,16},{56,20},{60,24},{64,28},{68,3... | collective-permute-start | bytes 786440 | tf_op jit(solution)/shard_map/ppermute | solution.py:17
  116.2 2.1 %collective-permute-start.10 = (bf16[8,128,128]{2,1,0:T(8,128)(2,1)S(1)}, bf16[8,128,128]{2,1,0:T(8,128)(2,1)S(1)}, u32[]{:S(2)}, u32[]{:S(2)}) collective-permute-start(bf16[8,128,128]{2,1,0:T(8,128)(2,1)S(1)} %add_convert_fusion), channel_id=1, source_target_pairs={{4,0},{8,4},{12,8},{16,12},{20,16},{24,20},{28,24},{32,28},{36,32}... | collective-permute-start | bytes 786440 | tf_op jit(solution)/shard_map/ppermute | solution.py:17
  118.5 0.9 copy.204
  119.4 0.9 copy.205
  120.5 7.3 %collective-permute-done.11 = bf16[8,128,128]{2,1,0:T(8,128)(2,1)S(1)} collective-permute-done((bf16[8,128,128]{2,1,0:T(8,128)(2,1)S(1)}, bf16[8,128,128]{2,1,0:T(8,128)(2,1)S(1)}, u32[]{:S(2)}, u32[]{:S(2)}) %collective-permute-start.11) | collective-permute-done | bytes 262176 | tf_op jit(solution)/shard_map/ppermute | solution.py:17
  127.8 2.3 %collective-permute-done.10 = bf16[8,128,128]{2,1,0:T(8,128)(2,1)S(1)} collective-permute-done((bf16[8,128,128]{2,1,0:T(8,128)(2,1)S(1)}, bf16[8,128,128]{2,1,0:T(8,128)(2,1)S(1)}, u32[]{:S(2)}, u32[]{:S(2)}) %collective-permute-start.10) | collective-permute-done | bytes 262176 | tf_op jit(solution)/shard_map/ppermute | solution.py:17
  130.1 0.5 fusion.26
  130.5 1.3 fusion.31
  131.8 0.7 fusion.28
  132.5 1.3 fusion.35
  133.8 0.9 copy.206
  134.7 0.9 copy.207
  (71 shorter events, 4.6 us)
Async XLA Ops:
  1.8 8.8 %copy-start.8 = (s32[64]{0:T(128)S(1)}, s32[64]{0:T(128)}, u32[]{:S(2)}) copy-start(s32[64]{0:T(128)} %param.10) | copy-start | bytes 772
  1.8 29.5 %collective-permute-start.1 = (bf16[2,128,8,128]{3,1,2,0:T(8,128)(2,1)S(1)}, bf16[2,128,8,128]{3,1,2,0:T(8,128)(2,1)S(1)}, u32[]{:S(2)}, u32[]{:S(2)}) collective-permute-start(bf16[2,128,8,128]{3,1,2,0:T(8,128)(2,1)S(1)} %pad_maximum_fusion), channel_id=1, source_target_pairs={{0,8},{4,12},{8,16},{12,20},{16,24},{20,28},{24,32},{28,36},{32,40... | collective-permute-start | bytes 1572872 | tf_op jit(solution)/shard_map/ppermute | solution.py:17
  6.5 25.1 %collective-permute-start = (bf16[2,128,8,128]{3,1,2,0:T(8,128)(2,1)S(1)}, bf16[2,128,8,128]{3,1,2,0:T(8,128)(2,1)S(1)}, u32[]{:S(2)}, u32[]{:S(2)}) collective-permute-start(bf16[2,128,8,128]{3,1,2,0:T(8,128)(2,1)S(1)} %pad_maximum_fusion), channel_id=1, source_target_pairs={{0,4},{4,8},{8,12},{12,16},{16,20},{20,24},{24,28},{28,32},{32,36}... | collective-permute-start | bytes 1572872 | tf_op jit(solution)/shard_map/ppermute | solution.py:17
  10.5 20.5 %copy-start.3 = (bf16[128,8,128]{2,1,0:T(8,128)(2,1)S(1)}, bf16[128,8,128]{2,1,0:T(8,128)(2,1)}, u32[]{:S(2)}) copy-start(bf16[128,8,128]{2,1,0:T(8,128)(2,1)} %param.7) | copy-start | bytes 786436
  10.5 20.5 %copy-start.1 = (bf16[128,8,128]{2,1,0:T(8,128)(2,1)S(1)}, bf16[128,8,128]{2,1,0:T(8,128)(2,1)}, u32[]{:S(2)}) copy-start(bf16[128,8,128]{2,1,0:T(8,128)(2,1)} %param.6) | copy-start | bytes 786436
  32.0 1.0 copy-start
  33.2 1.0 copy-start.2
  35.1 9.3 %collective-permute-start.2 = (bf16[8,128,128]{2,1,0:T(8,128)(2,1)S(1)}, bf16[8,128,128]{2,1,0:T(8,128)(2,1)S(1)}, u32[]{:S(2)}, u32[]{:S(2)}) collective-permute-start(bf16[8,128,128]{2,1,0:T(8,128)(2,1)S(1)} %get-tuple-element.71), channel_id=1, source_target_pairs={{0,8},{4,12},{8,16},{12,20},{16,24},{20,28},{24,32},{28,36},{32,40... | collective-permute-start | bytes 786440 | tf_op jit(solution)/shard_map/ppermute | solution.py:17
  44.5 11.2 %collective-permute-start.3 = (bf16[8,128,128]{2,1,0:T(8,128)(2,1)S(1)}, bf16[8,128,128]{2,1,0:T(8,128)(2,1)S(1)}, u32[]{:S(2)}, u32[]{:S(2)}) collective-permute-start(bf16[8,128,128]{2,1,0:T(8,128)(2,1)S(1)} %fusion.54), channel_id=1, source_target_pairs={{0,16},{4,20},{8,24},{12,28},{16,32},{20,36},{24,40},{28,44},{32,4... | collective-permute-start | bytes 786440 | tf_op jit(solution)/shard_map/ppermute | solution.py:17
  55.9 10.5 %collective-permute-start.4 = (bf16[8,128,128]{2,1,0:T(8,128)(2,1)S(1)}, bf16[8,128,128]{2,1,0:T(8,128)(2,1)S(1)}, u32[]{:S(2)}, u32[]{:S(2)}) collective-permute-start(bf16[8,128,128]{2,1,0:T(8,128)(2,1)S(1)} %convert_element_type.228), channel_id=1, source_target_pairs={{0,32},{4,36},{8,40},{12,44},{16,48},{20,52},{24,56},{28,60},{32,6... | collective-permute-start | bytes 786440 | tf_op jit(solution)/shard_map/ppermute | solution.py:17
  59.6 33.2 %collective-permute-start.6 = (bf16[2,128,8,128]{3,1,2,0:T(8,128)(2,1)}, bf16[2,128,8,128]{3,1,2,0:T(8,128)(2,1)}, u32[]{:S(2)}, u32[]{:S(2)}) collective-permute-start(bf16[2,128,8,128]{3,1,2,0:T(8,128)(2,1)} %pad_maximum_fusion.1), channel_id=1, source_target_pairs={{4,0},{8,4},{12,8},{16,12},{20,16},{24,20},{28,24},{32,28},{36,32}... | collective-permute-start | bytes 1572872 | tf_op jit(solution)/shard_map/ppermute | solution.py:17
  62.7 30.1 %collective-permute-start.7 = (bf16[2,128,8,128]{3,1,2,0:T(8,128)(2,1)}, bf16[2,128,8,128]{3,1,2,0:T(8,128)(2,1)}, u32[]{:S(2)}, u32[]{:S(2)}) collective-permute-start(bf16[2,128,8,128]{3,1,2,0:T(8,128)(2,1)} %pad_maximum_fusion.2), channel_id=1, source_target_pairs={{8,0},{12,4},{16,8},{20,12},{24,16},{28,20},{32,24},{36,28},{40,32... | collective-permute-start | bytes 1572872 | tf_op jit(solution)/shard_map/ppermute | solution.py:17
  66.3 0.7 copy-start.5
  66.4 0.7 copy-start.7
  76.5 5.3 %copy-start.4 = (f32[128,8,128]{2,0,1:T(8,128)S(1)}, f32[128,8,128]{2,0,1:T(8,128)}, u32[]{:S(2)}) copy-start(f32[128,8,128]{2,0,1:T(8,128)} %fusion.14) | copy-start | bytes 1572868
  76.9 15.8 %collective-permute-start.5 = (bf16[8,128,128]{2,1,0:T(8,128)(2,1)S(1)}, bf16[8,128,128]{2,1,0:T(8,128)(2,1)S(1)}, u32[]{:S(2)}, u32[]{:S(2)}) collective-permute-start(bf16[8,128,128]{2,1,0:T(8,128)(2,1)S(1)} %get-tuple-element.82), channel_id=1, source_target_pairs={{4,0},{8,4},{12,8},{16,12},{20,16},{24,20},{28,24},{32,28},{36,32}... | collective-permute-start | bytes 786440 | tf_op jit(solution)/shard_map/ppermute | solution.py:17
  92.8 2.0 %copy-start.6 = (bf16[8,128,128]{2,1,0:T(8,128)(2,1)S(1)}, bf16[8,128,128]{2,1,0:T(8,128)(2,1)}, u32[]{:S(2)}) copy-start(bf16[8,128,128]{2,1,0:T(8,128)(2,1)} %copy-done.5) | copy-start | bytes 786436
  92.9 10.4 %collective-permute-start.8 = (bf16[8,128,128]{2,1,0:T(8,128)(2,1)S(1)}, bf16[8,128,128]{2,1,0:T(8,128)(2,1)S(1)}, u32[]{:S(2)}, u32[]{:S(2)}) collective-permute-start(bf16[8,128,128]{2,1,0:T(8,128)(2,1)S(1)} %get-tuple-element.45), channel_id=1, source_target_pairs={{8,0},{12,4},{16,8},{20,12},{24,16},{28,20},{32,24},{36,28},{40,32... | collective-permute-start | bytes 786440 | tf_op jit(solution)/shard_map/ppermute | solution.py:17
  103.4 10.7 %collective-permute-start.9 = (bf16[8,128,128]{2,1,0:T(8,128)(2,1)S(1)}, bf16[8,128,128]{2,1,0:T(8,128)(2,1)S(1)}, u32[]{:S(2)}, u32[]{:S(2)}) collective-permute-start(bf16[8,128,128]{2,1,0:T(8,128)(2,1)S(1)} %fusion.55), channel_id=1, source_target_pairs={{16,0},{20,4},{24,8},{28,12},{32,16},{36,20},{40,24},{44,28},{48,3... | collective-permute-start | bytes 786440 | tf_op jit(solution)/shard_map/ppermute | solution.py:17
  114.3 13.5 %collective-permute-start.11 = (bf16[8,128,128]{2,1,0:T(8,128)(2,1)S(1)}, bf16[8,128,128]{2,1,0:T(8,128)(2,1)S(1)}, u32[]{:S(2)}, u32[]{:S(2)}) collective-permute-start(bf16[8,128,128]{2,1,0:T(8,128)(2,1)S(1)} %add_convert_fusion), channel_id=1, source_target_pairs={{36,0},{40,4},{44,8},{48,12},{52,16},{56,20},{60,24},{64,28},{68,3... | collective-permute-start | bytes 786440 | tf_op jit(solution)/shard_map/ppermute | solution.py:17
  116.2 13.9 %collective-permute-start.10 = (bf16[8,128,128]{2,1,0:T(8,128)(2,1)S(1)}, bf16[8,128,128]{2,1,0:T(8,128)(2,1)S(1)}, u32[]{:S(2)}, u32[]{:S(2)}) collective-permute-start(bf16[8,128,128]{2,1,0:T(8,128)(2,1)S(1)} %add_convert_fusion), channel_id=1, source_target_pairs={{4,0},{8,4},{12,8},{16,12},{20,16},{24,20},{28,24},{32,28},{36,32}... | collective-permute-start | bytes 786440 | tf_op jit(solution)/shard_map/ppermute | solution.py:17
